TPU v7x, 512 devices: a whole 4x8x8 slice. The times are simulated.
512 devices in a mesh: grp: 64 (over z_hi, y, core), mdl: 8 (over z_lo, x).
Axes of the slice: x: 4, y: 8, z: 8 (z_hi: 4, z_lo: 2; z = z_hi * 2 + z_lo), core: 2. Of those that a mesh axis runs over, the one named last changes fastest.
Arguments:
- draft_hidden: bfloat16 [128, 32, 2048], P('grp', None, 'mdl'), may hold values from -6 to 6
- q_weight: bfloat16 [4, 2048, 1024], P(None, None, 'mdl'), may hold values from -0.125 to 0.125
- kv_weight: bfloat16 [2, 2048, 1024], P(None, None, 'mdl'), may hold values from -0.125 to 0.125
- router_weight: float32 [2048, 4], replicated, may hold values from -0.125 to 0.125
- routes: int32 [128, 32, 2], P('grp'), may hold values from 0 to 3, all different within a row
- tree_mask: int32 [128, 32, 32], P('grp'), may hold values from 0 to 1, as said below
- accepted: int32 [128, 8], P('grp'), may hold values from 0 to 31, as said below
- cache_kv: bfloat16 [192, 2, 1024, 1024], P('grp', None, None, 'mdl')
- cache_len: int32 [192], P('grp'), may hold values from 1 to 1024
- slot_request: int32 [192], replicated, may hold values from 0 to 127, as said below
Outputs:
- verified: bfloat16 [128, 8, 2, 1024], P('grp', None, None, 'mdl')
Inputs may be any that keep to these rules, and one draw needn't show every extreme that they name: `routes`: the 2 experts of one token differ. tree_mask[r, i, j] is 1 exactly when draft j is draft i or an ancestor of it; every draft's parent has a lower index and draft 0 is the root. `accepted`: each row holds the first 8 drafts of the root-to-node chain of one draft, in increasing order; a shorter chain is followed by repeats of its last draft. `slot_request`: the requests of one index of grp are the 2 in a row that it holds; they are served by 3 slots in all, 1 of them by two slots and the others by one; no index of grp holds more than 1 slot serving requests of any one index of grp, and some pairs of indices have exactly 1 such slot.
All inputs are finite; a program needn't handle non-finite values.
Results may differ from a plain program's by a relative error of at most 0.014.
The roundings to bfloat16 on the way count: a program that leaves them out, or rounds other values in their place, can miss the bound.
Values may be sent and summed in bfloat16 or wider, within the bound.
No kernel may reach another device: no remote copies, remote signals or barrier semaphores. Data moves between devices by JAX's collectives and lax.ppermute only.
A program may use at most 64 MiB of HBM per device.

v0:
```python
import jax
import jax.numpy as jnp
from jax import lax
from jax.sharding import PartitionSpec as P

HEAD_SIZE = 128


def softmax_piece(scores, usable, values, contract):
    masked = jnp.where(usable, scores, -jnp.inf)
    peak_score = jnp.max(masked, axis=-1)
    weights_low = jnp.exp(masked - peak_score[..., None]).astype(jnp.bfloat16)
    denominator = jnp.sum(weights_low.astype(jnp.float32), axis=-1)
    numerator = jnp.einsum(contract, weights_low, values, preferred_element_type=jnp.float32)
    return (peak_score, denominator, numerator)


def blend(running, pieces, matched):
    running_max, denominator, numerator = running
    piece_peak, piece_den, piece_num = pieces
    candidate = jnp.where(matched[:, :, None, None, None], piece_peak[None], -jnp.inf)
    new_max = jnp.maximum(running_max, jnp.max(candidate, axis=1))
    rescale = jnp.exp(running_max - new_max)
    weight = jnp.exp(candidate - new_max[:, None])
    denominator = denominator * rescale + jnp.sum(weight * piece_den[None], axis=1)
    numerator = numerator * rescale[..., None] + jnp.einsum(
        "rnqkh,nqkhd->rqkhd", weight, piece_num, precision=lax.Precision.HIGHEST
    )
    return (new_max, denominator, numerator)


def on_device(
    draft_hidden,
    q_weight,
    kv_weight,
    router_weight,
    routes,
    tree_mask,
    accepted,
    cache_kv,
    cache_len,
    slot_request,
):
    highest = lax.Precision.HIGHEST
    requests, drafts, part_width = draft_hidden.shape
    experts = q_weight.shape[0]
    head_width = q_weight.shape[2]
    head_count = head_width // HEAD_SIZE
    topk_count = routes.shape[2]
    row_count = requests * drafts
    score_scale = HEAD_SIZE ** (-0.5)
    pieces = lax.all_gather(draft_hidden, "mdl", axis=2, tiled=True)
    piece_size = pieces.shape[2]
    piece_rows = pieces.reshape(row_count, piece_size)
    q_sum = jnp.einsum("nd,edw->new", piece_rows, q_weight, preferred_element_type=jnp.float32)
    kv_sum = jnp.einsum("nd,cdw->ncw", piece_rows, kv_weight, preferred_element_type=jnp.float32)
    logit_sum = jnp.dot(piece_rows.astype(jnp.float32), router_weight, precision=highest)
    route_flat = routes.reshape(row_count, topk_count)
    chosen_mask = route_flat[:, :, None] == jnp.arange(experts, dtype=jnp.int32)[None, None, :]
    chosen = jnp.sum(jnp.where(chosen_mask, logit_sum[:, None, :], 0.0), axis=2)
    gate_probs = jax.nn.softmax(chosen, axis=-1).reshape(requests, drafts, topk_count)
    queries = jnp.sum(jnp.where(chosen_mask[:, :, :, None], q_sum[:, None], 0.0), axis=2)
    queries = queries.astype(jnp.bfloat16).reshape(
        requests, drafts, topk_count, head_count, HEAD_SIZE
    )
    draft_keys = kv_sum[:, 0].astype(jnp.bfloat16).reshape(requests, drafts, head_count, HEAD_SIZE)
    draft_values = (
        kv_sum[:, 1].astype(jnp.bfloat16).reshape(requests, drafts, head_count, HEAD_SIZE)
    )
    query_len = queries.shape[1]
    tree_scores = (
        jnp.einsum("rqkhd,rjhd->rqkhj", queries, draft_keys, preferred_element_type=jnp.float32)
        * score_scale
    )
    allowed = (tree_mask > 0)[:, :, None, None, :]
    tree_peak, tree_den, tree_num = softmax_piece(
        tree_scores, allowed, draft_values, "rqkhj,rjhd->rqkhd"
    )
    slot_count = cache_kv.shape[0]
    cache_size = cache_kv.shape[2]
    group_idx = lax.axis_index("grp")
    sending = queries.reshape(requests, query_len, topk_count * head_width)
    my_requests = lax.dynamic_slice_in_dim(slot_request, group_idx * slot_count, slot_count)
    pieces = lax.all_gather(sending, "grp", axis=0, tiled=True)
    piece_count = pieces.shape[0]
    selector = (my_requests[:, None] == jnp.arange(piece_count, dtype=jnp.int32)[None, :]).astype(
        jnp.bfloat16
    )
    slot_queries = jnp.einsum(
        "sn,nqw->sqw", selector, pieces, preferred_element_type=jnp.float32
    ).astype(jnp.bfloat16)
    slot_queries = slot_queries.reshape(slot_count, query_len, topk_count, head_count, HEAD_SIZE)
    cache_keys = cache_kv[:, 0].reshape(slot_count, cache_size, head_count, HEAD_SIZE)
    cache_values = cache_kv[:, 1].reshape(slot_count, cache_size, head_count, HEAD_SIZE)
    slot_scores = (
        jnp.einsum(
            "sqkhd,schd->sqkhc", slot_queries, cache_keys, preferred_element_type=jnp.float32
        )
        * score_scale
    )
    in_cache = (jnp.arange(cache_size, dtype=jnp.int32)[None, :] < cache_len[:, None])[
        :, None, None, None, :
    ]
    slot_peak, slot_den, slot_num = softmax_piece(
        slot_scores, in_cache, cache_values, "sqkhc,schd->sqkhd"
    )
    home_ids = group_idx * requests + jnp.arange(requests, dtype=jnp.int32)
    pieces = (
        lax.all_gather(slot_peak, "grp", axis=0, tiled=True),
        lax.all_gather(slot_den, "grp", axis=0, tiled=True),
        lax.all_gather(slot_num, "grp", axis=0, tiled=True),
    )
    running_max, denominator, numerator = blend(
        (tree_peak, tree_den, tree_num), pieces, home_ids[:, None] == slot_request[None, :]
    )
    final_num = jnp.take_along_axis(numerator, accepted[:, :, None, None, None], axis=1)
    final_den = jnp.take_along_axis(denominator, accepted[:, :, None, None], axis=1)
    final_gate = jnp.take_along_axis(gate_probs, accepted[:, :, None], axis=1)
    mixed = final_gate[:, :, :, None, None] * final_num / final_den[..., None]
    kept_rows = accepted.shape[1]
    return mixed.reshape(requests, kept_rows, topk_count, head_width).astype(jnp.bfloat16)


def solution(mesh):
    in_specs = (
        P("grp", None, "mdl"),
        P(None, None, "mdl"),
        P(None, None, "mdl"),
        P(),
        P("grp", None, None),
        P("grp", None, None),
        P("grp", None),
        P("grp", None, None, "mdl"),
        P("grp"),
        P(),
    )
    out_specs = P("grp", None, None, "mdl")
    return jax.shard_map(
        on_device, mesh=mesh, in_specs=in_specs, out_specs=out_specs, check_vma=False
    )
```

profile of v0, /device:TPU:1, one launch (start us, length us, event | category | flops | bytes accessed | tf_op | source)
XLA Modules:
  0.0 317.8 jit_solution(7277483683072777976)
XLA Ops:
  6.5 0.8 copy.87
  7.5 24.4 %all_gather.15 = bf16[2,32,2048]{2,1,0:T(8,128)(2,1)S(1)} all-gather(bf16[2,32,256]{2,1,0:T(8,128)(2,1)} %param.10), channel_id=1, replica_groups=mesh['grp'=64,'mdl'=8] {'mdl'}, dimensions={2}, use_global_device_ids=true | all-gather | bytes 294912 | tf_op jit(solution)/shard_map/all_gather | solution.py:52
  31.9 0.5 fusion.48
  32.4 0.1 select_reduce_fusion
  32.6 0.6 convert_element_type.49
  33.4 94.7 %all-gather.5.cloned.1.call-done = bf16[128,32,256]{2,1,0:T(8,128)(2,1)} async-done(((bf16[2,32,256]{2,1,0:T(8,128)(2,1)}), bf16[128,32,256]{2,1,0:T(8,128)(2,1)}) %all-gather.5.cloned.1.call-update) | async-done | bytes 2097168 | tf_op jit(solution)/shard_map/all_gather | solution.py:84
  128.1 2.8 fusion.8
  131.0 1.6 fusion.45
  132.6 2.1 convolution_bitcast_fusion
  134.9 0.3 fusion.47
  135.7 0.6 gather_fusion
  136.4 1.5 convolution_convert_fusion
  138.0 0.2 fusion.46
  138.3 80.5 %all-gather = f32[192,32,2]{1,2,0:T(2,128)S(1)} all-gather(f32[3,32,2]{1,2,0:T(2,128)S(1)} %get-tuple-element.11), channel_id=2, replica_groups=mesh['grp'=64,'mdl'=8] {'grp'}, dimensions={0}, use_global_device_ids=true | all-gather | bytes 49920 | tf_op jit(solution)/shard_map/all_gather | solution.py:109
  218.9 0.1 copy.103
  219.2 0.3 convert_reduce_fusion
  219.5 77.0 %all-gather.1 = f32[192,32,2]{1,2,0:T(2,128)S(1)} all-gather(f32[3,32,2]{1,2,0:T(2,128)S(1)} %convert_reduce_fusion), channel_id=3, replica_groups=mesh['grp'=64,'mdl'=8] {'grp'}, dimensions={0}, use_global_device_ids=true | all-gather | bytes 49920 | tf_op jit(solution)/shard_map/all_gather | solution.py:110
  296.5 0.1 copy.107
  296.6 0.2 fusion.24
  296.9 0.6 gather_fusion.2
  297.8 11.6 %fusion = f32[32,2,128,2]{2,3,1,0:T(2,128)S(1)} fusion(f32[192,32,2,1,128]{4,1,3,2,0:T(8,128)} %all-gather.7.cloned.1.call-done, pred[2,192]{1,0:T(4,128)(4,1)S(1)} %broadcast_compare_fusion.1, f32[2,32,2]{0,2,1:T(2,128)S(1)} %copy.104, f32[192,32,2]{0,2,1:T(2,128)S(1)} %copy.103), kind=kOutput, calls=%fused_computation.3 | convolution fusion | flops 37797888 | bytes 6407040 | tf_op jit(solution)/shard_map/rnqkh,nqkhd->rqkhd/dot_general | solution.py:26
  309.4 0.2 fusion.14
  309.6 0.6 gather_fusion.1
  310.3 0.7 fusion.35
  (51 shorter events, 2.0 us)
Async XLA Ops:
  6.5 25.4 %copy-start = (bf16[4,2048,128]{2,1,0:T(8,128)(2,1)S(1)}, bf16[4,2048,128]{2,1,0:T(8,128)(2,1)}, u32[]{:S(2)}) copy-start(bf16[4,2048,128]{2,1,0:T(8,128)(2,1)} %param.11) | copy-start | bytes 6291460
  6.5 26.7 %copy-start.4 = (s32[192]{0:T(256)S(1)}, s32[192]{0:T(256)}, u32[]{:S(2)}) copy-start(s32[192]{0:T(256)} %param.19) | copy-start | bytes 2308
  6.5 26.8 %copy-start.5 = (s32[3]{0:T(128)S(1)}, s32[3]{0:T(128)}, u32[]{:S(2)}) copy-start(s32[3]{0:T(128)} %param.18) | copy-start | bytes 40
  6.5 121.6 %all-gather.5.cloned.1.call-start = ((), (), s32[]{:S(2)}) async-start(), calls=%async_computation | async-start | bytes 2129920 | tf_op jit(solution)/shard_map/all_gather | solution.py:84
  33.2 264.6 %all-gather.7.cloned.1.call-start = ((), (), s32[]{:S(2)}) async-start(), calls=%async_computation.1 | async-start | bytes 6389760 | tf_op jit(solution)/shard_map/all_gather | solution.py:111
  130.9 3.8 %copy-start.3 = (s32[2,8]{1,0:T(2,128)S(1)}, s32[2,8]{1,0:T(2,128)}, u32[]{:S(2)}) copy-start(s32[2,8]{1,0:T(2,128)} %param.16) | copy-start | bytes 196
  130.9 3.9 %copy-start.2 = (s32[2,32,32]{2,1,0:T(8,128)S(1)}, s32[2,32,32]{2,1,0:T(8,128)}, u32[]{:S(2)}) copy-start(s32[2,32,32]{2,1,0:T(8,128)} %param.15) | copy-start | bytes 24580
  130.9 4.0 %copy-start.1 = (f32[2048,4]{0,1:T(4,128)S(1)}, f32[2048,4]{0,1:T(4,128)}, u32[]{:S(2)}) copy-start(f32[2048,4]{0,1:T(4,128)} %param.13) | copy-start | bytes 98308
Sparse Core Ops, SparseCore 0:
  33.3 94.7 all-gather.4
  134.8 91.8 all-gather.6
where the time goes:
time: 318 us
  blocking collectives  182 us (57%)
  waiting for transfers between devices  94.7 us (30%)
  matrix products  20.8 us (7%)
  between operations  13.6 us (4%)
  local copies, waits for them, and re-layouts  4.98 us (2%)
    all_gather x1, waiting for transfers between devices, on_device(): pieces = lax.all_gather(sending, 'grp', axis=0, tiled=True)  94.7 us
    all_gather x1, blocking collectives, on_device(): lax.all_gather(slot_peak, 'grp', axis=0, tiled=True)  80.5 us
    all_gather x1, blocking collectives, on_device(): lax.all_gather(slot_den, 'grp', axis=0, tiled=True)  77 us
    all_gather x1, blocking collectives, on_device(): pieces = lax.all_gather(draft_hidden, 'mdl', axis=2, tiled=True)  24.4 us
    dot_general x1, matrix products, blend(): jnp.einsum('rnqkh,nqkhd->rqkhd', weight, piece_num, precision=lax.Precisi...  11.6 us
  transfers between devices with their start and end apart: 2, of which 1 were waited for; matrix products, arithmetic and copies ran while one was open for 2% of the time, Pallas kernels for 0%

commit v1 on v0

v1 whole, which is shorter than its diff:
```python
import jax
import jax.numpy as jnp
from jax import lax
from jax.sharding import PartitionSpec as P

HEAD_SIZE = 128


def softmax_piece(scores, usable, values, contract):
    masked = jnp.where(usable, scores, -jnp.inf)
    peak_score = jnp.max(masked, axis=-1)
    weights_low = jnp.exp(masked - peak_score[..., None]).astype(jnp.bfloat16)
    denominator = jnp.sum(weights_low.astype(jnp.float32), axis=-1)
    numerator = jnp.einsum(contract, weights_low, values, preferred_element_type=jnp.float32)
    return (peak_score, denominator, numerator)


def on_device(
    draft_hidden,
    q_weight,
    kv_weight,
    router_weight,
    routes,
    tree_mask,
    accepted,
    cache_kv,
    cache_len,
    slot_request,
):
    highest = lax.Precision.HIGHEST
    requests, drafts, part_width = draft_hidden.shape
    experts = q_weight.shape[0]
    head_width = q_weight.shape[2]
    head_count = head_width // HEAD_SIZE
    topk_count = routes.shape[2]
    kept_rows = accepted.shape[1]
    score_scale = HEAD_SIZE ** (-0.5)
    group_count = lax.axis_size("grp")
    group_idx = lax.axis_index("grp")
    slot_count = cache_kv.shape[0]
    cache_size = cache_kv.shape[2]

    hidden = lax.all_gather(draft_hidden, "mdl", axis=2, tiled=True)
    acc_hidden = jnp.take_along_axis(hidden, accepted[:, :, None], axis=1)
    acc_routes = jnp.take_along_axis(routes, accepted[:, :, None], axis=1)
    acc_mask = jnp.take_along_axis(tree_mask, accepted[:, :, None], axis=1)

    q_sum = jnp.einsum("rad,edw->raew", acc_hidden, q_weight, preferred_element_type=jnp.float32)
    kv_sum = jnp.einsum("rtd,cdw->rtcw", hidden, kv_weight, preferred_element_type=jnp.float32)
    logit_sum = jnp.einsum(
        "rad,de->rae", acc_hidden.astype(jnp.float32), router_weight, precision=highest
    )
    chosen_mask = acc_routes[..., None] == jnp.arange(experts, dtype=jnp.int32)
    chosen = jnp.sum(jnp.where(chosen_mask, logit_sum[:, :, None, :], 0.0), axis=3)
    gate_probs = jax.nn.softmax(chosen, axis=-1)
    queries = jnp.sum(jnp.where(chosen_mask[..., None], q_sum[:, :, None], 0.0), axis=3)
    queries = queries.astype(jnp.bfloat16)
    draft_keys = kv_sum[:, :, 0].astype(jnp.bfloat16)
    draft_values = kv_sum[:, :, 1].astype(jnp.bfloat16)

    tree_scores = (
        jnp.einsum("rakw,rjw->rakj", queries, draft_keys, preferred_element_type=jnp.float32)
        * score_scale
    )
    tree_peak, tree_den, tree_num = softmax_piece(
        tree_scores, (acc_mask > 0)[:, :, None, :], draft_values, "rakj,rjw->rakw"
    )

    slot_table = slot_request.reshape(group_count, slot_count)
    home_of = slot_table // requests
    local_of = slot_table % requests
    mine = home_of == group_idx
    picked = jnp.sum(jnp.where(mine, local_of, 0), axis=1)
    any_mine = jnp.any(mine, axis=1)
    outgoing = jnp.where(any_mine[:, None, None, None], queries[picked], jnp.zeros((), queries.dtype))
    incoming = lax.all_to_all(outgoing, "grp", 0, 0, tiled=True)

    my_slots = lax.dynamic_slice_in_dim(slot_request, group_idx * slot_count, slot_count)
    slot_queries = incoming[my_slots // requests]
    cache_keys = cache_kv[:, 0]
    cache_values = cache_kv[:, 1]
    slot_scores = (
        jnp.einsum("sakw,scw->sakc", slot_queries, cache_keys, preferred_element_type=jnp.float32)
        * score_scale
    )
    in_cache = (jnp.arange(cache_size, dtype=jnp.int32)[None, :] < cache_len[:, None])[
        :, None, None, :
    ]
    slot_peak, slot_den, slot_num = softmax_piece(
        slot_scores, in_cache, cache_values, "sakc,scw->sakw"
    )

    packed = jnp.concatenate([slot_num, slot_den[..., None], slot_peak[..., None]], axis=-1)
    to_home = (my_slots // requests)[None, :] == jnp.arange(group_count, dtype=jnp.int32)[:, None]
    returning = jnp.sum(
        jnp.where(to_home[:, :, None, None, None], packed[None], 0.0), axis=1
    )
    back = lax.all_to_all(returning, "grp", 0, 0, tiled=True)
    back_num = back[..., :head_width]
    back_den = back[..., head_width]
    back_peak = back[..., head_width + 1]

    home_ids = group_idx * requests + jnp.arange(requests, dtype=jnp.int32)
    matched = jnp.any(slot_table[None, :, :] == home_ids[:, None, None], axis=2)
    candidate = jnp.where(matched[:, :, None, None], back_peak[None], -jnp.inf)
    running_max = jnp.maximum(tree_peak, jnp.max(candidate, axis=1))
    rescale = jnp.exp(tree_peak - running_max)
    weight = jnp.exp(candidate - running_max[:, None])
    denominator = tree_den * rescale + jnp.sum(weight * back_den[None], axis=1)
    numerator = tree_num * rescale[..., None] + jnp.sum(
        weight[..., None] * back_num[None], axis=1
    )
    mixed = gate_probs[..., None] * numerator / denominator[..., None]
    return mixed.reshape(requests, kept_rows, topk_count, head_width).astype(jnp.bfloat16)


def solution(mesh):
    in_specs = (
        P("grp", None, "mdl"),
        P(None, None, "mdl"),
        P(None, None, "mdl"),
        P(),
        P("grp", None, None),
        P("grp", None, None),
        P("grp", None),
        P("grp", None, None, "mdl"),
        P("grp"),
        P(),
    )
    out_specs = P("grp", None, None, "mdl")
    return jax.shard_map(
        on_device, mesh=mesh, in_specs=in_specs, out_specs=out_specs, check_vma=False
    )
```

time: 318 us -> 114 us (0.36)
  blocking collectives: 182 us -> 24.4 us
  waiting for transfers between devices: 94.7 us -> 39.6 us
  starting transfers between devices: 0.04 us -> 28.4 us
  matrix products: 20.8 us -> 5.88 us
  between operations: 13.6 us -> 0.21 us
  local copies, waits for them, and re-layouts: 4.98 us -> 9.75 us
  other arithmetic: 1.84 us -> 5.62 us
    all_gather x3 -> x1, blocking collectives: 182 us -> 24.4 us  [on_device(): hidden = lax.all_gather(draft_hidden, 'mdl', axis=2, tiled=True)]
    all_gather x2 -> x0, waiting for transfers between devices: 94.7 us -> none  [the longest x1 94.7 us: on_device(): pieces = lax.all_gather(sending, 'grp', axis=0, tiled=True)]
    all_to_all x0 -> x2, waiting for transfers between devices: none -> 39.6 us  [the longest x1 27.4 us: on_device(): back = lax.all_to_all(returning, 'grp', 0, 0, tiled=True)]
    all_to_all x0 -> x2, starting transfers between devices: none -> 28.4 us  [the longest x1 22.1 us: on_device(): incoming = lax.all_to_all(outgoing, 'grp', 0, 0, tiled=True)]
    dot_general x7 -> x5, matrix products: 18.5 us -> 4.27 us  [the longest x1 1.54 us: on_device(): jnp.einsum('sakw,scw->sakc', slot_queries, cache_keys, preferred_element_...]
  transfers between devices with their start and end apart: 2 -> 2, of which waited for: 1 -> 2; matrix products, arithmetic and copies ran while one was open for 2% -> 3% of each run, Pallas kernels for 0% -> 0%
where the time goes in v1:
time: 114 us
  waiting for transfers between devices  39.6 us (35%)
  starting transfers between devices  28.4 us (25%)
  blocking collectives  24.4 us (21%)
  local copies, waits for them, and re-layouts  9.75 us (9%)
  matrix products  5.88 us (5%)
  other arithmetic  5.62 us (5%)
    all_to_all x1, waiting for transfers between devices, on_device(): back = lax.all_to_all(returning, 'grp', 0, 0, tiled=True)  27.4 us
    all_gather x1, blocking collectives, on_device(): hidden = lax.all_gather(draft_hidden, 'mdl', axis=2, tiled=True)  24.4 us
    all_to_all x1, starting transfers between devices, on_device(): incoming = lax.all_to_all(outgoing, 'grp', 0, 0, tiled=True)  22.1 us
    all_to_all x1, waiting for transfers between devices, on_device(): incoming = lax.all_to_all(outgoing, 'grp', 0, 0, tiled=True)  12.2 us
    all_to_all x1, starting transfers between devices, on_device(): back = lax.all_to_all(returning, 'grp', 0, 0, tiled=True)  6.26 us
    unnamed x13, local copies, waits for them, and re-layouts  3.37 us
  transfers between devices with their start and end apart: 2, of which 2 were waited for; matrix products, arithmetic and copies ran while one was open for 3% of the time, Pallas kernels for 0%

profile of v1, /device:TPU:1, one launch (start us, length us, event | category | flops | bytes accessed | tf_op | source)
XLA Modules:
  0.0 113.9 jit_solution(4306026398381764789)
XLA Ops:
  0.0 0.8 bitcast_or_fusion
  0.8 0.7 compare_and_fusion
  1.6 24.4 %all_gather.3 = bf16[2,32,2048]{2,1,0:T(8,128)(2,1)S(1)} all-gather(bf16[2,32,256]{2,1,0:T(8,128)(2,1)} %param.10), channel_id=1, replica_groups=mesh['grp'=64,'mdl'=8] {'mdl'}, dimensions={2}, use_global_device_ids=true | all-gather | bytes 294912 | tf_op jit(solution)/shard_map/all_gather | solution.py:43
  26.0 0.8 copy.69
  26.8 0.8 gather_fusion.3
  27.6 0.6 gather_fusion.2
  28.4 0.8 eq.60
  30.0 0.6 gather_fusion
  30.6 0.8 broadcast_select_fusion
  31.5 22.1 %all-to-all-start = ((bf16[64,8,2,128]{3,1,2,0:T(8,128)(2,1)}), bf16[64,8,2,128]{3,1,2,0:T(8,128)(2,1)S(1)}, u32[]{:S(2)}, u32[]{:S(2)}) async-start(bf16[64,8,2,128]{3,1,2,0:T(8,128)(2,1)} %broadcast_select_fusion), calls=%async_computation | async-start | bytes 524288 | tf_op jit(solution)/shard_map/all_to_all | solution.py:76
  53.9 0.6 gather_fusion.4
  54.5 0.6 fusion.19
  55.3 12.2 %all-to-all-done = bf16[64,8,2,128]{3,1,2,0:T(8,128)(2,1)S(1)} async-done(((bf16[64,8,2,128]{3,1,2,0:T(8,128)(2,1)}), bf16[64,8,2,128]{3,1,2,0:T(8,128)(2,1)S(1)}, u32[]{:S(2)}, u32[]{:S(2)}) %all-to-all-start) | async-done | bytes 262176 | tf_op jit(solution)/shard_map/all_to_all | solution.py:76
  67.5 0.6 gather_fusion.1
  68.0 1.5 %fusion.36 = (f32[3,8,2]{1,2,0:T(2,128)S(1)}, f32[3,8,2,1024]{3,1,2,0:T(8,128)S(1)}) fusion(bf16[3,8,2,128]{3,1,2,0:T(8,128)(2,1)S(1)} %gather_fusion.1, bf16[3,2,1024,128]{3,2,1,0:T(8,128)(2,1)} %param.17, pred[3,1024]{1,0:T(4,128)(4,1)S(1)} %iota_compare_fusion.1), kind=kOutput, calls=%fused_computation.87 | convolution fusion | flops 12730320 | bytes 998592 | tf_op jit(solution)/shard_map/sakw,scw->sakc/dot_general | solution.py:83
  69.6 1.4 %fusion.12 = f32[3,8,2,128]{3,1,2,0:T(8,128)S(1)} fusion(bf16[3,2,1024,128]{3,2,1,0:T(8,128)(2,1)} %param.17, f32[3,8,2,1024]{3,1,2,0:T(8,128)S(1)} %get-tuple-element.16, f32[3,8,2]{1,2,0:T(2,128)S(1)} %get-tuple-element.15), kind=kOutput, calls=%fused_computation.23 | convolution fusion | flops 12681216 | bytes 1007808 | tf_op jit(solution)/shard_map/sakc,scw->sakw/dot_general | solution.py:14
  71.5 1.4 %select_reduce_fusion = f32[64,8,2,130]{3,1,2,0:T(8,128)} fusion(f32[3,8,2,130]{3,1,2,0:T(8,128)S(1)} %pad_maximum_fusion, pred[64,3]{1,0:T(8,128)(4,1)S(1)} %iota_compare_fusion), kind=kLoop, calls=%fused_computation.6 | loop fusion | flops 665600 | bytes 557632 | tf_op jit(solution)/shard_map/reduce_sum | solution.py:95
  72.9 6.3 %all-to-all-start.1 = ((f32[64,8,2,130]{3,1,2,0:T(8,128)}), f32[64,8,2,130]{3,1,2,0:T(8,128)S(1)}, u32[]{:S(2)}, u32[]{:S(2)}) async-start(f32[64,8,2,130]{3,1,2,0:T(8,128)} %select_reduce_fusion), calls=%async_computation.1 | async-start | bytes 2097152 | tf_op jit(solution)/shard_map/all_to_all | solution.py:98
  79.2 1.5 %convolution_convert_fusion = bf16[2,32,2,128]{3,1,2,0:T(8,128)(2,1)S(1)} fusion(bf16[2,2048,128]{2,1,0:T(8,128)(2,1)} %param.12, bf16[2,32,2048]{2,1,0:T(8,128)(2,1)S(1)} %all_gather.3), kind=kOutput, calls=%fused_computation.11 | convolution fusion | flops 67125248 | bytes 1343488 | tf_op jit(solution)/shard_map/rtd,cdw->rtcw/dot_general | solution.py:49
  81.2 27.4 %all-to-all-done.1 = f32[64,8,2,130]{3,1,2,0:T(8,128)S(1)} async-done(((f32[64,8,2,130]{3,1,2,0:T(8,128)}), f32[64,8,2,130]{3,1,2,0:T(8,128)S(1)}, u32[]{:S(2)}, u32[]{:S(2)}) %all-to-all-start.1) | async-done | bytes 532512 | tf_op jit(solution)/shard_map/all_to_all | solution.py:98
  108.6 1.1 fusion.35
  109.8 1.3 %copy.90 = f32[64,8,2,1]{0,1,3,2:T(8,128)S(1)} copy(f32[64,8,2,1]{3,1,2,0:T(8,128)} %get-tuple-element.12) | data formatting | bytes 8192
  111.2 1.3 %copy.91 = f32[64,8,2,1]{0,1,3,2:T(8,128)S(1)} copy(f32[64,8,2,1]{3,1,2,0:T(8,128)} %get-tuple-element.11) | data formatting | bytes 8192
  113.3 0.6 copy.80
  (46 shorter events, 3.3 us)
Async XLA Ops:
  0.0 29.5 %copy-start = (bf16[4,2048,128]{2,1,0:T(8,128)(2,1)S(1)}, bf16[4,2048,128]{2,1,0:T(8,128)(2,1)}, u32[]{:S(2)}) copy-start(bf16[4,2048,128]{2,1,0:T(8,128)(2,1)} %param.11) | copy-start | bytes 6291460
  27.6 26.1 %copy-start.2 = (s32[192]{0:T(256)S(1)}, s32[192]{0:T(256)}, u32[]{:S(2)}) copy-start(s32[192]{0:T(256)} %param.19) | copy-start | bytes 2308
  27.6 26.2 %copy-start.3 = (s32[3]{0:T(128)S(1)}, s32[3]{0:T(128)}, u32[]{:S(2)}) copy-start(s32[3]{0:T(128)} %param.18) | copy-start | bytes 40
  27.6 26.3 %copy-start.1 = (s32[2,32,32]{2,1,0:T(8,128)S(1)}, s32[2,32,32]{2,1,0:T(8,128)}, u32[]{:S(2)}) copy-start(s32[2,32,32]{2,1,0:T(8,128)} %param.15) | copy-start | bytes 24580
  27.6 26.9 %copy-start.4 = (f32[2048,4]{0,1:T(4,128)S(1)}, f32[2048,4]{0,1:T(4,128)}, u32[]{:S(2)}) copy-start(f32[2048,4]{0,1:T(4,128)} %param.13) | copy-start | bytes 98308
  31.5 36.0 %all-to-all-start = ((bf16[64,8,2,128]{3,1,2,0:T(8,128)(2,1)}), bf16[64,8,2,128]{3,1,2,0:T(8,128)(2,1)S(1)}, u32[]{:S(2)}, u32[]{:S(2)}) async-start(bf16[64,8,2,128]{3,1,2,0:T(8,128)(2,1)} %broadcast_select_fusion), calls=%async_computation | async-start | bytes 524288 | tf_op jit(solution)/shard_map/all_to_all | solution.py:76
  72.9 35.8 %all-to-all-start.1 = ((f32[64,8,2,130]{3,1,2,0:T(8,128)}), f32[64,8,2,130]{3,1,2,0:T(8,128)S(1)}, u32[]{:S(2)}, u32[]{:S(2)}) async-start(f32[64,8,2,130]{3,1,2,0:T(8,128)} %select_reduce_fusion), calls=%async_computation.1 | async-start | bytes 2097152 | tf_op jit(solution)/shard_map/all_to_all | solution.py:98

commit v2 on v1

--- a/solution.py
+++ b/solution.py
@@ -72,11 +72,18 @@
     mine = home_of == group_idx
     picked = jnp.sum(jnp.where(mine, local_of, 0), axis=1)
     any_mine = jnp.any(mine, axis=1)
-    outgoing = jnp.where(any_mine[:, None, None, None], queries[picked], jnp.zeros((), queries.dtype))
+    query_rows = queries.reshape(requests, kept_rows * topk_count, head_width)
+    outgoing = jnp.where(
+        any_mine[:, None, None],
+        jnp.where((picked == 1)[:, None, None], query_rows[1][None], query_rows[0][None]),
+        jnp.zeros((), query_rows.dtype),
+    )
     incoming = lax.all_to_all(outgoing, "grp", 0, 0, tiled=True)
 
     my_slots = lax.dynamic_slice_in_dim(slot_request, group_idx * slot_count, slot_count)
-    slot_queries = incoming[my_slots // requests]
+    slot_queries = incoming[my_slots // requests].reshape(
+        slot_count, kept_rows, topk_count, head_width
+    )
     cache_keys = cache_kv[:, 0]
     cache_values = cache_kv[:, 1]
     slot_scores = (
@@ -90,15 +97,32 @@
         slot_scores, in_cache, cache_values, "sakc,scw->sakw"
     )
 
-    packed = jnp.concatenate([slot_num, slot_den[..., None], slot_peak[..., None]], axis=-1)
+    peak_low = lax.reduce_precision(slot_peak, exponent_bits=8, mantissa_bits=7)
+    shift = jnp.exp(slot_peak - peak_low)
+    shifted_num = slot_num * shift[..., None]
+    shifted_den = slot_den * shift
+    den_high = lax.reduce_precision(shifted_den, exponent_bits=8, mantissa_bits=7)
+    den_rest = shifted_den - den_high
+    row_count = kept_rows * topk_count
+    facts = jnp.stack(
+        [v.reshape(slot_count, row_count) for v in (peak_low, den_high, den_rest)], axis=1
+    ).astype(jnp.bfloat16)
+    facts = jnp.pad(facts, ((0, 0), (0, row_count - 3), (0, head_width - row_count)))
+    packed = jnp.concatenate(
+        [shifted_num.astype(jnp.bfloat16).reshape(slot_count, row_count, head_width), facts],
+        axis=1,
+    )
     to_home = (my_slots // requests)[None, :] == jnp.arange(group_count, dtype=jnp.int32)[:, None]
-    returning = jnp.sum(
-        jnp.where(to_home[:, :, None, None, None], packed[None], 0.0), axis=1
+    returning = jnp.zeros((), packed.dtype)
+    for i in range(slot_count):
+        returning = jnp.where(to_home[:, i, None, None], packed[i][None], returning)
+    back = lax.all_to_all(returning, "grp", 0, 0, tiled=True)
+    back_num = back[:, :row_count].astype(jnp.float32).reshape(
+        group_count, kept_rows, topk_count, head_width
     )
-    back = lax.all_to_all(returning, "grp", 0, 0, tiled=True)
-    back_num = back[..., :head_width]
-    back_den = back[..., head_width]
-    back_peak = back[..., head_width + 1]
+    back_facts = back[:, row_count:row_count + 3, :row_count].astype(jnp.float32)
+    back_peak = back_facts[:, 0].reshape(group_count, kept_rows, topk_count)
+    back_den = (back_facts[:, 1] + back_facts[:, 2]).reshape(group_count, kept_rows, topk_count)
 
     home_ids = group_idx * requests + jnp.arange(requests, dtype=jnp.int32)
     matched = jnp.any(slot_table[None, :, :] == home_ids[:, None, None], axis=2)

time: 114 us -> 99.3 us (0.87)
  waiting for transfers between devices: 39.6 us -> 28.7 us
  local copies, waits for them, and re-layouts: 9.75 us -> 5.71 us
    all_to_all x1, waiting for transfers between devices: 27.4 us -> 16.6 us  [on_device(): back = lax.all_to_all(returning, 'grp', 0, 0, tiled=True)]
    unnamed x13 -> x12, local copies, waits for them, and re-layouts: 3.37 us -> 0.89 us
    reduce_sum x1 -> x0, other arithmetic: 1.41 us -> none  [on_device(): jnp.sum(jnp.where(to_home[:, :, None, None, None], packed[None], 0.0), ax...]
  transfers between devices with their start and end apart: 2 -> 2, of which waited for: 2 -> 2; matrix products, arithmetic and copies ran while one was open for 3% -> 4% of each run, Pallas kernels for 0% -> 0%
where the time goes in v2:
time: 99.3 us; the launch traced here: 98.8 us
  waiting for transfers between devices  28.7 us (29%)
  starting transfers between devices  28.4 us (29%)
  blocking collectives  24.4 us (25%)
  matrix products  5.88 us (6%)
  local copies, waits for them, and re-layouts  5.71 us (6%)
  other arithmetic  5.41 us (5%)
    all_gather x1, blocking collectives, on_device(): hidden = lax.all_gather(draft_hidden, 'mdl', axis=2, tiled=True)  24.4 us
    all_to_all x1, starting transfers between devices, on_device(): incoming = lax.all_to_all(outgoing, 'grp', 0, 0, tiled=True)  22.1 us
    all_to_all x1, waiting for transfers between devices, on_device(): back = lax.all_to_all(returning, 'grp', 0, 0, tiled=True)  16.6 us
    all_to_all x1, waiting for transfers between devices, on_device(): incoming = lax.all_to_all(outgoing, 'grp', 0, 0, tiled=True)  12.1 us
    all_to_all x1, starting transfers between devices, on_device(): back = lax.all_to_all(returning, 'grp', 0, 0, tiled=True)  6.26 us
  transfers between devices with their start and end apart: 2, of which 2 were waited for; matrix products, arithmetic and copies ran while one was open for 4% of the time, Pallas kernels for 0%

profile of v2, /device:TPU:1, one launch (start us, length us, event | category | flops | bytes accessed | tf_op | source)
XLA Modules:
  0.0 98.8 jit_solution(17956994910120072349)
XLA Ops:
  0.0 0.8 compare_and_fusion
  0.8 0.7 bitcast_or_fusion
  1.6 0.8 eq.66
  2.7 0.8 copy.63
  3.5 0.6 gather_fusion.1
  4.2 24.4 %all_gather.3 = bf16[2,32,2048]{2,1,0:T(8,128)(2,1)S(1)} all-gather(bf16[2,32,256]{2,1,0:T(8,128)(2,1)} %param.10), channel_id=1, replica_groups=mesh['grp'=64,'mdl'=8] {'mdl'}, dimensions={2}, use_global_device_ids=true | all-gather | bytes 294912 | tf_op jit(solution)/shard_map/all_gather | solution.py:43
  28.6 0.8 gather_fusion.2
  29.5 0.4 fusion.1
  30.0 0.9 select_select_fusion.1
  30.9 22.1 %all-to-all-start = ((bf16[64,16,128]{2,1,0:T(8,128)(2,1)}), bf16[64,16,128]{2,1,0:T(8,128)(2,1)S(1)}, u32[]{:S(2)}, u32[]{:S(2)}) async-start(bf16[64,16,128]{2,1,0:T(8,128)(2,1)} %select_select_fusion.1), calls=%async_computation | async-start | bytes 524288 | tf_op jit(solution)/shard_map/all_to_all | solution.py:81
  53.3 0.6 gather_fusion.3
  54.0 0.6 fusion.19
  54.8 12.1 %all-to-all-done = bf16[64,16,128]{2,1,0:T(8,128)(2,1)S(1)} async-done(((bf16[64,16,128]{2,1,0:T(8,128)(2,1)}), bf16[64,16,128]{2,1,0:T(8,128)(2,1)S(1)}, u32[]{:S(2)}, u32[]{:S(2)}) %all-to-all-start) | async-done | bytes 262176 | tf_op jit(solution)/shard_map/all_to_all | solution.py:81
  66.9 0.6 gather_fusion
  67.5 1.5 %fusion.55 = (f32[3,8,2]{1,2,0:T(2,128)S(1)}, f32[3,8,2,1024]{3,1,2,0:T(8,128)S(1)}) fusion(bf16[3,2,1024,128]{3,2,1,0:T(8,128)(2,1)} %param.17, bf16[3,8,2,128]{3,2,1,0:T(2,128)(2,1)S(1)} %bitcast.90, pred[3,1024]{1,0:T(4,128)(4,1)S(1)} %iota_compare_fusion.2), kind=kOutput, calls=%fused_computation.120 | convolution fusion | flops 12730320 | bytes 998592 | tf_op jit(solution)/shard_map/sakw,scw->sakc/dot_general | solution.py:90
  69.3 1.4 %fusion.4 = bf16[3,8,2,128]{3,1,2,0:T(8,128)(2,1)S(1)} fusion(bf16[3,2,1024,128]{3,2,1,0:T(8,128)(2,1)} %param.17, f32[3,8,2,1024]{3,1,2,0:T(8,128)S(1)} %get-tuple-element.25, f32[3,8,2]{1,2,0:T(2,128)S(1)} %get-tuple-element.24, f32[3,8,2]{1,2,0:T(2,128)S(1)} %fusion.45), kind=kOutput, calls=%fused_computation.11 | convolution fusion | flops 12693504 | bytes 995712 | tf_op jit(solution)/shard_map/sakc,scw->sakw/dot_general | solution.py:14
  71.1 1.1 %select_select_fusion = bf16[64,32,128]{2,1,0:T(8,128)(2,1)} fusion(pred[64]{0:T(512)(128)(4,1)S(1)} %get-tuple-element.22, pred[64]{0:T(512)(128)(4,1)S(1)} %get-tuple-element.23, pred[64]{0:T(512)(128)(4,1)S(1)} %get-tuple-element.21, bf16[32,128]{1,0:T(8,128)(2,1)S(1)} %get-tuple-element.14, bf16[32,128]{1,0:T(8,128)(2,1)S(1)} %get-tuple-element.15, ...), kind=kLoop, calls=%fused_computation.27 | loop fusion | flops 786432 | bytes 549056 | tf_op jit(solution)/shard_map/jit(_where)/select_n | solution.py:118
  72.2 6.3 %all-to-all-start.1 = ((bf16[64,32,128]{2,1,0:T(8,128)(2,1)}), bf16[64,32,128]{2,1,0:T(8,128)(2,1)S(1)}, u32[]{:S(2)}, u32[]{:S(2)}) async-start(bf16[64,32,128]{2,1,0:T(8,128)(2,1)} %select_select_fusion), calls=%async_computation.1 | async-start | bytes 1048576 | tf_op jit(solution)/shard_map/all_to_all | solution.py:119
  78.5 1.5 %convolution_convert_fusion = bf16[2,32,2,128]{3,1,2,0:T(8,128)(2,1)S(1)} fusion(bf16[2,2048,128]{2,1,0:T(8,128)(2,1)} %param.12, bf16[2,32,2048]{2,1,0:T(8,128)(2,1)S(1)} %all_gather.3), kind=kOutput, calls=%fused_computation.9 | convolution fusion | flops 67125248 | bytes 1343488 | tf_op jit(solution)/shard_map/rtd,cdw->rtcw/dot_general | solution.py:49
  80.0 0.2 fusion.56
  80.5 16.6 %all-to-all-done.1 = bf16[64,32,128]{2,1,0:T(8,128)(2,1)S(1)} async-done(((bf16[64,32,128]{2,1,0:T(8,128)(2,1)}), bf16[64,32,128]{2,1,0:T(8,128)(2,1)S(1)}, u32[]{:S(2)}, u32[]{:S(2)}) %all-to-all-start.1) | async-done | bytes 524320 | tf_op jit(solution)/shard_map/all_to_all | solution.py:119
  97.7 0.3 multiply_reduce_fusion
  98.0 0.2 fusion.9
  98.2 0.6 copy.83
  (59 shorter events, 2.5 us)
Async XLA Ops:
  0.0 29.4 %copy-start = (bf16[4,2048,128]{2,1,0:T(8,128)(2,1)S(1)}, bf16[4,2048,128]{2,1,0:T(8,128)(2,1)}, u32[]{:S(2)}) copy-start(bf16[4,2048,128]{2,1,0:T(8,128)(2,1)} %param.11) | copy-start | bytes 6291460
  29.4 23.7 %copy-start.2 = (s32[192]{0:T(256)S(1)}, s32[192]{0:T(256)}, u32[]{:S(2)}) copy-start(s32[192]{0:T(256)} %param.19) | copy-start | bytes 2308
  29.4 23.9 %copy-start.1 = (s32[2,32,32]{2,1,0:T(8,128)S(1)}, s32[2,32,32]{2,1,0:T(8,128)}, u32[]{:S(2)}) copy-start(s32[2,32,32]{2,1,0:T(8,128)} %param.15) | copy-start | bytes 24580
  29.4 24.5 %copy-start.4 = (f32[2048,4]{0,1:T(4,128)S(1)}, f32[2048,4]{0,1:T(4,128)}, u32[]{:S(2)}) copy-start(f32[2048,4]{0,1:T(4,128)} %param.13) | copy-start | bytes 98308
  29.5 25.3 %copy-start.3 = (s32[3]{0:T(128)S(1)}, s32[3]{0:T(128)}, u32[]{:S(2)}) copy-start(s32[3]{0:T(128)} %param.18) | copy-start | bytes 40
  30.9 36.0 %all-to-all-start = ((bf16[64,16,128]{2,1,0:T(8,128)(2,1)}), bf16[64,16,128]{2,1,0:T(8,128)(2,1)S(1)}, u32[]{:S(2)}, u32[]{:S(2)}) async-start(bf16[64,16,128]{2,1,0:T(8,128)(2,1)} %select_select_fusion.1), calls=%async_computation | async-start | bytes 524288 | tf_op jit(solution)/shard_map/all_to_all | solution.py:81
  72.2 24.9 %all-to-all-start.1 = ((bf16[64,32,128]{2,1,0:T(8,128)(2,1)}), bf16[64,32,128]{2,1,0:T(8,128)(2,1)S(1)}, u32[]{:S(2)}, u32[]{:S(2)}) async-start(bf16[64,32,128]{2,1,0:T(8,128)(2,1)} %select_select_fusion), calls=%async_computation.1 | async-start | bytes 1048576 | tf_op jit(solution)/shard_map/all_to_all | solution.py:119

commit v3 on v2

--- a/solution.py
+++ b/solution.py
@@ -40,7 +40,15 @@
     slot_count = cache_kv.shape[0]
     cache_size = cache_kv.shape[2]
 
-    hidden = lax.all_gather(draft_hidden, "mdl", axis=2, tiled=True)
+    model_count = lax.axis_size("mdl")
+    hidden_parts = lax.all_to_all(
+        jnp.broadcast_to(draft_hidden[None], (model_count,) + draft_hidden.shape),
+        "mdl",
+        0,
+        0,
+        tiled=True,
+    )
+    hidden = hidden_parts.transpose(1, 2, 0, 3).reshape(requests, drafts, model_count * part_width)
     acc_hidden = jnp.take_along_axis(hidden, accepted[:, :, None], axis=1)
     acc_routes = jnp.take_along_axis(routes, accepted[:, :, None], axis=1)
     acc_mask = jnp.take_along_axis(tree_mask, accepted[:, :, None], axis=1)

time: 99.3 us -> 80.4 us (0.81)
  blocking collectives: 24.4 us -> 0 us
  local copies, waits for them, and re-layouts: 5.71 us -> 8.36 us
  starting transfers between devices: 28.4 us -> 29.9 us
    all_gather x1 -> x0, blocking collectives: 24.4 us -> none  [on_device(): hidden = lax.all_gather(draft_hidden, 'mdl', axis=2, tiled=True)]
    all_to_all x0 -> x1, starting transfers between devices: none -> 6.66 us  [on_device(): lax.all_to_all(jnp.broadcast_to(draft_hidden[None], (model_count,) + draf...]
    all_to_all x1, starting transfers between devices: 22.1 us -> 17 us  [on_device(): incoming = lax.all_to_all(outgoing, 'grp', 0, 0, tiled=True)]
    broadcast_in_dim x0 -> x1, local copies, waits for them, and re-layouts: none -> 1.62 us  [on_device(): jnp.broadcast_to(draft_hidden[None], (model_count,) + draft_hidden.shape)]
    all_to_all x1, waiting for transfers between devices: 12.1 us -> 13.7 us  [on_device(): incoming = lax.all_to_all(outgoing, 'grp', 0, 0, tiled=True)]
  transfers between devices with their start and end apart: 2 -> 3, of which waited for: 2 -> 2; matrix products, arithmetic and copies ran while one was open for 4% -> 12% of each run, Pallas kernels for 0% -> 0%
where the time goes in v3:
time: 80.4 us; the launch traced here: 79.8 us
  starting transfers between devices  29.9 us (37%)
  waiting for transfers between devices  29.4 us (37%)
  local copies, waits for them, and re-layouts  8.36 us (10%)
  other arithmetic  5.92 us (7%)
  matrix products  5.89 us (7%)
    all_to_all x1, starting transfers between devices, on_device(): incoming = lax.all_to_all(outgoing, 'grp', 0, 0, tiled=True)  17 us
    all_to_all x1, waiting for transfers between devices, on_device(): back = lax.all_to_all(returning, 'grp', 0, 0, tiled=True)  15.7 us
    all_to_all x1, waiting for transfers between devices, on_device(): incoming = lax.all_to_all(outgoing, 'grp', 0, 0, tiled=True)  13.7 us
    all_to_all x1, starting transfers between devices, on_device(): lax.all_to_all(jnp.broadcast_to(draft_hidden[None], (model_count,) + draf...  6.66 us
    all_to_all x1, starting transfers between devices, on_device(): back = lax.all_to_all(returning, 'grp', 0, 0, tiled=True)  6.32 us
    broadcast_in_dim x1, local copies, waits for them, and re-layouts, on_device(): jnp.broadcast_to(draft_hidden[None], (model_count,) + draft_hidden.shape)  1.62 us
  transfers between devices with their start and end apart: 3, of which 2 were waited for; matrix products, arithmetic and copies ran while one was open for 12% of the time, Pallas kernels for 0%

profile of v3, /device:TPU:1, one launch (start us, length us, event | category | flops | bytes accessed | tf_op | source)
XLA Modules:
  0.0 79.8 jit_solution(17784843972178306900)
XLA Ops:
  0.0 1.6 %broadcast_in_dim.242 = bf16[8,2,32,256]{3,2,1,0:T(8,128)(2,1)} broadcast(bf16[2,32,256]{2,1,0:T(8,128)(2,1)} %param.10), dimensions={1,2,3} | broadcast | bytes 294912 | tf_op jit(solution)/shard_map/broadcast_in_dim | solution.py:45
  1.6 6.7 %all-to-all-start = ((bf16[8,2,32,256]{3,2,1,0:T(8,128)(2,1)}), bf16[8,2,32,256]{3,2,1,0:T(8,128)(2,1)S(1)}, u32[]{:S(2)}, u32[]{:S(2)}) async-start(bf16[8,2,32,256]{3,2,1,0:T(8,128)(2,1)} %broadcast_in_dim.242), calls=%async_computation | async-start | bytes 524288 | tf_op jit(solution)/shard_map/all_to_all | solution.py:44
  8.3 0.7 compare_and_fusion
  9.0 0.7 bitcast_or_fusion
  9.7 0.8 %eq.66 = s32[64,3]{1,0:T(8,128)S(1)} reshape(s32[192]{0:T(256)} %param.19) | data formatting | bytes 1536 | tf_op jit(solution)/shard_map/eq | solution.py:136
  10.7 0.8 compare_select_fusion.1
  11.7 0.8 copy.64
  12.5 0.6 gather_fusion.1
  13.3 1.4 %gather_fusion.3 = s32[16,32]{1,0:T(8,128)S(1)} fusion(s32[2,32,32]{2,1,0:T(8,128)} %param.15, s32[16]{0:T(128)S(1)} %reshape.185), kind=kCustom, calls=%fused_computation.3 | custom fusion | bytes 4224 | tf_op jit(solution)/shard_map/jit(take_along_axis)/gather | solution.py:54
  14.7 0.8 gather_fusion.2
  15.6 0.4 fusion.1
  16.1 0.9 %select_select_fusion.1 = bf16[64,16,128]{2,1,0:T(8,128)(2,1)} fusion(pred[64]{0:T(512)(128)(4,1)S(1)} %broadcast_compare_fusion, pred[64]{0:T(512)(128)(4,1)S(1)} %get-tuple-element.11, bf16[16,128]{1,0:T(8,128)(2,1)S(1)} %bitcast.102, bf16[16,128]{1,0:T(8,128)(2,1)S(1)} %bitcast.101), kind=kLoop, calls=%fused_computation.30 | loop fusion | flops 262144 | bytes 270464 | tf_op jit(solution)/shard_map/jit(_where)/select_n | solution.py:84
  17.0 17.0 %all-to-all-start.1 = ((bf16[64,16,128]{2,1,0:T(8,128)(2,1)}), bf16[64,16,128]{2,1,0:T(8,128)(2,1)S(1)}, u32[]{:S(2)}, u32[]{:S(2)}) async-start(bf16[64,16,128]{2,1,0:T(8,128)(2,1)} %select_select_fusion.1), calls=%async_computation.1 | async-start | bytes 524288 | tf_op jit(solution)/shard_map/all_to_all | solution.py:89
  34.2 13.7 %all-to-all-done.1 = bf16[64,16,128]{2,1,0:T(8,128)(2,1)S(1)} async-done(((bf16[64,16,128]{2,1,0:T(8,128)(2,1)}), bf16[64,16,128]{2,1,0:T(8,128)(2,1)S(1)}, u32[]{:S(2)}, u32[]{:S(2)}) %all-to-all-start.1) | async-done | bytes 262176 | tf_op jit(solution)/shard_map/all_to_all | solution.py:89
  47.8 0.6 gather_fusion
  48.4 1.5 %fusion.55 = (f32[3,8,2]{1,2,0:T(2,128)S(1)}, f32[3,8,2,1024]{3,1,2,0:T(8,128)S(1)}) fusion(bf16[3,2,1024,128]{3,2,1,0:T(8,128)(2,1)} %param.17, bf16[3,8,2,128]{3,2,1,0:T(2,128)(2,1)S(1)} %bitcast.96, pred[3,1024]{1,0:T(4,128)(4,1)S(1)} %iota_compare_fusion.2), kind=kOutput, calls=%fused_computation.120 | convolution fusion | flops 12730320 | bytes 998592 | tf_op jit(solution)/shard_map/sakw,scw->sakc/dot_general | solution.py:98
  50.2 1.4 %fusion.4 = bf16[3,8,2,128]{3,1,2,0:T(8,128)(2,1)S(1)} fusion(bf16[3,2,1024,128]{3,2,1,0:T(8,128)(2,1)} %param.17, f32[3,8,2,1024]{3,1,2,0:T(8,128)S(1)} %get-tuple-element.25, f32[3,8,2]{1,2,0:T(2,128)S(1)} %get-tuple-element.24, f32[3,8,2]{1,2,0:T(2,128)S(1)} %fusion.45), kind=kOutput, calls=%fused_computation.11 | convolution fusion | flops 12693504 | bytes 995712 | tf_op jit(solution)/shard_map/sakc,scw->sakw/dot_general | solution.py:14
  52.0 1.1 %select_select_fusion = bf16[64,32,128]{2,1,0:T(8,128)(2,1)} fusion(pred[64]{0:T(512)(128)(4,1)S(1)} %get-tuple-element.22, pred[64]{0:T(512)(128)(4,1)S(1)} %get-tuple-element.23, pred[64]{0:T(512)(128)(4,1)S(1)} %get-tuple-element.21, bf16[32,128]{1,0:T(8,128)(2,1)S(1)} %get-tuple-element.14, bf16[32,128]{1,0:T(8,128)(2,1)S(1)} %get-tuple-element.15, ...), kind=kLoop, calls=%fused_computation.27 | loop fusion | flops 786432 | bytes 549056 | tf_op jit(solution)/shard_map/jit(_where)/select_n | solution.py:126
  53.1 6.3 %all-to-all-start.2 = ((bf16[64,32,128]{2,1,0:T(8,128)(2,1)}), bf16[64,32,128]{2,1,0:T(8,128)(2,1)S(1)}, u32[]{:S(2)}, u32[]{:S(2)}) async-start(bf16[64,32,128]{2,1,0:T(8,128)(2,1)} %select_select_fusion), calls=%async_computation.2 | async-start | bytes 1048576 | tf_op jit(solution)/shard_map/all_to_all | solution.py:127
  59.4 0.6 fusion.19
  60.3 1.5 %convolution_convert_fusion = bf16[2,32,2,128]{3,1,2,0:T(8,128)(2,1)S(1)} fusion(bf16[2,2048,128]{2,1,0:T(8,128)(2,1)} %param.12, bf16[2,32,2048,1]{2,1,0,3:T(8,128)(2,1)S(1)} %reshape.212), kind=kOutput, calls=%fused_computation.9 | convolution fusion | flops 67125248 | bytes 1343488 | tf_op jit(solution)/shard_map/rtd,cdw->rtcw/dot_general | solution.py:57
  62.3 15.7 %all-to-all-done.2 = bf16[64,32,128]{2,1,0:T(8,128)(2,1)S(1)} async-done(((bf16[64,32,128]{2,1,0:T(8,128)(2,1)}), bf16[64,32,128]{2,1,0:T(8,128)(2,1)S(1)}, u32[]{:S(2)}, u32[]{:S(2)}) %all-to-all-start.2) | async-done | bytes 524320 | tf_op jit(solution)/shard_map/all_to_all | solution.py:127
  78.6 0.3 multiply_reduce_fusion
  79.2 0.6 copy.85
  (60 shorter events, 3.1 us)
Async XLA Ops:
  0.0 15.5 %copy-start = (bf16[4,2048,128]{2,1,0:T(8,128)(2,1)S(1)}, bf16[4,2048,128]{2,1,0:T(8,128)(2,1)}, u32[]{:S(2)}) copy-start(bf16[4,2048,128]{2,1,0:T(8,128)(2,1)} %param.11) | copy-start | bytes 6291460
  1.6 13.1 %all-to-all-start = ((bf16[8,2,32,256]{3,2,1,0:T(8,128)(2,1)}), bf16[8,2,32,256]{3,2,1,0:T(8,128)(2,1)S(1)}, u32[]{:S(2)}, u32[]{:S(2)}) async-start(bf16[8,2,32,256]{3,2,1,0:T(8,128)(2,1)} %broadcast_in_dim.242), calls=%async_computation | async-start | bytes 524288 | tf_op jit(solution)/shard_map/all_to_all | solution.py:44
  15.5 18.5 %copy-start.1 = (s32[3]{0:T(128)S(1)}, s32[3]{0:T(128)}, u32[]{:S(2)}) copy-start(s32[3]{0:T(128)} %param.18) | copy-start | bytes 40
  17.0 30.8 %all-to-all-start.1 = ((bf16[64,16,128]{2,1,0:T(8,128)(2,1)}), bf16[64,16,128]{2,1,0:T(8,128)(2,1)S(1)}, u32[]{:S(2)}, u32[]{:S(2)}) async-start(bf16[64,16,128]{2,1,0:T(8,128)(2,1)} %select_select_fusion.1), calls=%async_computation.1 | async-start | bytes 524288 | tf_op jit(solution)/shard_map/all_to_all | solution.py:89
  49.9 9.5 %copy-start.2 = (f32[2048,4]{0,1:T(4,128)S(1)}, f32[2048,4]{0,1:T(4,128)}, u32[]{:S(2)}) copy-start(f32[2048,4]{0,1:T(4,128)} %param.13) | copy-start | bytes 98308
  53.1 24.9 %all-to-all-start.2 = ((bf16[64,32,128]{2,1,0:T(8,128)(2,1)}), bf16[64,32,128]{2,1,0:T(8,128)(2,1)S(1)}, u32[]{:S(2)}, u32[]{:S(2)}) async-start(bf16[64,32,128]{2,1,0:T(8,128)(2,1)} %select_select_fusion), calls=%async_computation.2 | async-start | bytes 1048576 | tf_op jit(solution)/shard_map/all_to_all | solution.py:127

commit v4 on v3

--- a/solution.py
+++ b/solution.py
@@ -80,17 +80,30 @@
     mine = home_of == group_idx
     picked = jnp.sum(jnp.where(mine, local_of, 0), axis=1)
     any_mine = jnp.any(mine, axis=1)
-    query_rows = queries.reshape(requests, kept_rows * topk_count, head_width)
-    outgoing = jnp.where(
-        any_mine[:, None, None],
-        jnp.where((picked == 1)[:, None, None], query_rows[1][None], query_rows[0][None]),
-        jnp.zeros((), query_rows.dtype),
+    query_rows = queries.reshape(requests, kept_rows * topk_count * head_width)
+    send_pick = (
+        any_mine[:, None] & (picked[:, None] == jnp.arange(requests, dtype=jnp.int32)[None, :])
+    ).astype(query_rows.dtype)
+    outgoing = jnp.einsum(
+        "dr,rx->dx", send_pick, query_rows, preferred_element_type=jnp.float32
+    ).astype(query_rows.dtype)
+    incoming = lax.all_to_all(
+        outgoing.reshape(group_count, kept_rows * topk_count, head_width), "grp", 0, 0, tiled=True
     )
-    incoming = lax.all_to_all(outgoing, "grp", 0, 0, tiled=True)
 
     my_slots = lax.dynamic_slice_in_dim(slot_request, group_idx * slot_count, slot_count)
-    slot_queries = incoming[my_slots // requests].reshape(
-        slot_count, kept_rows, topk_count, head_width
+    take_pick = (
+        (my_slots // requests)[:, None] == jnp.arange(group_count, dtype=jnp.int32)[None, :]
+    ).astype(incoming.dtype)
+    slot_queries = (
+        jnp.einsum(
+            "sd,dx->sx",
+            take_pick,
+            incoming.reshape(group_count, -1),
+            preferred_element_type=jnp.float32,
+        )
+        .astype(incoming.dtype)
+        .reshape(slot_count, kept_rows, topk_count, head_width)
     )
     cache_keys = cache_kv[:, 0]
     cache_values = cache_kv[:, 1]
@@ -120,10 +133,16 @@
         [shifted_num.astype(jnp.bfloat16).reshape(slot_count, row_count, head_width), facts],
         axis=1,
     )
-    to_home = (my_slots // requests)[None, :] == jnp.arange(group_count, dtype=jnp.int32)[:, None]
-    returning = jnp.zeros((), packed.dtype)
-    for i in range(slot_count):
-        returning = jnp.where(to_home[:, i, None, None], packed[i][None], returning)
+    returning = (
+        jnp.einsum(
+            "ds,sx->dx",
+            take_pick.T,
+            packed.reshape(slot_count, -1),
+            preferred_element_type=jnp.float32,
+        )
+        .astype(packed.dtype)
+        .reshape(group_count, 2 * row_count, head_width)
+    )
     back = lax.all_to_all(returning, "grp", 0, 0, tiled=True)
     back_num = back[:, :row_count].astype(jnp.float32).reshape(
         group_count, kept_rows, topk_count, head_width

time: 80.4 us -> 80.2 us (level)
  other arithmetic: 5.92 us -> 3.18 us
  local copies, waits for them, and re-layouts: 8.36 us -> 9.47 us
  matrix products: 5.89 us -> 6.78 us
    select_n x3 -> x1, other arithmetic: 2.73 us -> 0.09 us  [on_device(): my_slots // requests]
    unnamed x8 -> x12, local copies, waits for them, and re-layouts: 0.88 us -> 2.52 us
    dot_general x0 -> x3, matrix products: none -> 0.89 us  [the longest x1 0.41 us: on_device(): jnp.einsum('ds,sx->dx', take_pick.T, packed.reshape(slot_count, -1), pref...]
  transfers between devices with their start and end apart: 3 -> 3, of which waited for: 2 -> 3; matrix products, arithmetic and copies ran while one was open for 12% -> 11% of each run, Pallas kernels for 0% -> 0%
where the time goes in v4:
time: 80.2 us; the launch traced here: 79.6 us
  starting transfers between devices  30.1 us (38%)
  waiting for transfers between devices  29.9 us (37%)
  local copies, waits for them, and re-layouts  9.47 us (12%)
  matrix products  6.78 us (8%)
  other arithmetic  3.18 us (4%)
    all_to_all x1, starting transfers between devices, on_device(): lax.all_to_all(outgoing.reshape(group_count, kept_rows * topk_count, head...  17.3 us
    all_to_all x1, waiting for transfers between devices, on_device(): back = lax.all_to_all(returning, 'grp', 0, 0, tiled=True)  15.7 us
    all_to_all x1, waiting for transfers between devices, on_device(): lax.all_to_all(outgoing.reshape(group_count, kept_rows * topk_count, head...  13.6 us
    all_to_all x1, starting transfers between devices, on_device(): lax.all_to_all(jnp.broadcast_to(draft_hidden[None], (model_count,) + draf...  6.66 us
    all_to_all x1, starting transfers between devices, on_device(): back = lax.all_to_all(returning, 'grp', 0, 0, tiled=True)  6.07 us
    unnamed x12, local copies, waits for them, and re-layouts  2.52 us
    broadcast_in_dim x1, local copies, waits for them, and re-layouts, on_device(): jnp.broadcast_to(draft_hidden[None], (model_count,) + draft_hidden.shape)  1.62 us
    dot_general x2, matrix products, softmax_piece(): jnp.einsum(contract, weights_low, values, preferred_element_type=jnp.floa...  1.6 us
  transfers between devices with their start and end apart: 3, of which 3 were waited for; matrix products, arithmetic and copies ran while one was open for 11% of the time, Pallas kernels for 0%

profile of v4, /device:TPU:1, one launch (start us, length us, event | category | flops | bytes accessed | tf_op | source)
XLA Modules:
  0.0 79.6 jit_solution(1673587308852755204)
XLA Ops:
  0.0 1.6 %broadcast_in_dim.142 = bf16[8,2,32,256]{3,2,1,0:T(8,128)(2,1)} broadcast(bf16[2,32,256]{2,1,0:T(8,128)(2,1)} %param.10), dimensions={1,2,3} | broadcast | bytes 294912 | tf_op jit(solution)/shard_map/broadcast_in_dim | solution.py:45
  1.6 6.7 %all-to-all-start = ((bf16[8,2,32,256]{3,2,1,0:T(8,128)(2,1)}), bf16[8,2,32,256]{3,2,1,0:T(8,128)(2,1)S(1)}, u32[]{:S(2)}, u32[]{:S(2)}) async-start(bf16[8,2,32,256]{3,2,1,0:T(8,128)(2,1)} %broadcast_in_dim.142), calls=%async_computation | async-start | bytes 524288 | tf_op jit(solution)/shard_map/all_to_all | solution.py:44
  8.3 0.7 compare_and_fusion
  9.0 0.7 bitcast_or_fusion
  9.7 0.8 %eq.69 = s32[64,3]{1,0:T(8,128)S(1)} reshape(s32[192]{0:T(256)} %param.19) | data formatting | bytes 1536 | tf_op jit(solution)/shard_map/eq | solution.py:155
  10.7 0.8 copy.65
  11.5 0.6 gather_fusion
  12.3 1.4 %gather_fusion.2 = s32[16,32]{1,0:T(8,128)S(1)} fusion(s32[2,32,32]{2,1,0:T(8,128)} %param.15, s32[16]{0:T(128)S(1)} %reshape.186), kind=kCustom, calls=%fused_computation.2 | custom fusion | bytes 4224 | tf_op jit(solution)/shard_map/jit(take_along_axis)/gather | solution.py:54
  13.8 0.5 all-to-all-done
  14.4 0.8 gather_fusion.1
  15.2 0.4 fusion.1
  16.0 0.7 copy.97
  16.8 17.3 %all-to-all-start.1 = ((bf16[64,16,128]{2,1,0:T(8,128)(2,1)}), bf16[64,16,128]{2,1,0:T(8,128)(2,1)S(1)}, u32[]{:S(2)}, u32[]{:S(2)}) async-start(bf16[64,16,128]{2,1,0:T(8,128)(2,1)} %bitcast.42), calls=%async_computation.1 | async-start | bytes 524288 | tf_op jit(solution)/shard_map/all_to_all | solution.py:90
  34.3 13.6 %all-to-all-done.1 = bf16[64,16,128]{2,1,0:T(8,128)(2,1)S(1)} async-done(((bf16[64,16,128]{2,1,0:T(8,128)(2,1)}), bf16[64,16,128]{2,1,0:T(8,128)(2,1)S(1)}, u32[]{:S(2)}, u32[]{:S(2)}) %all-to-all-start.1) | async-done | bytes 262176 | tf_op jit(solution)/shard_map/all_to_all | solution.py:90
  48.2 1.5 %fusion.61 = (f32[3,8,2]{1,2,0:T(2,128)S(1)}, f32[3,8,2,1024]{3,1,2,0:T(8,128)S(1)}) fusion(bf16[3,2,1024,128]{3,2,1,0:T(8,128)(2,1)} %param.17, bf16[3,8,2,128]{3,2,1,0:T(2,128)(2,1)S(1)} %reshape.181, pred[3,1024]{1,0:T(4,128)(4,1)S(1)} %iota_compare_fusion.3), kind=kOutput, calls=%fused_computation.116 | convolution fusion | flops 12730320 | bytes 998592 | tf_op jit(solution)/shard_map/sakw,scw->sakc/dot_general | solution.py:111
  50.0 1.4 %fusion.6 = bf16[3,8,2,128]{3,1,2,0:T(8,128)(2,1)S(1)} fusion(bf16[3,2,1024,128]{3,2,1,0:T(8,128)(2,1)} %param.17, f32[3,8,2,1024]{3,1,2,0:T(8,128)S(1)} %get-tuple-element.15, f32[3,8,2]{1,2,0:T(2,128)S(1)} %get-tuple-element.14, f32[3,8,2]{1,2,0:T(2,128)S(1)} %fusion.50), kind=kOutput, calls=%fused_computation.15 | convolution fusion | flops 12693504 | bytes 995712 | tf_op jit(solution)/shard_map/sakc,scw->sakw/dot_general | solution.py:14
  51.8 0.4 fusion.3
  52.2 0.9 %copy.100 = bf16[8,8,32,128]{3,2,1,0:T(8,128)(2,1)} copy(bf16[8,8,32,128]{3,1,2,0:T(8,128)(2,1)S(1)} %fusion.3) | data formatting | bytes 1048576
  53.1 6.1 %all-to-all-start.2 = ((bf16[64,32,128]{2,1,0:T(8,128)(2,1)}), bf16[64,32,128]{2,1,0:T(8,128)(2,1)S(1)}, u32[]{:S(2)}, u32[]{:S(2)}) async-start(bf16[64,32,128]{2,1,0:T(8,128)(2,1)} %bitcast.48), calls=%async_computation.2 | async-start | bytes 1048576 | tf_op jit(solution)/shard_map/all_to_all | solution.py:146
  59.2 0.6 fusion.23
  60.1 1.5 %convolution_convert_fusion.3 = bf16[2,32,2,128]{3,1,2,0:T(8,128)(2,1)S(1)} fusion(bf16[2,2048,128]{2,1,0:T(8,128)(2,1)} %param.12, bf16[2,32,2048,1]{2,1,0,3:T(8,128)(2,1)S(1)} %reshape.212), kind=kOutput, calls=%fused_computation.13 | convolution fusion | flops 67125248 | bytes 1343488 | tf_op jit(solution)/shard_map/rtd,cdw->rtcw/dot_general | solution.py:57
  62.1 15.7 %all-to-all-done.2 = bf16[64,32,128]{2,1,0:T(8,128)(2,1)S(1)} async-done(((bf16[64,32,128]{2,1,0:T(8,128)(2,1)}), bf16[64,32,128]{2,1,0:T(8,128)(2,1)S(1)}, u32[]{:S(2)}, u32[]{:S(2)}) %all-to-all-start.2) | async-done | bytes 524320 | tf_op jit(solution)/shard_map/all_to_all | solution.py:146
  78.4 0.3 multiply_reduce_fusion
  79.0 0.6 copy.85
  (60 shorter events, 3.6 us)
Async XLA Ops:
  0.0 15.2 %copy-start = (bf16[4,2048,128]{2,1,0:T(8,128)(2,1)S(1)}, bf16[4,2048,128]{2,1,0:T(8,128)(2,1)}, u32[]{:S(2)}) copy-start(bf16[4,2048,128]{2,1,0:T(8,128)(2,1)} %param.11) | copy-start | bytes 6291460
  1.6 12.7 %all-to-all-start = ((bf16[8,2,32,256]{3,2,1,0:T(8,128)(2,1)}), bf16[8,2,32,256]{3,2,1,0:T(8,128)(2,1)S(1)}, u32[]{:S(2)}, u32[]{:S(2)}) async-start(bf16[8,2,32,256]{3,2,1,0:T(8,128)(2,1)} %broadcast_in_dim.142), calls=%async_computation | async-start | bytes 524288 | tf_op jit(solution)/shard_map/all_to_all | solution.py:44
  15.2 18.9 %copy-start.1 = (s32[192]{0:T(256)S(1)}, s32[192]{0:T(256)}, u32[]{:S(2)}) copy-start(s32[192]{0:T(256)} %param.19) | copy-start | bytes 2308
  15.2 19.0 %copy-start.2 = (s32[3]{0:T(128)S(1)}, s32[3]{0:T(128)}, u32[]{:S(2)}) copy-start(s32[3]{0:T(128)} %param.18) | copy-start | bytes 40
  16.8 31.2 %all-to-all-start.1 = ((bf16[64,16,128]{2,1,0:T(8,128)(2,1)}), bf16[64,16,128]{2,1,0:T(8,128)(2,1)S(1)}, u32[]{:S(2)}, u32[]{:S(2)}) async-start(bf16[64,16,128]{2,1,0:T(8,128)(2,1)} %bitcast.42), calls=%async_computation.1 | async-start | bytes 524288 | tf_op jit(solution)/shard_map/all_to_all | solution.py:90
  51.4 7.7 %copy-start.3 = (f32[2048,4]{0,1:T(4,128)S(1)}, f32[2048,4]{0,1:T(4,128)}, u32[]{:S(2)}) copy-start(f32[2048,4]{0,1:T(4,128)} %param.13) | copy-start | bytes 98308
  53.1 24.7 %all-to-all-start.2 = ((bf16[64,32,128]{2,1,0:T(8,128)(2,1)}), bf16[64,32,128]{2,1,0:T(8,128)(2,1)S(1)}, u32[]{:S(2)}, u32[]{:S(2)}) async-start(bf16[64,32,128]{2,1,0:T(8,128)(2,1)} %bitcast.48), calls=%async_computation.2 | async-start | bytes 1048576 | tf_op jit(solution)/shard_map/all_to_all | solution.py:146

commit v5 on v1

--- a/solution.py
+++ b/solution.py
@@ -1,6 +1,10 @@
 import jax
 import jax.numpy as jnp
+import functools
+
 from jax import lax
+from jax.experimental import pallas as pl
+from jax.experimental.pallas import tpu as pltpu
 from jax.sharding import PartitionSpec as P
 
 HEAD_SIZE = 128
@@ -13,6 +17,63 @@
     denominator = jnp.sum(weights_low.astype(jnp.float32), axis=-1)
     numerator = jnp.einsum(contract, weights_low, values, preferred_element_type=jnp.float32)
     return (peak_score, denominator, numerator)
+
+
+def slot_attention_kernel(home_ref, len_ref, incoming_ref, cache_ref, out_ref, *, scale):
+    slot_count = cache_ref.shape[0]
+    rows = incoming_ref.shape[1]
+    out_ref[...] = jnp.zeros(out_ref.shape, out_ref.dtype)
+    for i in range(slot_count):
+        home = home_ref[i]
+        scores = (
+            lax.dot_general(
+                incoming_ref[home],
+                cache_ref[i, 0],
+                (((1,), (1,)), ((), ())),
+                preferred_element_type=jnp.float32,
+            )
+            * scale
+        )
+        position = lax.broadcasted_iota(jnp.int32, scores.shape, 1)
+        masked = jnp.where(position < len_ref[i], scores, -jnp.inf)
+        peak = jnp.max(masked, axis=1, keepdims=True)
+        weights = jnp.exp(masked - peak).astype(jnp.bfloat16)
+        den = jnp.sum(weights.astype(jnp.float32), axis=1, keepdims=True)
+        num = jnp.dot(weights, cache_ref[i, 1], preferred_element_type=jnp.float32)
+        peak_low = peak.astype(jnp.bfloat16).astype(jnp.float32)
+        shift = jnp.exp(peak - peak_low)
+        shifted_den = den * shift
+        den_high = shifted_den.astype(jnp.bfloat16).astype(jnp.float32)
+        den_rest = shifted_den - den_high
+        lane = lax.broadcasted_iota(jnp.int32, (rows, out_ref.shape[2]), 1)
+        facts = jnp.where(
+            lane == 0,
+            peak_low,
+            jnp.where(lane == 1, den_high, jnp.where(lane == 2, den_rest, 0.0)),
+        )
+        out_ref[home, :rows, :] = (num * shift).astype(out_ref.dtype)
+        out_ref[home, rows:, :] = facts.astype(out_ref.dtype)
+
+
+def slot_attention(home, cache_len, incoming, cache_kv, scale):
+    groups, rows, width = incoming.shape
+    slot_count, _, cache_size, _ = cache_kv.shape
+    flops = 4 * slot_count * rows * cache_size * width
+    moved = 2 * (cache_kv.size + incoming.size + 2 * groups * rows * width)
+    return pl.pallas_call(
+        functools.partial(slot_attention_kernel, scale=scale),
+        out_shape=jax.ShapeDtypeStruct((groups, 2 * rows, width), incoming.dtype),
+        in_specs=[
+            pl.BlockSpec(memory_space=pltpu.SMEM),
+            pl.BlockSpec(memory_space=pltpu.SMEM),
+            pl.BlockSpec(memory_space=pltpu.VMEM),
+            pl.BlockSpec(memory_space=pltpu.VMEM),
+        ],
+        out_specs=pl.BlockSpec(memory_space=pltpu.VMEM),
+        cost_estimate=pl.CostEstimate(
+            flops=flops, transcendentals=slot_count * rows * cache_size, bytes_accessed=moved
+        ),
+    )(home, cache_len, incoming, cache_kv)
 
 
 def on_device(
@@ -40,7 +101,15 @@
     slot_count = cache_kv.shape[0]
     cache_size = cache_kv.shape[2]
 
-    hidden = lax.all_gather(draft_hidden, "mdl", axis=2, tiled=True)
+    model_count = lax.axis_size("mdl")
+    hidden_parts = lax.all_to_all(
+        jnp.broadcast_to(draft_hidden[None], (model_count,) + draft_hidden.shape),
+        "mdl",
+        0,
+        0,
+        tiled=True,
+    )
+    hidden = hidden_parts.transpose(1, 2, 0, 3).reshape(requests, drafts, model_count * part_width)
     acc_hidden = jnp.take_along_axis(hidden, accepted[:, :, None], axis=1)
     acc_routes = jnp.take_along_axis(routes, accepted[:, :, None], axis=1)
     acc_mask = jnp.take_along_axis(tree_mask, accepted[:, :, None], axis=1)
@@ -72,33 +141,27 @@
     mine = home_of == group_idx
     picked = jnp.sum(jnp.where(mine, local_of, 0), axis=1)
     any_mine = jnp.any(mine, axis=1)
-    outgoing = jnp.where(any_mine[:, None, None, None], queries[picked], jnp.zeros((), queries.dtype))
-    incoming = lax.all_to_all(outgoing, "grp", 0, 0, tiled=True)
+    query_rows = queries.reshape(requests, kept_rows * topk_count * head_width)
+    send_pick = (
+        any_mine[:, None] & (picked[:, None] == jnp.arange(requests, dtype=jnp.int32)[None, :])
+    ).astype(query_rows.dtype)
+    outgoing = jnp.einsum(
+        "dr,rx->dx", send_pick, query_rows, preferred_element_type=jnp.float32
+    ).astype(query_rows.dtype)
+    incoming = lax.all_to_all(
+        outgoing.reshape(group_count, kept_rows * topk_count, head_width), "grp", 0, 0, tiled=True
+    )
 
     my_slots = lax.dynamic_slice_in_dim(slot_request, group_idx * slot_count, slot_count)
-    slot_queries = incoming[my_slots // requests]
-    cache_keys = cache_kv[:, 0]
-    cache_values = cache_kv[:, 1]
-    slot_scores = (
-        jnp.einsum("sakw,scw->sakc", slot_queries, cache_keys, preferred_element_type=jnp.float32)
-        * score_scale
+    row_count = kept_rows * topk_count
+    returning = slot_attention(my_slots // requests, cache_len, incoming, cache_kv, score_scale)
+    back = lax.all_to_all(returning, "grp", 0, 0, tiled=True)
+    back_num = back[:, :row_count].astype(jnp.float32).reshape(
+        group_count, kept_rows, topk_count, head_width
     )
-    in_cache = (jnp.arange(cache_size, dtype=jnp.int32)[None, :] < cache_len[:, None])[
-        :, None, None, :
-    ]
-    slot_peak, slot_den, slot_num = softmax_piece(
-        slot_scores, in_cache, cache_values, "sakc,scw->sakw"
-    )
-
-    packed = jnp.concatenate([slot_num, slot_den[..., None], slot_peak[..., None]], axis=-1)
-    to_home = (my_slots // requests)[None, :] == jnp.arange(group_count, dtype=jnp.int32)[:, None]
-    returning = jnp.sum(
-        jnp.where(to_home[:, :, None, None, None], packed[None], 0.0), axis=1
-    )
-    back = lax.all_to_all(returning, "grp", 0, 0, tiled=True)
-    back_num = back[..., :head_width]
-    back_den = back[..., head_width]
-    back_peak = back[..., head_width + 1]
+    back_facts = back[:, row_count:, :3].astype(jnp.float32)
+    back_peak = back_facts[..., 0].reshape(group_count, kept_rows, topk_count)
+    back_den = (back_facts[..., 1] + back_facts[..., 2]).reshape(group_count, kept_rows, topk_count)
 
     home_ids = group_idx * requests + jnp.arange(requests, dtype=jnp.int32)
     matched = jnp.any(slot_table[None, :, :] == home_ids[:, None, None], axis=2)

time: 114 us -> 81.8 us (0.72)
  blocking collectives: 24.4 us -> 0 us
  waiting for transfers between devices: 39.6 us -> 29.4 us
  Pallas kernels: 0 us -> 3.3 us
  matrix products: 5.88 us -> 3.2 us
  starting transfers between devices: 28.4 us -> 30.2 us
    all_gather x1 -> x0, blocking collectives: 24.4 us -> none  [on_device(): hidden = lax.all_gather(draft_hidden, 'mdl', axis=2, tiled=True)]
    all_to_all x1, waiting for transfers between devices: 27.4 us -> 15.7 us  [on_device(): back = lax.all_to_all(returning, 'grp', 0, 0, tiled=True)]
    pallas_call x0 -> x1, Pallas kernels: none -> 3.3 us  [slot_attention(): pl.pallas_call(functools.partial(slot_attention_kernel, scale=scale), out...]
    all_to_all x1 -> x2, starting transfers between devices: 22.1 us -> 24.1 us  [the longest x1 17.5 us: on_device(): lax.all_to_all(outgoing.reshape(group_count, kept_rows * topk_count, head...]
    all_to_all x1 -> x2, waiting for transfers between devices: 12.2 us -> 13.7 us  [the longest x1 13.1 us: on_device(): lax.all_to_all(outgoing.reshape(group_count, kept_rows * topk_count, head...]
    dot_general x2 -> x1, matrix products: 1.61 us -> 0.2 us  [softmax_piece(): jnp.einsum(contract, weights_low, values, preferred_element_type=jnp.floa...]
    reduce_sum x1 -> x0, other arithmetic: 1.41 us -> none  [on_device(): jnp.sum(jnp.where(to_home[:, :, None, None, None], packed[None], 0.0), ax...]
    broadcast_in_dim x2, local copies, waits for them, and re-layouts: 0.22 us -> 1.63 us  [the longest x1 1.62 us: on_device(): jnp.broadcast_to(draft_hidden[None], (model_count,) + draft_hidden.shape)]
  transfers between devices with their start and end apart: 2 -> 3, of which waited for: 2 -> 3; matrix products, arithmetic and copies ran while one was open for 3% -> 11% of each run, Pallas kernels for 0% -> 0%
where the time goes in v5:
time: 81.8 us; the launch traced here: 81.2 us
  starting transfers between devices  30.2 us (37%)
  waiting for transfers between devices  29.4 us (36%)
  local copies, waits for them, and re-layouts  10.1 us (12%)
  other arithmetic  4.78 us (6%)
  Pallas kernels  3.3 us (4%)
  matrix products  3.2 us (4%)
    all_to_all x1, starting transfers between devices, on_device(): lax.all_to_all(outgoing.reshape(group_count, kept_rows * topk_count, head...  17.5 us
    all_to_all x1, waiting for transfers between devices, on_device(): back = lax.all_to_all(returning, 'grp', 0, 0, tiled=True)  15.7 us
    all_to_all x1, waiting for transfers between devices, on_device(): lax.all_to_all(outgoing.reshape(group_count, kept_rows * topk_count, head...  13.1 us
    all_to_all x1, starting transfers between devices, on_device(): lax.all_to_all(jnp.broadcast_to(draft_hidden[None], (model_count,) + draf...  6.66 us
    all_to_all x1, starting transfers between devices, on_device(): back = lax.all_to_all(returning, 'grp', 0, 0, tiled=True)  6.07 us
    pallas_call x1, Pallas kernels, slot_attention(): pl.pallas_call(functools.partial(slot_attention_kernel, scale=scale), out...  3.3 us
    unnamed x10, local copies, waits for them, and re-layouts  2.24 us
  transfers between devices with their start and end apart: 3, of which 3 were waited for; matrix products, arithmetic and copies ran while one was open for 11% of the time, Pallas kernels for 0%

profile of v5, /device:TPU:1, one launch (start us, length us, event | category | flops | bytes accessed | tf_op | source)
XLA Modules:
  0.0 81.2 jit_solution(10298804259593934295)
XLA Ops:
  0.0 1.6 %broadcast_in_dim.123 = bf16[8,2,32,256]{3,2,1,0:T(8,128)(2,1)} broadcast(bf16[2,32,256]{2,1,0:T(8,128)(2,1)} %param.10), dimensions={1,2,3} | broadcast | bytes 294912 | tf_op jit(solution)/shard_map/broadcast_in_dim | solution.py:106
  1.6 6.7 %all-to-all-start = ((bf16[8,2,32,256]{3,2,1,0:T(8,128)(2,1)}), bf16[8,2,32,256]{3,2,1,0:T(8,128)(2,1)S(1)}, u32[]{:S(2)}, u32[]{:S(2)}) async-start(bf16[8,2,32,256]{3,2,1,0:T(8,128)(2,1)} %broadcast_in_dim.123), calls=%async_computation | async-start | bytes 524288 | tf_op jit(solution)/shard_map/all_to_all | solution.py:105
  8.3 0.7 compare_and_fusion
  9.0 0.7 bitcast_or_fusion
  9.7 0.8 eq.56
  10.6 0.8 copy.43
  11.4 1.4 %gather_fusion.2 = s32[16,32]{1,0:T(8,128)S(1)} fusion(s32[2,32,32]{2,1,0:T(8,128)} %param.15, s32[16]{0:T(128)S(1)} %reshape.89), kind=kCustom, calls=%fused_computation.2 | custom fusion | bytes 4224 | tf_op jit(solution)/shard_map/jit(take_along_axis)/gather | solution.py:115
  12.8 0.6 gather_fusion
  13.7 0.6 all-to-all-done
  14.4 0.8 gather_fusion.1
  15.2 0.4 fusion.1
  16.0 0.7 copy.62
  16.8 17.5 %all-to-all-start.1 = ((bf16[64,16,128]{2,1,0:T(8,128)(2,1)}), bf16[64,16,128]{2,1,0:T(8,128)(2,1)S(1)}, u32[]{:S(2)}, u32[]{:S(2)}) async-start(bf16[64,16,128]{2,1,0:T(8,128)(2,1)} %bitcast.29), calls=%async_computation.1 | async-start | bytes 524288 | tf_op jit(solution)/shard_map/all_to_all | solution.py:151
  34.2 0.6 and_select_fusion.home_ref
  35.0 13.1 %all-to-all-done.1.incoming_ref = bf16[64,16,128]{2,1,0:T(8,128)(2,1)S(1)} async-done(((bf16[64,16,128]{2,1,0:T(8,128)(2,1)}), bf16[64,16,128]{2,1,0:T(8,128)(2,1)S(1)}, u32[]{:S(2)}, u32[]{:S(2)}) %all-to-all-start.1) | async-done | bytes 262176 | tf_op jit(solution)/shard_map/all_to_all | solution.py:151
  48.1 0.7 copy-done.1
  48.8 3.3 %shard_map.100 = bf16[64,32,128]{2,1,0:T(8,128)(2,1)} custom-call(s32[3]{0:T(128)} %and_select_fusion.home_ref, s32[3]{0:T(128)} %len_ref.1, bf16[64,16,128]{2,1,0:T(8,128)(2,1)} %copy-done.1, bf16[3,2,1024,128]{3,2,1,0:T(8,128)(2,1)} %cache_ref.1), custom_call_target="tpu_custom_call" | custom-call | flops 25165824 | bytes 2359296 | tf_op jit(solution)/shard_map/pallas_call | solution.py:63
  52.1 6.1 %all-to-all-start.2 = ((bf16[64,32,128]{2,1,0:T(8,128)(2,1)}), bf16[64,32,128]{2,1,0:T(8,128)(2,1)S(1)}, u32[]{:S(2)}, u32[]{:S(2)}) async-start(bf16[64,32,128]{2,1,0:T(8,128)(2,1)} %shard_map.100), calls=%async_computation.2 | async-start | bytes 1048576 | tf_op jit(solution)/shard_map/all_to_all | solution.py:158
  58.2 0.6 fusion.14
  59.1 1.5 %convolution_convert_fusion.1 = bf16[2,32,2,128]{3,1,2,0:T(8,128)(2,1)S(1)} fusion(bf16[2,2048,128]{2,1,0:T(8,128)(2,1)} %param.12, bf16[2,32,2048,1]{2,1,0,3:T(8,128)(2,1)S(1)} %reshape.115), kind=kOutput, calls=%fused_computation.8 | convolution fusion | flops 67125248 | bytes 1343488 | tf_op jit(solution)/shard_map/rtd,cdw->rtcw/dot_general | solution.py:118
  61.0 15.7 %all-to-all-done.2 = bf16[64,32,128]{2,1,0:T(8,128)(2,1)S(1)} async-done(((bf16[64,32,128]{2,1,0:T(8,128)(2,1)}), bf16[64,32,128]{2,1,0:T(8,128)(2,1)S(1)}, u32[]{:S(2)}, u32[]{:S(2)}) %all-to-all-start.2) | async-done | bytes 524320 | tf_op jit(solution)/shard_map/all_to_all | solution.py:158
  76.8 0.8 %copy.52 = f32[64,8,2,128]{3,1,2,0:T(8,128)} copy(f32[64,8,2,128]{3,2,1,0:T(2,128)S(1)} %bitcast.65) | data formatting | bytes 1048576 | tf_op jit(solution)/shard_map/mul | solution.py:174
  78.9 1.4 %multiply_reduce_fusion = f32[2,8,2,128]{3,1,2,0:T(8,128)S(1)} fusion(f32[64,8,2,128]{3,1,2,0:T(8,128)} %copy.52, f32[2,64,8,2]{2,3,1,0:T(2,128)S(1)} %copy.51), kind=kLoop, calls=%fused_computation.19 | loop fusion | flops 520192 | bytes 548864 | tf_op jit(solution)/shard_map/reduce_sum | solution.py:173
  80.5 0.6 copy.55
  (42 shorter events, 3.4 us)
Async XLA Ops:
  0.0 15.2 %copy-start = (bf16[4,2048,128]{2,1,0:T(8,128)(2,1)S(1)}, bf16[4,2048,128]{2,1,0:T(8,128)(2,1)}, u32[]{:S(2)}) copy-start(bf16[4,2048,128]{2,1,0:T(8,128)(2,1)} %param.11) | copy-start | bytes 6291460
  1.6 12.7 %all-to-all-start = ((bf16[8,2,32,256]{3,2,1,0:T(8,128)(2,1)}), bf16[8,2,32,256]{3,2,1,0:T(8,128)(2,1)S(1)}, u32[]{:S(2)}, u32[]{:S(2)}) async-start(bf16[8,2,32,256]{3,2,1,0:T(8,128)(2,1)} %broadcast_in_dim.123), calls=%async_computation | async-start | bytes 524288 | tf_op jit(solution)/shard_map/all_to_all | solution.py:105
  14.4 19.8 %copy-start.2 = (s32[192]{0:T(256)S(1)}, s32[192]{0:T(256)}, u32[]{:S(2)}) copy-start(s32[192]{0:T(256)} %param.19) | copy-start | bytes 2308
  16.7 41.4 %copy-start.3 = (f32[2048,4]{0,1:T(4,128)S(1)}, f32[2048,4]{0,1:T(4,128)}, u32[]{:S(2)}) copy-start(f32[2048,4]{0,1:T(4,128)} %param.13) | copy-start | bytes 98308
  16.8 31.3 %all-to-all-start.1 = ((bf16[64,16,128]{2,1,0:T(8,128)(2,1)}), bf16[64,16,128]{2,1,0:T(8,128)(2,1)S(1)}, u32[]{:S(2)}, u32[]{:S(2)}) async-start(bf16[64,16,128]{2,1,0:T(8,128)(2,1)} %bitcast.29), calls=%async_computation.1 | async-start | bytes 524288 | tf_op jit(solution)/shard_map/all_to_all | solution.py:151
  48.1 0.7 copy-start.1
  52.1 24.7 %all-to-all-start.2 = ((bf16[64,32,128]{2,1,0:T(8,128)(2,1)}), bf16[64,32,128]{2,1,0:T(8,128)(2,1)S(1)}, u32[]{:S(2)}, u32[]{:S(2)}) async-start(bf16[64,32,128]{2,1,0:T(8,128)(2,1)} %shard_map.100), calls=%async_computation.2 | async-start | bytes 1048576 | tf_op jit(solution)/shard_map/all_to_all | solution.py:158

commit v6 on v5

--- a/solution.py
+++ b/solution.py
@@ -110,9 +110,12 @@
         tiled=True,
     )
     hidden = hidden_parts.transpose(1, 2, 0, 3).reshape(requests, drafts, model_count * part_width)
-    acc_hidden = jnp.take_along_axis(hidden, accepted[:, :, None], axis=1)
-    acc_routes = jnp.take_along_axis(routes, accepted[:, :, None], axis=1)
-    acc_mask = jnp.take_along_axis(tree_mask, accepted[:, :, None], axis=1)
+    row_pick = accepted[:, :, None] == jnp.arange(drafts, dtype=jnp.int32)[None, None, :]
+    acc_hidden = jnp.einsum(
+        "rat,rtd->rad", row_pick.astype(hidden.dtype), hidden, preferred_element_type=jnp.float32
+    ).astype(hidden.dtype)
+    acc_routes = jnp.sum(jnp.where(row_pick[..., None], routes[:, None], 0), axis=2)
+    acc_mask = jnp.sum(jnp.where(row_pick[..., None], tree_mask[:, None], 0), axis=2)
 
     q_sum = jnp.einsum("rad,edw->raew", acc_hidden, q_weight, preferred_element_type=jnp.float32)
     kv_sum = jnp.einsum("rtd,cdw->rtcw", hidden, kv_weight, preferred_element_type=jnp.float32)
@@ -141,16 +144,14 @@
     mine = home_of == group_idx
     picked = jnp.sum(jnp.where(mine, local_of, 0), axis=1)
     any_mine = jnp.any(mine, axis=1)
-    query_rows = queries.reshape(requests, kept_rows * topk_count * head_width)
+    query_rows = queries.reshape(requests, kept_rows * topk_count, head_width)
     send_pick = (
         any_mine[:, None] & (picked[:, None] == jnp.arange(requests, dtype=jnp.int32)[None, :])
     ).astype(query_rows.dtype)
     outgoing = jnp.einsum(
-        "dr,rx->dx", send_pick, query_rows, preferred_element_type=jnp.float32
+        "dr,rxw->dxw", send_pick, query_rows, preferred_element_type=jnp.float32
     ).astype(query_rows.dtype)
-    incoming = lax.all_to_all(
-        outgoing.reshape(group_count, kept_rows * topk_count, head_width), "grp", 0, 0, tiled=True
-    )
+    incoming = lax.all_to_all(outgoing, "grp", 0, 0, tiled=True)
 
     my_slots = lax.dynamic_slice_in_dim(slot_request, group_idx * slot_count, slot_count)
     row_count = kept_rows * topk_count

time: 81.8 us -> 82 us (level)
  local copies, waits for them, and re-layouts: 10.1 us -> 6.49 us
  waiting for transfers between devices: 29.4 us -> 31.5 us
  other arithmetic: 4.78 us -> 5.75 us
    gather x5 -> x0, local copies, waits for them, and re-layouts: 2.92 us -> none  [the longest x1 1.35 us: on_device(): acc_mask = jnp.take_along_axis(tree_mask, accepted[:, :, None], axis=1)]
    unnamed x10 -> x8, local copies, waits for them, and re-layouts: 2.24 us -> 0.71 us
    all_to_all x1, waiting for transfers between devices: 0.62 us -> 2.06 us  [on_device(): lax.all_to_all(jnp.broadcast_to(draft_hidden[None], (model_count,) + draf...]
    reduce_sum x0 -> x2, other arithmetic: none -> 0.97 us  [the longest x1 0.82 us: on_device(): jnp.sum(jnp.where(row_pick[..., None], routes[:, None], 0), axis=2)]
    dot_general x1 -> x2, matrix products: 0.26 us -> 1.17 us  [the longest x1 0.89 us: on_device(): jnp.einsum('rat,rtd->rad', row_pick.astype(hidden.dtype), hidden, preferr...]
    dot_general x0 -> x1, local copies, waits for them, and re-layouts: none -> 0.87 us  [on_device(): jnp.einsum('dr,rxw->dxw', send_pick, query_rows, preferred_element_type=j...]
  transfers between devices with their start and end apart: 3 -> 3, of which waited for: 3 -> 3; matrix products, arithmetic and copies ran while one was open for 11% -> 9% of each run, Pallas kernels for 0% -> 0%
where the time goes in v6:
time: 82 us; the launch traced here: 81.4 us
  waiting for transfers between devices  31.5 us (38%)
  starting transfers between devices  30.2 us (37%)
  local copies, waits for them, and re-layouts  6.49 us (8%)
  other arithmetic  5.75 us (7%)
  matrix products  4 us (5%)
  Pallas kernels  3.3 us (4%)
    all_to_all x1, starting transfers between devices, on_device(): incoming = lax.all_to_all(outgoing, 'grp', 0, 0, tiled=True)  17.5 us
    all_to_all x1, waiting for transfers between devices, on_device(): back = lax.all_to_all(returning, 'grp', 0, 0, tiled=True)  15.8 us
    all_to_all x1, waiting for transfers between devices, on_device(): incoming = lax.all_to_all(outgoing, 'grp', 0, 0, tiled=True)  13.6 us
    all_to_all x1, starting transfers between devices, on_device(): lax.all_to_all(jnp.broadcast_to(draft_hidden[None], (model_count,) + draf...  6.66 us
    all_to_all x1, starting transfers between devices, on_device(): back = lax.all_to_all(returning, 'grp', 0, 0, tiled=True)  6.07 us
    pallas_call x1, Pallas kernels, slot_attention(): pl.pallas_call(functools.partial(slot_attention_kernel, scale=scale), out...  3.3 us
    all_to_all x1, waiting for transfers between devices, on_device(): lax.all_to_all(jnp.broadcast_to(draft_hidden[None], (model_count,) + draf...  2.06 us
  transfers between devices with their start and end apart: 3, of which 3 were waited for; matrix products, arithmetic and copies ran while one was open for 9% of the time, Pallas kernels for 0%

profile of v6, /device:TPU:1, one launch (start us, length us, event | category | flops | bytes accessed | tf_op | source)
XLA Modules:
  0.0 81.4 jit_solution(14201983087728385754)
XLA Ops:
  0.0 1.6 %broadcast_in_dim.142 = bf16[8,2,32,256]{3,2,1,0:T(8,128)(2,1)} broadcast(bf16[2,32,256]{2,1,0:T(8,128)(2,1)} %param.10), dimensions={1,2,3} | broadcast | bytes 294912 | tf_op jit(solution)/shard_map/broadcast_in_dim | solution.py:106
  1.6 6.7 %all-to-all-start = ((bf16[8,2,32,256]{3,2,1,0:T(8,128)(2,1)}), bf16[8,2,32,256]{3,2,1,0:T(8,128)(2,1)S(1)}, u32[]{:S(2)}, u32[]{:S(2)}) async-start(bf16[8,2,32,256]{3,2,1,0:T(8,128)(2,1)} %broadcast_in_dim.142), calls=%async_computation | async-start | bytes 524288 | tf_op jit(solution)/shard_map/all_to_all | solution.py:105
  8.3 0.8 eq.76
  9.2 0.8 iota_compare_fusion.1
  10.2 1.3 %and_select_fusion.home_ref = s32[3]{0:T(128)} fusion(s32[192]{0:T(256)} %param.19, s32[]{:T(128)S(6)} %select_n.57), kind=kLoop, calls=%fused_computation.58 | loop fusion | flops 45 | bytes 28 | tf_op jit(solution)/shard_map/jit(floor_divide)/jit(_where)/select_n | solution.py:158
  11.5 0.8 %select_reduce_fusion.3 = s32[2,8,2]{1,2,0:T(2,128)S(1)} fusion(s32[2,32,2]{1,2,0:T(2,128)} %param.14, pred[2,8,32]{2,1,0:T(8,128)(4,1)S(1)} %iota_compare_fusion.1), kind=kLoop, calls=%fused_computation.45 | loop fusion | flops 2016 | bytes 1152 | tf_op jit(solution)/shard_map/reduce_sum | solution.py:117
  12.3 2.1 %all-to-all-done = bf16[8,2,32,256]{3,2,1,0:T(8,128)(2,1)S(1)} async-done(((bf16[8,2,32,256]{3,2,1,0:T(8,128)(2,1)}), bf16[8,2,32,256]{3,2,1,0:T(8,128)(2,1)S(1)}, u32[]{:S(2)}, u32[]{:S(2)}) %all-to-all-start) | async-done | bytes 262176 | tf_op jit(solution)/shard_map/all_to_all | solution.py:105
  14.4 0.9 %convolution_convert_fusion = bf16[2,8,2048]{2,1,0:T(8,128)(2,1)S(1)} fusion(bf16[2,32,2048]{2,1,0:T(8,128)(2,1)S(1)} %bitcast.52, s32[2,8]{1,0:T(2,128)} %param.16), kind=kOutput, calls=%fused_computation.1 | convolution fusion | flops 2130432 | bytes 327744 | tf_op jit(solution)/shard_map/rat,rtd->rad/dot_general | solution.py:114
  15.3 0.4 fusion.1
  15.8 0.3 fusion.21
  16.1 0.9 %copy.71 = bf16[64,16,128]{2,1,0:T(8,128)(2,1)} copy(bf16[64,16,128]{2,0,1:T(8,128)(2,1)S(1)} %fusion.21) | data formatting | bytes 524288 | tf_op jit(solution)/shard_map/dr,rxw->dxw/dot_general | solution.py:151
  16.9 17.5 %all-to-all-start.1 = ((bf16[64,16,128]{2,1,0:T(8,128)(2,1)}), bf16[64,16,128]{2,1,0:T(8,128)(2,1)S(1)}, u32[]{:S(2)}, u32[]{:S(2)}) async-start(bf16[64,16,128]{2,1,0:T(8,128)(2,1)} %copy.71), calls=%async_computation.1 | async-start | bytes 524288 | tf_op jit(solution)/shard_map/all_to_all | solution.py:154
  34.7 13.6 %all-to-all-done.1.incoming_ref = bf16[64,16,128]{2,1,0:T(8,128)(2,1)S(1)} async-done(((bf16[64,16,128]{2,1,0:T(8,128)(2,1)}), bf16[64,16,128]{2,1,0:T(8,128)(2,1)S(1)}, u32[]{:S(2)}, u32[]{:S(2)}) %all-to-all-start.1) | async-done | bytes 262176 | tf_op jit(solution)/shard_map/all_to_all | solution.py:154
  48.3 0.7 copy-done.1
  49.0 3.3 %shard_map.100 = bf16[64,32,128]{2,1,0:T(8,128)(2,1)} custom-call(s32[3]{0:T(128)} %and_select_fusion.home_ref, s32[3]{0:T(128)} %len_ref.1, bf16[64,16,128]{2,1,0:T(8,128)(2,1)} %copy-done.1, bf16[3,2,1024,128]{3,2,1,0:T(8,128)(2,1)} %cache_ref.1), custom_call_target="tpu_custom_call" | custom-call | flops 25165824 | bytes 2359296 | tf_op jit(solution)/shard_map/pallas_call | solution.py:63
  52.3 6.1 %all-to-all-start.2 = ((bf16[64,32,128]{2,1,0:T(8,128)(2,1)}), bf16[64,32,128]{2,1,0:T(8,128)(2,1)S(1)}, u32[]{:S(2)}, u32[]{:S(2)}) async-start(bf16[64,32,128]{2,1,0:T(8,128)(2,1)} %shard_map.100), calls=%async_computation.2 | async-start | bytes 1048576 | tf_op jit(solution)/shard_map/all_to_all | solution.py:159
  58.4 0.5 fusion.16
  59.2 1.5 %convolution_convert_fusion.1 = bf16[2,32,2,128]{3,1,2,0:T(8,128)(2,1)S(1)} fusion(bf16[2,2048,128]{2,1,0:T(8,128)(2,1)} %param.12, bf16[2,32,2048,1]{2,1,0,3:T(8,128)(2,1)S(1)} %reshape.83), kind=kOutput, calls=%fused_computation.4 | convolution fusion | flops 67125248 | bytes 1343488 | tf_op jit(solution)/shard_map/rtd,cdw->rtcw/dot_general | solution.py:121
  61.2 15.8 %all-to-all-done.2 = bf16[64,32,128]{2,1,0:T(8,128)(2,1)S(1)} async-done(((bf16[64,32,128]{2,1,0:T(8,128)(2,1)}), bf16[64,32,128]{2,1,0:T(8,128)(2,1)S(1)}, u32[]{:S(2)}, u32[]{:S(2)}) %all-to-all-start.2) | async-done | bytes 524320 | tf_op jit(solution)/shard_map/all_to_all | solution.py:159
  77.0 0.8 %copy.59 = f32[64,8,2,128]{3,1,2,0:T(8,128)} copy(f32[64,8,2,128]{3,2,1,0:T(2,128)S(1)} %bitcast.51) | data formatting | bytes 1048576 | tf_op jit(solution)/shard_map/mul | solution.py:175
  77.9 0.3 slice_add_fusion
  78.2 0.3 copy.60
  79.1 1.4 %multiply_reduce_fusion = f32[2,8,2,128]{3,1,2,0:T(8,128)S(1)} fusion(f32[64,8,2,128]{3,1,2,0:T(8,128)} %copy.59, f32[2,64,8,2]{2,3,1,0:T(2,128)S(1)} %copy.58), kind=kLoop, calls=%fused_computation.15 | loop fusion | flops 520192 | bytes 548864 | tf_op jit(solution)/shard_map/reduce_sum | solution.py:174
  80.7 0.6 copy.62
  (35 shorter events, 2.4 us)
Async XLA Ops:
  0.0 15.3 %copy-start = (bf16[4,2048,128]{2,1,0:T(8,128)(2,1)S(1)}, bf16[4,2048,128]{2,1,0:T(8,128)(2,1)}, u32[]{:S(2)}) copy-start(bf16[4,2048,128]{2,1,0:T(8,128)(2,1)} %param.11) | copy-start | bytes 6291460
  1.6 12.7 %all-to-all-start = ((bf16[8,2,32,256]{3,2,1,0:T(8,128)(2,1)}), bf16[8,2,32,256]{3,2,1,0:T(8,128)(2,1)S(1)}, u32[]{:S(2)}, u32[]{:S(2)}) async-start(bf16[8,2,32,256]{3,2,1,0:T(8,128)(2,1)} %broadcast_in_dim.142), calls=%async_computation | async-start | bytes 524288 | tf_op jit(solution)/shard_map/all_to_all | solution.py:105
  14.4 20.2 %copy-start.3 = (s32[2,32,32]{2,1,0:T(8,128)S(1)}, s32[2,32,32]{2,1,0:T(8,128)}, u32[]{:S(2)}) copy-start(s32[2,32,32]{2,1,0:T(8,128)} %param.15) | copy-start | bytes 24580
  16.9 41.4 %copy-start.2 = (f32[2048,4]{0,1:T(4,128)S(1)}, f32[2048,4]{0,1:T(4,128)}, u32[]{:S(2)}) copy-start(f32[2048,4]{0,1:T(4,128)} %param.13) | copy-start | bytes 98308
  16.9 31.3 %all-to-all-start.1 = ((bf16[64,16,128]{2,1,0:T(8,128)(2,1)}), bf16[64,16,128]{2,1,0:T(8,128)(2,1)S(1)}, u32[]{:S(2)}, u32[]{:S(2)}) async-start(bf16[64,16,128]{2,1,0:T(8,128)(2,1)} %copy.71), calls=%async_computation.1 | async-start | bytes 524288 | tf_op jit(solution)/shard_map/all_to_all | solution.py:154
  48.3 0.7 copy-start.1
  52.3 24.7 %all-to-all-start.2 = ((bf16[64,32,128]{2,1,0:T(8,128)(2,1)}), bf16[64,32,128]{2,1,0:T(8,128)(2,1)S(1)}, u32[]{:S(2)}, u32[]{:S(2)}) async-start(bf16[64,32,128]{2,1,0:T(8,128)(2,1)} %shard_map.100), calls=%async_computation.2 | async-start | bytes 1048576 | tf_op jit(solution)/shard_map/all_to_all | solution.py:159

commit v7 on v6

--- a/solution.py
+++ b/solution.py
@@ -101,24 +101,37 @@
     slot_count = cache_kv.shape[0]
     cache_size = cache_kv.shape[2]
 
+    row_pick = accepted[:, :, None] == jnp.arange(drafts, dtype=jnp.int32)[None, None, :]
+    acc_part = jnp.einsum(
+        "rat,rtd->rad",
+        row_pick.astype(draft_hidden.dtype),
+        draft_hidden,
+        preferred_element_type=jnp.float32,
+    ).astype(draft_hidden.dtype)
+    acc_routes = jnp.sum(jnp.where(row_pick[..., None], routes[:, None], 0), axis=2)
+    mask_rows = jnp.sum(jnp.where(row_pick[..., None], tree_mask[:, None], 0), axis=2)
+    acc_mask = jnp.sum(jnp.where(row_pick[:, None, :, :], mask_rows[:, :, None, :], 0), axis=3)
+    order = jnp.arange(kept_rows, dtype=jnp.int32)
+    repeated = jnp.any(
+        (accepted[:, :, None] == accepted[:, None, :]) & (order[None, None, :] < order[None, :, None]),
+        axis=2,
+    )
+    usable_keys = (acc_mask > 0) & ~repeated[:, None, :]
+
     model_count = lax.axis_size("mdl")
     hidden_parts = lax.all_to_all(
-        jnp.broadcast_to(draft_hidden[None], (model_count,) + draft_hidden.shape),
+        jnp.broadcast_to(acc_part[None], (model_count,) + acc_part.shape),
         "mdl",
         0,
         0,
         tiled=True,
     )
-    hidden = hidden_parts.transpose(1, 2, 0, 3).reshape(requests, drafts, model_count * part_width)
-    row_pick = accepted[:, :, None] == jnp.arange(drafts, dtype=jnp.int32)[None, None, :]
-    acc_hidden = jnp.einsum(
-        "rat,rtd->rad", row_pick.astype(hidden.dtype), hidden, preferred_element_type=jnp.float32
-    ).astype(hidden.dtype)
-    acc_routes = jnp.sum(jnp.where(row_pick[..., None], routes[:, None], 0), axis=2)
-    acc_mask = jnp.sum(jnp.where(row_pick[..., None], tree_mask[:, None], 0), axis=2)
+    acc_hidden = hidden_parts.transpose(1, 2, 0, 3).reshape(
+        requests, kept_rows, model_count * part_width
+    )
 
     q_sum = jnp.einsum("rad,edw->raew", acc_hidden, q_weight, preferred_element_type=jnp.float32)
-    kv_sum = jnp.einsum("rtd,cdw->rtcw", hidden, kv_weight, preferred_element_type=jnp.float32)
+    kv_sum = jnp.einsum("rtd,cdw->rtcw", acc_hidden, kv_weight, preferred_element_type=jnp.float32)
     logit_sum = jnp.einsum(
         "rad,de->rae", acc_hidden.astype(jnp.float32), router_weight, precision=highest
     )
@@ -135,7 +148,7 @@
         * score_scale
     )
     tree_peak, tree_den, tree_num = softmax_piece(
-        tree_scores, (acc_mask > 0)[:, :, None, :], draft_values, "rakj,rjw->rakw"
+        tree_scores, usable_keys[:, :, None, :], draft_values, "rakj,rjw->rakw"
     )
 
     slot_table = slot_request.reshape(group_count, slot_count)

time: 82 us -> 80.3 us (0.979)
  waiting for transfers between devices: 31.5 us -> 29.6 us
  other arithmetic: 5.75 us -> 7.04 us
  local copies, waits for them, and re-layouts: 6.49 us -> 5.3 us
    all_to_all x1, waiting for transfers between devices: 2.06 us -> 0.2 us  [on_device(): lax.all_to_all(jnp.broadcast_to(acc_part[None], (model_count,) + acc_part...]
    broadcast_in_dim x1, local copies, waits for them, and re-layouts: 1.62 us -> 0.63 us  [on_device(): jnp.broadcast_to(acc_part[None], (model_count,) + acc_part.shape)]
    reduce_or x0 -> x1, other arithmetic: none -> 0.97 us  [on_device(): jnp.any((accepted[:, :, None] == accepted[:, None, :]) & (order[None, Non...]
  transfers between devices with their start and end apart: 3 -> 3, of which waited for: 3 -> 3; matrix products, arithmetic and copies ran while one was open for 9% -> 10% of each run, Pallas kernels for 0% -> 0%
where the time goes in v7:
time: 80.3 us; the launch traced here: 79.7 us
  starting transfers between devices  30.2 us (38%)
  waiting for transfers between devices  29.6 us (37%)
  other arithmetic  7.04 us (9%)
  local copies, waits for them, and re-layouts  5.3 us (7%)
  matrix products  4.13 us (5%)
  Pallas kernels  3.3 us (4%)
    all_to_all x1, starting transfers between devices, on_device(): incoming = lax.all_to_all(outgoing, 'grp', 0, 0, tiled=True)  17.5 us
    all_to_all x1, waiting for transfers between devices, on_device(): back = lax.all_to_all(returning, 'grp', 0, 0, tiled=True)  16.3 us
    all_to_all x1, waiting for transfers between devices, on_device(): incoming = lax.all_to_all(outgoing, 'grp', 0, 0, tiled=True)  13.1 us
    all_to_all x1, starting transfers between devices, on_device(): lax.all_to_all(jnp.broadcast_to(acc_part[None], (model_count,) + acc_part...  6.66 us
    all_to_all x1, starting transfers between devices, on_device(): back = lax.all_to_all(returning, 'grp', 0, 0, tiled=True)  6.06 us
    pallas_call x1, Pallas kernels, slot_attention(): pl.pallas_call(functools.partial(slot_attention_kernel, scale=scale), out...  3.3 us
  transfers between devices with their start and end apart: 3, of which 3 were waited for; matrix products, arithmetic and copies ran while one was open for 10% of the time, Pallas kernels for 0%

profile of v7, /device:TPU:1, one launch (start us, length us, event | category | flops | bytes accessed | tf_op | source)
XLA Modules:
  0.0 79.7 jit_solution(11716907232712778946)
XLA Ops:
  0.0 1.1 %convolution_convert_fusion.1 = bf16[2,8,256]{2,1,0:T(8,128)(2,1)S(1)} fusion(bf16[2,32,256]{2,1,0:T(8,128)(2,1)} %param.10, s32[2,8]{1,0:T(2,128)} %param.16), kind=kOutput, calls=%fused_computation.11 | convolution fusion | flops 266752 | bytes 41024 | tf_op jit(solution)/shard_map/rat,rtd->rad/dot_general | solution.py:105
  1.1 0.6 broadcast_in_dim.169
  1.7 6.7 %all-to-all-start = ((bf16[8,2,8,256]{3,2,1,0:T(8,128)(2,1)}), bf16[8,2,8,256]{3,2,1,0:T(8,128)(2,1)S(1)}, u32[]{:S(2)}, u32[]{:S(2)}) async-start(bf16[8,2,8,256]{3,2,1,0:T(8,128)(2,1)} %broadcast_in_dim.169), calls=%async_computation | async-start | bytes 131072 | tf_op jit(solution)/shard_map/all_to_all | solution.py:122
  8.4 0.8 iota_compare_fusion.1
  9.2 0.8 %select_reduce_fusion.4 = s32[2,8,2]{1,2,0:T(2,128)S(1)} fusion(s32[2,32,2]{1,2,0:T(2,128)} %param.14, pred[2,8,32]{2,1,0:T(8,128)(4,1)S(1)} %iota_compare_fusion.1), kind=kLoop, calls=%fused_computation.42 | loop fusion | flops 2016 | bytes 1152 | tf_op jit(solution)/shard_map/reduce_sum | solution.py:111
  10.0 0.9 %select_reduce_fusion = s32[2,8,32]{2,1,0:T(8,128)S(1)} fusion(s32[2,32,32]{2,1,0:T(8,128)} %param.15, pred[2,8,32]{2,1,0:T(8,128)(4,1)S(1)} %iota_compare_fusion.1), kind=kLoop, calls=%fused_computation.20 | loop fusion | flops 32256 | bytes 10752 | tf_op jit(solution)/shard_map/reduce_sum | solution.py:112
  10.9 0.8 %eq.96 = s32[64,3]{1,0:T(8,128)S(1)} reshape(s32[192]{0:T(256)} %param.19) | data formatting | bytes 1536 | tf_op jit(solution)/shard_map/eq | solution.py:181
  11.9 1.0 %and_reduce_fusion = pred[2,8]{1,0:T(4,128)(4,1)S(1)} fusion(s32[2,8]{1,0:T(2,128)} %param.16, pred[8,8]{1,0:T(8,128)(4,1)S(1)} %iota_compare_fusion.2), kind=kLoop, calls=%fused_computation.48 | loop fusion | flops 368 | bytes 144 | tf_op jit(solution)/shard_map/reduce_or | solution.py:115
  13.0 0.4 select_reduce_fusion.2
  13.6 0.4 fusion.1
  14.4 0.9 %copy.77 = bf16[64,16,128]{2,1,0:T(8,128)(2,1)} copy(bf16[64,16,128]{2,0,1:T(8,128)(2,1)S(1)} %fusion.19) | data formatting | bytes 524288 | tf_op jit(solution)/shard_map/dr,rxw->dxw/dot_general | solution.py:164
  15.3 17.5 %all-to-all-start.1 = ((bf16[64,16,128]{2,1,0:T(8,128)(2,1)}), bf16[64,16,128]{2,1,0:T(8,128)(2,1)S(1)}, u32[]{:S(2)}, u32[]{:S(2)}) async-start(bf16[64,16,128]{2,1,0:T(8,128)(2,1)} %copy.77), calls=%async_computation.1 | async-start | bytes 524288 | tf_op jit(solution)/shard_map/all_to_all | solution.py:167
  32.8 0.6 and_select_fusion.home_ref
  33.5 13.1 %all-to-all-done.1.incoming_ref = bf16[64,16,128]{2,1,0:T(8,128)(2,1)S(1)} async-done(((bf16[64,16,128]{2,1,0:T(8,128)(2,1)}), bf16[64,16,128]{2,1,0:T(8,128)(2,1)S(1)}, u32[]{:S(2)}, u32[]{:S(2)}) %all-to-all-start.1) | async-done | bytes 262176 | tf_op jit(solution)/shard_map/all_to_all | solution.py:167
  46.6 0.7 copy-done.1
  47.3 3.3 %shard_map.100 = bf16[64,32,128]{2,1,0:T(8,128)(2,1)} custom-call(s32[3]{0:T(128)} %and_select_fusion.home_ref, s32[3]{0:T(128)} %len_ref.1, bf16[64,16,128]{2,1,0:T(8,128)(2,1)} %copy-done.1, bf16[3,2,1024,128]{3,2,1,0:T(8,128)(2,1)} %cache_ref.1), custom_call_target="tpu_custom_call" | custom-call | flops 25165824 | bytes 2359296 | tf_op jit(solution)/shard_map/pallas_call | solution.py:63
  50.6 6.1 %all-to-all-start.2 = ((bf16[64,32,128]{2,1,0:T(8,128)(2,1)}), bf16[64,32,128]{2,1,0:T(8,128)(2,1)S(1)}, u32[]{:S(2)}, u32[]{:S(2)}) async-start(bf16[64,32,128]{2,1,0:T(8,128)(2,1)} %shard_map.100), calls=%async_computation.2 | async-start | bytes 1048576 | tf_op jit(solution)/shard_map/all_to_all | solution.py:172
  56.7 0.5 fusion.14
  57.2 1.5 %convolution_convert_fusion = bf16[2,8,2,128]{3,1,2,0:T(8,128)(2,1)S(1)} fusion(bf16[2,8,2048,1]{2,1,3,0:T(8,128)(2,1)S(1)} %bitcast.47, bf16[2,2048,128]{2,1,0:T(8,128)(2,1)} %param.12), kind=kOutput, calls=%fused_computation.10 | convolution fusion | flops 16781312 | bytes 1122304 | tf_op jit(solution)/shard_map/rtd,cdw->rtcw/dot_general | solution.py:134
  59.0 16.3 %all-to-all-done.2 = bf16[64,32,128]{2,1,0:T(8,128)(2,1)S(1)} async-done(((bf16[64,32,128]{2,1,0:T(8,128)(2,1)}), bf16[64,32,128]{2,1,0:T(8,128)(2,1)S(1)}, u32[]{:S(2)}, u32[]{:S(2)}) %all-to-all-start.2) | async-done | bytes 524320 | tf_op jit(solution)/shard_map/all_to_all | solution.py:172
  75.3 0.8 %copy.66 = f32[64,8,2,128]{3,1,2,0:T(8,128)} copy(f32[64,8,2,128]{3,2,1,0:T(2,128)S(1)} %bitcast.44) | data formatting | bytes 1048576 | tf_op jit(solution)/shard_map/mul | solution.py:188
  76.2 0.3 slice_add_fusion
  77.5 1.4 %multiply_reduce_fusion = f32[2,8,2,128]{3,1,2,0:T(8,128)S(1)} fusion(f32[64,8,2,128]{3,1,2,0:T(8,128)} %copy.66, f32[2,64,8,2]{2,3,1,0:T(2,128)S(1)} %copy.65), kind=kLoop, calls=%fused_computation.15 | loop fusion | flops 520192 | bytes 548864 | tf_op jit(solution)/shard_map/reduce_sum | solution.py:187
  79.1 0.6 copy.69
  (38 shorter events, 2.6 us)
Async XLA Ops:
  0.0 13.6 %copy-start = (bf16[4,2048,128]{2,1,0:T(8,128)(2,1)S(1)}, bf16[4,2048,128]{2,1,0:T(8,128)(2,1)}, u32[]{:S(2)}) copy-start(bf16[4,2048,128]{2,1,0:T(8,128)(2,1)} %param.11) | copy-start | bytes 6291460
  0.0 32.8 %copy-start.3 = (s32[192]{0:T(256)S(1)}, s32[192]{0:T(256)}, u32[]{:S(2)}) copy-start(s32[192]{0:T(256)} %param.19) | copy-start | bytes 2308
  1.7 11.9 %all-to-all-start = ((bf16[8,2,8,256]{3,2,1,0:T(8,128)(2,1)}), bf16[8,2,8,256]{3,2,1,0:T(8,128)(2,1)S(1)}, u32[]{:S(2)}, u32[]{:S(2)}) async-start(bf16[8,2,8,256]{3,2,1,0:T(8,128)(2,1)} %broadcast_in_dim.169), calls=%async_computation | async-start | bytes 131072 | tf_op jit(solution)/shard_map/all_to_all | solution.py:122
  15.3 41.4 %copy-start.2 = (f32[2048,4]{0,1:T(4,128)S(1)}, f32[2048,4]{0,1:T(4,128)}, u32[]{:S(2)}) copy-start(f32[2048,4]{0,1:T(4,128)} %param.13) | copy-start | bytes 98308
  15.3 31.3 %all-to-all-start.1 = ((bf16[64,16,128]{2,1,0:T(8,128)(2,1)}), bf16[64,16,128]{2,1,0:T(8,128)(2,1)S(1)}, u32[]{:S(2)}, u32[]{:S(2)}) async-start(bf16[64,16,128]{2,1,0:T(8,128)(2,1)} %copy.77), calls=%async_computation.1 | async-start | bytes 524288 | tf_op jit(solution)/shard_map/all_to_all | solution.py:167
  46.6 0.7 copy-start.1
  50.6 24.7 %all-to-all-start.2 = ((bf16[64,32,128]{2,1,0:T(8,128)(2,1)}), bf16[64,32,128]{2,1,0:T(8,128)(2,1)S(1)}, u32[]{:S(2)}, u32[]{:S(2)}) async-start(bf16[64,32,128]{2,1,0:T(8,128)(2,1)} %shard_map.100), calls=%async_computation.2 | async-start | bytes 1048576 | tf_op jit(solution)/shard_map/all_to_all | solution.py:172

commit v8 on v7

--- a/solution.py
+++ b/solution.py
@@ -19,16 +19,25 @@
     return (peak_score, denominator, numerator)
 
 
-def slot_attention_kernel(home_ref, len_ref, incoming_ref, cache_ref, out_ref, *, scale):
-    slot_count = cache_ref.shape[0]
+def slot_attention_kernel(
+    home_ref, len_ref, incoming_ref, cache_hbm, out_ref, cache_buf, sems, *, scale
+):
+    slot_count = cache_buf.shape[0]
     rows = incoming_ref.shape[1]
+    copies = [
+        pltpu.make_async_copy(cache_hbm.at[i], cache_buf.at[i], sems.at[i])
+        for i in range(slot_count)
+    ]
+    for copy in copies:
+        copy.start()
     out_ref[...] = jnp.zeros(out_ref.shape, out_ref.dtype)
     for i in range(slot_count):
         home = home_ref[i]
+        copies[i].wait()
         scores = (
             lax.dot_general(
                 incoming_ref[home],
-                cache_ref[i, 0],
+                cache_buf[i, 0],
                 (((1,), (1,)), ((), ())),
                 preferred_element_type=jnp.float32,
             )
@@ -39,7 +48,7 @@
         peak = jnp.max(masked, axis=1, keepdims=True)
         weights = jnp.exp(masked - peak).astype(jnp.bfloat16)
         den = jnp.sum(weights.astype(jnp.float32), axis=1, keepdims=True)
-        num = jnp.dot(weights, cache_ref[i, 1], preferred_element_type=jnp.float32)
+        num = jnp.dot(weights, cache_buf[i, 1], preferred_element_type=jnp.float32)
         peak_low = peak.astype(jnp.bfloat16).astype(jnp.float32)
         shift = jnp.exp(peak - peak_low)
         shifted_den = den * shift
@@ -67,9 +76,14 @@
             pl.BlockSpec(memory_space=pltpu.SMEM),
             pl.BlockSpec(memory_space=pltpu.SMEM),
             pl.BlockSpec(memory_space=pltpu.VMEM),
-            pl.BlockSpec(memory_space=pltpu.VMEM),
+            pl.BlockSpec(memory_space=pl.ANY),
         ],
         out_specs=pl.BlockSpec(memory_space=pltpu.VMEM),
+        scratch_shapes=[
+            pltpu.VMEM(cache_kv.shape, cache_kv.dtype),
+            pltpu.SemaphoreType.DMA((slot_count,)),
+        ],
+        compiler_params=pltpu.CompilerParams(vmem_limit_bytes=16 * 1024 * 1024),
         cost_estimate=pl.CostEstimate(
             flops=flops, transcendentals=slot_count * rows * cache_size, bytes_accessed=moved
         ),

time: 80.3 us -> 80.6 us (level)
  transfers between devices with their start and end apart: 3 -> 3, of which waited for: 3 -> 3; matrix products, arithmetic and copies ran while one was open for 10% -> 9% of each run, Pallas kernels for 0% -> 0%
where the time goes in v8:
time: 80.6 us; the launch traced here: 79.9 us
  starting transfers between devices  30.2 us (37%)
  waiting for transfers between devices  30.1 us (37%)
  other arithmetic  6.53 us (8%)
  local copies, waits for them, and re-layouts  6.01 us (7%)
  matrix products  4.13 us (5%)
  Pallas kernels  2.77 us (3%)
    all_to_all x1, starting transfers between devices, on_device(): incoming = lax.all_to_all(outgoing, 'grp', 0, 0, tiled=True)  17.5 us
    all_to_all x1, waiting for transfers between devices, on_device(): back = lax.all_to_all(returning, 'grp', 0, 0, tiled=True)  16.3 us
    all_to_all x1, waiting for transfers between devices, on_device(): incoming = lax.all_to_all(outgoing, 'grp', 0, 0, tiled=True)  13.6 us
    all_to_all x1, starting transfers between devices, on_device(): lax.all_to_all(jnp.broadcast_to(acc_part[None], (model_count,) + acc_part...  6.66 us
    all_to_all x1, starting transfers between devices, on_device(): back = lax.all_to_all(returning, 'grp', 0, 0, tiled=True)  6.08 us
    pallas_call x1, Pallas kernels, slot_attention(): pl.pallas_call(functools.partial(slot_attention_kernel, scale=scale), out...  2.77 us
  transfers between devices with their start and end apart: 3, of which 3 were waited for; matrix products, arithmetic and copies ran while one was open for 9% of the time, Pallas kernels for 0%

profile of v8, /device:TPU:1, one launch (start us, length us, event | category | flops | bytes accessed | tf_op | source)
XLA Modules:
  0.0 79.9 jit_solution(2884342851136793369)
XLA Ops:
  0.0 1.1 %convolution_convert_fusion.1 = bf16[2,8,256]{2,1,0:T(8,128)(2,1)S(1)} fusion(bf16[2,32,256]{2,1,0:T(8,128)(2,1)} %param.10, s32[2,8]{1,0:T(2,128)} %param.16), kind=kOutput, calls=%fused_computation.11 | convolution fusion | flops 266752 | bytes 41024 | tf_op jit(solution)/shard_map/rat,rtd->rad/dot_general | solution.py:119
  1.1 0.6 broadcast_in_dim.169
  1.7 6.7 %all-to-all-start = ((bf16[8,2,8,256]{3,2,1,0:T(8,128)(2,1)}), bf16[8,2,8,256]{3,2,1,0:T(8,128)(2,1)S(1)}, u32[]{:S(2)}, u32[]{:S(2)}) async-start(bf16[8,2,8,256]{3,2,1,0:T(8,128)(2,1)} %broadcast_in_dim.169), calls=%async_computation | async-start | bytes 131072 | tf_op jit(solution)/shard_map/all_to_all | solution.py:136
  8.4 0.8 iota_compare_fusion.1
  9.2 0.8 %select_reduce_fusion.4 = s32[2,8,2]{1,2,0:T(2,128)S(1)} fusion(s32[2,32,2]{1,2,0:T(2,128)} %param.14, pred[2,8,32]{2,1,0:T(8,128)(4,1)S(1)} %iota_compare_fusion.1), kind=kLoop, calls=%fused_computation.42 | loop fusion | flops 2016 | bytes 1152 | tf_op jit(solution)/shard_map/reduce_sum | solution.py:125
  10.0 0.9 %select_reduce_fusion = s32[2,8,32]{2,1,0:T(8,128)S(1)} fusion(s32[2,32,32]{2,1,0:T(8,128)} %param.15, pred[2,8,32]{2,1,0:T(8,128)(4,1)S(1)} %iota_compare_fusion.1), kind=kLoop, calls=%fused_computation.20 | loop fusion | flops 32256 | bytes 10752 | tf_op jit(solution)/shard_map/reduce_sum | solution.py:126
  10.9 0.8 %eq.96 = s32[64,3]{1,0:T(8,128)S(1)} reshape(s32[192]{0:T(256)} %param.19) | data formatting | bytes 1536 | tf_op jit(solution)/shard_map/eq | solution.py:195
  11.9 1.0 %and_reduce_fusion = pred[2,8]{1,0:T(4,128)(4,1)S(1)} fusion(s32[2,8]{1,0:T(2,128)} %param.16, pred[8,8]{1,0:T(8,128)(4,1)S(1)} %iota_compare_fusion.2), kind=kLoop, calls=%fused_computation.48 | loop fusion | flops 368 | bytes 144 | tf_op jit(solution)/shard_map/reduce_or | solution.py:129
  13.0 0.4 select_reduce_fusion.2
  13.6 0.4 fusion.1
  14.1 0.3 fusion.19
  14.4 0.9 %copy.77 = bf16[64,16,128]{2,1,0:T(8,128)(2,1)} copy(bf16[64,16,128]{2,0,1:T(8,128)(2,1)S(1)} %fusion.19) | data formatting | bytes 524288 | tf_op jit(solution)/shard_map/dr,rxw->dxw/dot_general | solution.py:178
  15.3 17.5 %all-to-all-start.1 = ((bf16[64,16,128]{2,1,0:T(8,128)(2,1)}), bf16[64,16,128]{2,1,0:T(8,128)(2,1)S(1)}, u32[]{:S(2)}, u32[]{:S(2)}) async-start(bf16[64,16,128]{2,1,0:T(8,128)(2,1)} %copy.77), calls=%async_computation.1 | async-start | bytes 524288 | tf_op jit(solution)/shard_map/all_to_all | solution.py:181
  33.0 13.6 %all-to-all-done.1.incoming_ref = bf16[64,16,128]{2,1,0:T(8,128)(2,1)S(1)} async-done(((bf16[64,16,128]{2,1,0:T(8,128)(2,1)}), bf16[64,16,128]{2,1,0:T(8,128)(2,1)S(1)}, u32[]{:S(2)}, u32[]{:S(2)}) %all-to-all-start.1) | async-done | bytes 262176 | tf_op jit(solution)/shard_map/all_to_all | solution.py:181
  46.6 1.4 %copy-done.1 = bf16[3,2,1024,128]{3,2,1,0:T(8,128)(2,1)S(1)} copy-done((bf16[3,2,1024,128]{3,2,1,0:T(8,128)(2,1)S(1)}, bf16[3,2,1024,128]{3,2,1,0:T(8,128)(2,1)}, u32[]{:S(2)}) %copy-start.1) | copy-done | bytes 1572888
  48.0 2.8 %shard_map.100 = bf16[64,32,128]{2,1,0:T(8,128)(2,1)} custom-call(s32[3]{0:T(128)S(1)} %and_select_fusion.home_ref, s32[3]{0:T(128)S(1)} %copy-done.2, bf16[64,16,128]{2,1,0:T(8,128)(2,1)S(1)} %all-to-all-done.1.incoming_ref, bf16[3,2,1024,128]{3,2,1,0:T(8,128)(2,1)S(1)} %copy-done.1), custom_call_target="tpu_custom_call" | custom-call | flops 25165824 | bytes 2359296 | tf_op jit(solution)/shard_map/pallas_call | solution.py:72
  50.8 6.1 %all-to-all-start.2 = ((bf16[64,32,128]{2,1,0:T(8,128)(2,1)}), bf16[64,32,128]{2,1,0:T(8,128)(2,1)S(1)}, u32[]{:S(2)}, u32[]{:S(2)}) async-start(bf16[64,32,128]{2,1,0:T(8,128)(2,1)} %shard_map.100), calls=%async_computation.2 | async-start | bytes 1048576 | tf_op jit(solution)/shard_map/all_to_all | solution.py:186
  56.9 0.5 fusion.14
  57.5 1.5 %convolution_convert_fusion = bf16[2,8,2,128]{3,1,2,0:T(8,128)(2,1)S(1)} fusion(bf16[2,8,2048,1]{2,1,3,0:T(8,128)(2,1)S(1)} %bitcast.47, bf16[2,2048,128]{2,1,0:T(8,128)(2,1)} %param.12), kind=kOutput, calls=%fused_computation.10 | convolution fusion | flops 16781312 | bytes 1122304 | tf_op jit(solution)/shard_map/rtd,cdw->rtcw/dot_general | solution.py:148
  59.2 16.3 %all-to-all-done.2 = bf16[64,32,128]{2,1,0:T(8,128)(2,1)S(1)} async-done(((bf16[64,32,128]{2,1,0:T(8,128)(2,1)}), bf16[64,32,128]{2,1,0:T(8,128)(2,1)S(1)}, u32[]{:S(2)}, u32[]{:S(2)}) %all-to-all-start.2) | async-done | bytes 524320 | tf_op jit(solution)/shard_map/all_to_all | solution.py:186
  75.6 0.8 %copy.66 = f32[64,8,2,128]{3,1,2,0:T(8,128)} copy(f32[64,8,2,128]{3,2,1,0:T(2,128)S(1)} %bitcast.44) | data formatting | bytes 1048576 | tf_op jit(solution)/shard_map/mul | solution.py:202
  76.4 0.3 slice_add_fusion
  77.7 1.4 %multiply_reduce_fusion = f32[2,8,2,128]{3,1,2,0:T(8,128)S(1)} fusion(f32[64,8,2,128]{3,1,2,0:T(8,128)} %copy.66, f32[2,64,8,2]{2,3,1,0:T(2,128)S(1)} %copy.65), kind=kLoop, calls=%fused_computation.15 | loop fusion | flops 520192 | bytes 548864 | tf_op jit(solution)/shard_map/reduce_sum | solution.py:201
  79.3 0.6 copy.69
  (40 shorter events, 2.4 us)
Async XLA Ops:
  0.0 13.6 %copy-start = (bf16[4,2048,128]{2,1,0:T(8,128)(2,1)S(1)}, bf16[4,2048,128]{2,1,0:T(8,128)(2,1)}, u32[]{:S(2)}) copy-start(bf16[4,2048,128]{2,1,0:T(8,128)(2,1)} %param.11) | copy-start | bytes 6291460
  0.0 32.8 %copy-start.4 = (s32[192]{0:T(256)S(1)}, s32[192]{0:T(256)}, u32[]{:S(2)}) copy-start(s32[192]{0:T(256)} %param.19) | copy-start | bytes 2308
  0.0 46.6 %copy-start.2 = (s32[3]{0:T(128)S(1)}, s32[3]{0:T(128)}, u32[]{:S(2)}) copy-start(s32[3]{0:T(128)} %len_ref.1) | copy-start | bytes 40
  1.7 11.9 %all-to-all-start = ((bf16[8,2,8,256]{3,2,1,0:T(8,128)(2,1)}), bf16[8,2,8,256]{3,2,1,0:T(8,128)(2,1)S(1)}, u32[]{:S(2)}, u32[]{:S(2)}) async-start(bf16[8,2,8,256]{3,2,1,0:T(8,128)(2,1)} %broadcast_in_dim.169), calls=%async_computation | async-start | bytes 131072 | tf_op jit(solution)/shard_map/all_to_all | solution.py:136
  15.3 41.6 %copy-start.3 = (f32[2048,4]{0,1:T(4,128)S(1)}, f32[2048,4]{0,1:T(4,128)}, u32[]{:S(2)}) copy-start(f32[2048,4]{0,1:T(4,128)} %param.13) | copy-start | bytes 98308
  15.3 31.3 %all-to-all-start.1 = ((bf16[64,16,128]{2,1,0:T(8,128)(2,1)}), bf16[64,16,128]{2,1,0:T(8,128)(2,1)S(1)}, u32[]{:S(2)}, u32[]{:S(2)}) async-start(bf16[64,16,128]{2,1,0:T(8,128)(2,1)} %copy.77), calls=%async_computation.1 | async-start | bytes 524288 | tf_op jit(solution)/shard_map/all_to_all | solution.py:181
  46.6 1.4 %copy-start.1 = (bf16[3,2,1024,128]{3,2,1,0:T(8,128)(2,1)S(1)}, bf16[3,2,1024,128]{3,2,1,0:T(8,128)(2,1)}, u32[]{:S(2)}) copy-start(bf16[3,2,1024,128]{3,2,1,0:T(8,128)(2,1)} %cache_hbm.1) | copy-start | bytes 4718596
  50.8 24.7 %all-to-all-start.2 = ((bf16[64,32,128]{2,1,0:T(8,128)(2,1)}), bf16[64,32,128]{2,1,0:T(8,128)(2,1)S(1)}, u32[]{:S(2)}, u32[]{:S(2)}) async-start(bf16[64,32,128]{2,1,0:T(8,128)(2,1)} %shard_map.100), calls=%async_computation.2 | async-start | bytes 1048576 | tf_op jit(solution)/shard_map/all_to_all | solution.py:186

commit v9 on v8

--- a/solution.py
+++ b/solution.py
@@ -184,15 +184,33 @@
     row_count = kept_rows * topk_count
     returning = slot_attention(my_slots // requests, cache_len, incoming, cache_kv, score_scale)
     back = lax.all_to_all(returning, "grp", 0, 0, tiled=True)
-    back_num = back[:, :row_count].astype(jnp.float32).reshape(
-        group_count, kept_rows, topk_count, head_width
-    )
-    back_facts = back[:, row_count:, :3].astype(jnp.float32)
-    back_peak = back_facts[..., 0].reshape(group_count, kept_rows, topk_count)
-    back_den = (back_facts[..., 1] + back_facts[..., 2]).reshape(group_count, kept_rows, topk_count)
-
-    home_ids = group_idx * requests + jnp.arange(requests, dtype=jnp.int32)
-    matched = jnp.any(slot_table[None, :, :] == home_ids[:, None, None], axis=2)
+    serving = jnp.any(home_of == group_idx, axis=1)
+    place = jnp.cumsum(serving.astype(jnp.int32)) - 1
+    source_pick = serving[None, :] & (
+        place[None, :] == jnp.arange(slot_count, dtype=jnp.int32)[:, None]
+    )
+    source_valid = jnp.any(source_pick, axis=1)
+    source_request = jnp.sum(
+        jnp.where(source_pick, jnp.sum(jnp.where(mine, local_of, 0), axis=1)[None, :], 0), axis=1
+    )
+    chosen_blocks = (
+        jnp.einsum(
+            "kd,dx->kx",
+            source_pick.astype(back.dtype),
+            back.reshape(group_count, -1),
+            preferred_element_type=jnp.float32,
+        )
+        .reshape(slot_count, 2 * row_count, head_width)
+    )
+    back_num = chosen_blocks[:, :row_count].reshape(slot_count, kept_rows, topk_count, head_width)
+    back_facts = chosen_blocks[:, row_count:, :3]
+    back_peak = back_facts[..., 0].reshape(slot_count, kept_rows, topk_count)
+    back_den = (back_facts[..., 1] + back_facts[..., 2]).reshape(slot_count, kept_rows, topk_count)
+
+    matched = (
+        source_valid[None, :]
+        & (source_request[None, :] == jnp.arange(requests, dtype=jnp.int32)[:, None])
+    )
     candidate = jnp.where(matched[:, :, None, None], back_peak[None], -jnp.inf)
     running_max = jnp.maximum(tree_peak, jnp.max(candidate, axis=1))
     rescale = jnp.exp(tree_peak - running_max)

time: 80.6 us -> 79.2 us (0.983)
  other arithmetic: 6.53 us -> 5.27 us
  local copies, waits for them, and re-layouts: 6.01 us -> 4.76 us
  waiting for transfers between devices: 30.1 us -> 31 us
    reduce_sum x1, other arithmetic: 1.38 us -> 0.08 us  [on_device(): jnp.sum(weight[..., None] * back_num[None], axis=1)]
    dot_general x0 -> x1, matrix products: none -> 1.3 us  [on_device(): jnp.einsum('kd,dx->kx', source_pick.astype(back.dtype), back.reshape(grou...]
    dot_general x1, matrix products: 1.47 us -> 0.25 us  [on_device(): jnp.einsum('rtd,cdw->rtcw', acc_hidden, kv_weight, preferred_element_type...]
    all_to_all x1, waiting for transfers between devices: 16.3 us -> 17.4 us  [on_device(): back = lax.all_to_all(returning, 'grp', 0, 0, tiled=True)]
    eq x2 -> x0, local copies, waits for them, and re-layouts: 0.88 us -> none  [on_device(): matched = jnp.any(slot_table[None, :, :] == home_ids[:, None, None], axis=2)]
    mul x1, local copies, waits for them, and re-layouts: 0.82 us -> 0.01 us  [on_device(): weight[..., None] * back_num[None]]
    reshape x0 -> x1, local copies, waits for them, and re-layouts: none -> 0.81 us  [on_device(): slot_table = slot_request.reshape(group_count, slot_count)]
  transfers between devices with their start and end apart: 3 -> 3, of which waited for: 3 -> 2; matrix products, arithmetic and copies ran while one was open for 9% -> 8% of each run, Pallas kernels for 0% -> 0%
where the time goes in v9:
time: 79.2 us; the launch traced here: 78.6 us
  waiting for transfers between devices  31 us (39%)
  starting transfers between devices  30.4 us (38%)
  other arithmetic  5.27 us (7%)
  local copies, waits for them, and re-layouts  4.76 us (6%)
  matrix products  4.21 us (5%)
  Pallas kernels  2.79 us (4%)
    all_to_all x1, waiting for transfers between devices, on_device(): back = lax.all_to_all(returning, 'grp', 0, 0, tiled=True)  17.4 us
    all_to_all x1, starting transfers between devices, on_device(): incoming = lax.all_to_all(outgoing, 'grp', 0, 0, tiled=True)  17.2 us
    all_to_all x1, waiting for transfers between devices, on_device(): incoming = lax.all_to_all(outgoing, 'grp', 0, 0, tiled=True)  13.5 us
    all_to_all x1, starting transfers between devices, on_device(): lax.all_to_all(jnp.broadcast_to(acc_part[None], (model_count,) + acc_part...  6.79 us
    all_to_all x1, starting transfers between devices, on_device(): back = lax.all_to_all(returning, 'grp', 0, 0, tiled=True)  6.42 us
    pallas_call x1, Pallas kernels, slot_attention(): pl.pallas_call(functools.partial(slot_attention_kernel, scale=scale), out...  2.79 us
  transfers between devices with their start and end apart: 3, of which 2 were waited for; matrix products, arithmetic and copies ran while one was open for 8% of the time, Pallas kernels for 0%

profile of v9, /device:TPU:1, one launch (start us, length us, event | category | flops | bytes accessed | tf_op | source)
XLA Modules:
  0.0 78.6 jit_solution(10892840599902959905)
XLA Ops:
  0.0 1.1 %convolution_convert_fusion.1 = bf16[2,8,256]{2,1,0:T(8,128)(2,1)S(1)} fusion(bf16[2,32,256]{2,1,0:T(8,128)(2,1)} %param.10, s32[2,8]{1,0:T(2,128)} %param.16), kind=kOutput, calls=%fused_computation.11 | convolution fusion | flops 266752 | bytes 41024 | tf_op jit(solution)/shard_map/rat,rtd->rad/dot_general | solution.py:119
  1.1 0.6 broadcast_in_dim.188
  1.7 6.8 %all-to-all-start = ((bf16[8,2,8,256]{3,2,1,0:T(8,128)(2,1)}), bf16[8,2,8,256]{3,2,1,0:T(8,128)(2,1)S(1)}, u32[]{:S(2)}, u32[]{:S(2)}) async-start(bf16[8,2,8,256]{3,2,1,0:T(8,128)(2,1)} %broadcast_in_dim.188), calls=%async_computation | async-start | bytes 131072 | tf_op jit(solution)/shard_map/all_to_all | solution.py:136
  8.5 0.8 iota_compare_fusion.1
  9.3 1.0 %and_reduce_fusion = pred[2,8]{1,0:T(4,128)(4,1)S(1)} fusion(s32[2,8]{1,0:T(2,128)} %param.16, pred[8,8]{1,0:T(8,128)(4,1)S(1)} %iota_compare_fusion.2), kind=kLoop, calls=%fused_computation.49 | loop fusion | flops 368 | bytes 144 | tf_op jit(solution)/shard_map/reduce_or | solution.py:129
  10.3 0.8 %select_reduce_fusion.3 = s32[2,8,2]{1,2,0:T(2,128)S(1)} fusion(s32[2,32,2]{1,2,0:T(2,128)} %param.14, pred[2,8,32]{2,1,0:T(8,128)(4,1)S(1)} %iota_compare_fusion.1), kind=kLoop, calls=%fused_computation.43 | loop fusion | flops 2016 | bytes 1152 | tf_op jit(solution)/shard_map/reduce_sum | solution.py:125
  11.1 0.9 %select_reduce_fusion = s32[2,8,32]{2,1,0:T(8,128)S(1)} fusion(s32[2,32,32]{2,1,0:T(8,128)} %param.15, pred[2,8,32]{2,1,0:T(8,128)(4,1)S(1)} %iota_compare_fusion.1), kind=kLoop, calls=%fused_computation.20 | loop fusion | flops 32256 | bytes 10752 | tf_op jit(solution)/shard_map/reduce_sum | solution.py:126
  12.0 0.3 select_reduce_fusion.2
  12.4 0.8 %reshape.169 = s32[64,3]{1,0:T(8,128)S(1)} reshape(s32[192]{0:T(256)} %param.19) | data formatting | bytes 1536 | tf_op jit(solution)/shard_map/reshape | solution.py:168
  13.9 0.4 fusion.1
  14.4 0.3 fusion.22
  14.7 0.9 %copy.94 = bf16[64,16,128]{2,1,0:T(8,128)(2,1)} copy(bf16[64,16,128]{2,0,1:T(8,128)(2,1)S(1)} %fusion.22) | data formatting | bytes 524288 | tf_op jit(solution)/shard_map/dr,rxw->dxw/dot_general | solution.py:178
  15.6 17.2 %all-to-all-start.1 = ((bf16[64,16,128]{2,1,0:T(8,128)(2,1)}), bf16[64,16,128]{2,1,0:T(8,128)(2,1)S(1)}, u32[]{:S(2)}, u32[]{:S(2)}) async-start(bf16[64,16,128]{2,1,0:T(8,128)(2,1)} %copy.94), calls=%async_computation.1 | async-start | bytes 524288 | tf_op jit(solution)/shard_map/all_to_all | solution.py:181
  33.1 13.5 %all-to-all-done.1.incoming_ref = bf16[64,16,128]{2,1,0:T(8,128)(2,1)S(1)} async-done(((bf16[64,16,128]{2,1,0:T(8,128)(2,1)}), bf16[64,16,128]{2,1,0:T(8,128)(2,1)S(1)}, u32[]{:S(2)}, u32[]{:S(2)}) %all-to-all-start.1) | async-done | bytes 262176 | tf_op jit(solution)/shard_map/all_to_all | solution.py:181
  46.6 1.4 %copy-done.1 = bf16[3,2,1024,128]{3,2,1,0:T(8,128)(2,1)S(1)} copy-done((bf16[3,2,1024,128]{3,2,1,0:T(8,128)(2,1)S(1)}, bf16[3,2,1024,128]{3,2,1,0:T(8,128)(2,1)}, u32[]{:S(2)}) %copy-start.1) | copy-done | bytes 1572888
  48.0 2.8 %shard_map.100 = bf16[64,32,128]{2,1,0:T(8,128)(2,1)} custom-call(s32[3]{0:T(128)S(1)} %and_select_fusion.home_ref, s32[3]{0:T(128)S(1)} %copy-done.2, bf16[64,16,128]{2,1,0:T(8,128)(2,1)S(1)} %all-to-all-done.1.incoming_ref, bf16[3,2,1024,128]{3,2,1,0:T(8,128)(2,1)S(1)} %copy-done.1), custom_call_target="tpu_custom_call" | custom-call | flops 25165824 | bytes 2359296 | tf_op jit(solution)/shard_map/pallas_call | solution.py:72
  50.8 6.4 %all-to-all-start.2 = ((bf16[64,32,128]{2,1,0:T(8,128)(2,1)}), bf16[64,32,128]{2,1,0:T(8,128)(2,1)}, u32[]{:S(2)}, u32[]{:S(2)}) async-start(bf16[64,32,128]{2,1,0:T(8,128)(2,1)} %shard_map.100), calls=%async_computation.2 | async-start | bytes 1048576 | tf_op jit(solution)/shard_map/all_to_all | solution.py:186
  57.3 0.5 fusion.18
  57.8 0.2 convolution_convert_fusion
  58.3 17.4 %all-to-all-done.2 = bf16[64,32,128]{2,1,0:T(8,128)(2,1)} async-done(((bf16[64,32,128]{2,1,0:T(8,128)(2,1)}), bf16[64,32,128]{2,1,0:T(8,128)(2,1)}, u32[]{:S(2)}, u32[]{:S(2)}) %all-to-all-start.2) | async-done | bytes 524320 | tf_op jit(solution)/shard_map/all_to_all | solution.py:186
  75.8 1.3 %fusion.11 = f32[3,32,128]{2,0,1:T(4,128)S(1)} fusion(s32[64]{0:T(128)S(1)} %add_reduce_fusion, pred[64]{0:T(512)(128)(4,1)S(1)} %reduce_or.32, bf16[8,8,32,128]{3,2,1,0:T(8,128)(2,1)} %bitcast.27), kind=kOutput, calls=%fused_computation.16 | convolution fusion | flops 1573248 | bytes 573760 | tf_op jit(solution)/shard_map/kd,dx->kx/dot_general | solution.py:197
  77.1 0.2 fusion.17
  77.8 0.2 fusion.7
  78.0 0.6 copy.75
  (43 shorter events, 1.9 us)
Async XLA Ops:
  0.0 13.9 %copy-start = (bf16[4,2048,128]{2,1,0:T(8,128)(2,1)S(1)}, bf16[4,2048,128]{2,1,0:T(8,128)(2,1)}, u32[]{:S(2)}) copy-start(bf16[4,2048,128]{2,1,0:T(8,128)(2,1)} %param.11) | copy-start | bytes 6291460
  1.7 31.0 %copy-start.5 = (s32[192]{0:T(256)S(1)}, s32[192]{0:T(256)}, u32[]{:S(2)}) copy-start(s32[192]{0:T(256)} %param.19) | copy-start | bytes 2308
  1.7 44.9 %copy-start.2 = (s32[3]{0:T(128)S(1)}, s32[3]{0:T(128)}, u32[]{:S(2)}) copy-start(s32[3]{0:T(128)} %len_ref.1) | copy-start | bytes 40
  1.7 12.1 %all-to-all-start = ((bf16[8,2,8,256]{3,2,1,0:T(8,128)(2,1)}), bf16[8,2,8,256]{3,2,1,0:T(8,128)(2,1)S(1)}, u32[]{:S(2)}, u32[]{:S(2)}) async-start(bf16[8,2,8,256]{3,2,1,0:T(8,128)(2,1)} %broadcast_in_dim.188), calls=%async_computation | async-start | bytes 131072 | tf_op jit(solution)/shard_map/all_to_all | solution.py:136
  14.4 42.9 %copy-start.4 = (f32[2048,4]{0,1:T(4,128)S(1)}, f32[2048,4]{0,1:T(4,128)}, u32[]{:S(2)}) copy-start(f32[2048,4]{0,1:T(4,128)} %param.13) | copy-start | bytes 98308
  14.7 43.1 %copy-start.3 = (bf16[2,2048,128]{2,1,0:T(8,128)(2,1)S(1)}, bf16[2,2048,128]{2,1,0:T(8,128)(2,1)}, u32[]{:S(2)}) copy-start(bf16[2,2048,128]{2,1,0:T(8,128)(2,1)} %param.12) | copy-start | bytes 3145732
  15.6 31.0 %all-to-all-start.1 = ((bf16[64,16,128]{2,1,0:T(8,128)(2,1)}), bf16[64,16,128]{2,1,0:T(8,128)(2,1)S(1)}, u32[]{:S(2)}, u32[]{:S(2)}) async-start(bf16[64,16,128]{2,1,0:T(8,128)(2,1)} %copy.94), calls=%async_computation.1 | async-start | bytes 524288 | tf_op jit(solution)/shard_map/all_to_all | solution.py:181
  46.6 1.4 %copy-start.1 = (bf16[3,2,1024,128]{3,2,1,0:T(8,128)(2,1)S(1)}, bf16[3,2,1024,128]{3,2,1,0:T(8,128)(2,1)}, u32[]{:S(2)}) copy-start(bf16[3,2,1024,128]{3,2,1,0:T(8,128)(2,1)} %cache_hbm.1) | copy-start | bytes 4718596
  50.8 25.0 %all-to-all-start.2 = ((bf16[64,32,128]{2,1,0:T(8,128)(2,1)}), bf16[64,32,128]{2,1,0:T(8,128)(2,1)}, u32[]{:S(2)}, u32[]{:S(2)}) async-start(bf16[64,32,128]{2,1,0:T(8,128)(2,1)} %shard_map.100), calls=%async_computation.2 | async-start | bytes 1048576 | tf_op jit(solution)/shard_map/all_to_all | solution.py:186

commit v10 on v9

--- a/solution.py
+++ b/solution.py
@@ -193,15 +193,12 @@
     source_request = jnp.sum(
         jnp.where(source_pick, jnp.sum(jnp.where(mine, local_of, 0), axis=1)[None, :], 0), axis=1
     )
-    chosen_blocks = (
-        jnp.einsum(
-            "kd,dx->kx",
-            source_pick.astype(back.dtype),
-            back.reshape(group_count, -1),
-            preferred_element_type=jnp.float32,
-        )
-        .reshape(slot_count, 2 * row_count, head_width)
-    )
+    source_index = jnp.sum(
+        jnp.where(source_pick, jnp.arange(group_count, dtype=jnp.int32)[None, :], 0), axis=1
+    )
+    chosen_blocks = jnp.stack(
+        [lax.dynamic_index_in_dim(back, source_index[k], 0, keepdims=False) for k in range(slot_count)]
+    ).astype(jnp.float32)
     back_num = chosen_blocks[:, :row_count].reshape(slot_count, kept_rows, topk_count, head_width)
     back_facts = chosen_blocks[:, row_count:, :3]
     back_peak = back_facts[..., 0].reshape(slot_count, kept_rows, topk_count)

time: 79.2 us -> 82.8 us (1.045)
  between operations: 0.23 us -> 5.97 us
  waiting for transfers between devices: 31 us -> 29.2 us
  local copies, waits for them, and re-layouts: 4.76 us -> 6.3 us
  matrix products: 4.21 us -> 2.91 us
  starting transfers between devices: 30.4 us -> 29.5 us
    all_to_all x1, waiting for transfers between devices: 13.5 us -> 11.7 us  [on_device(): incoming = lax.all_to_all(outgoing, 'grp', 0, 0, tiled=True)]
    dot_general x1 -> x0, matrix products: 1.3 us -> none  [on_device(): jnp.einsum('kd,dx->kx', source_pick.astype(back.dtype), back.reshape(grou...]
    all_to_all x1, starting transfers between devices: 17.2 us -> 16.2 us  [on_device(): incoming = lax.all_to_all(outgoing, 'grp', 0, 0, tiled=True)]
  transfers between devices with their start and end apart: 3 -> 3, of which waited for: 2 -> 2; matrix products, arithmetic and copies ran while one was open for 8% -> 9% of each run, Pallas kernels for 0% -> 0%
where the time goes in v10:
time: 82.8 us; the launch traced here: 82 us
  starting transfers between devices  29.5 us (36%)
  waiting for transfers between devices  29.2 us (35%)
  local copies, waits for them, and re-layouts  6.3 us (8%)
  between operations  5.97 us (7%)
  other arithmetic  5.29 us (6%)
  matrix products  2.91 us (4%)
  Pallas kernels  2.79 us (3%)
    all_to_all x1, waiting for transfers between devices, on_device(): back = lax.all_to_all(returning, 'grp', 0, 0, tiled=True)  17.5 us
    all_to_all x1, starting transfers between devices, on_device(): incoming = lax.all_to_all(outgoing, 'grp', 0, 0, tiled=True)  16.2 us
    all_to_all x1, waiting for transfers between devices, on_device(): incoming = lax.all_to_all(outgoing, 'grp', 0, 0, tiled=True)  11.7 us
    all_to_all x1, starting transfers between devices, on_device(): lax.all_to_all(jnp.broadcast_to(acc_part[None], (model_count,) + acc_part...  6.79 us
    all_to_all x1, starting transfers between devices, on_device(): back = lax.all_to_all(returning, 'grp', 0, 0, tiled=True)  6.58 us
    pallas_call x1, Pallas kernels, slot_attention(): pl.pallas_call(functools.partial(slot_attention_kernel, scale=scale), out...  2.79 us
  transfers between devices with their start and end apart: 3, of which 2 were waited for; matrix products, arithmetic and copies ran while one was open for 9% of the time, Pallas kernels for 0%

profile of v10, /device:TPU:1, one launch (start us, length us, event | category | flops | bytes accessed | tf_op | source)
XLA Modules:
  0.0 82.0 jit_solution(7398635236818769388)
XLA Ops:
  0.0 1.1 %convolution_convert_fusion.1 = bf16[2,8,256]{2,1,0:T(8,128)(2,1)S(1)} fusion(bf16[2,32,256]{2,1,0:T(8,128)(2,1)} %param.10, s32[2,8]{1,0:T(2,128)} %param.16), kind=kOutput, calls=%fused_computation.11 | convolution fusion | flops 266752 | bytes 41024 | tf_op jit(solution)/shard_map/rat,rtd->rad/dot_general | solution.py:119
  1.1 0.6 broadcast_in_dim.195
  1.7 6.8 %all-to-all-start = ((bf16[8,2,8,256]{3,2,1,0:T(8,128)(2,1)}), bf16[8,2,8,256]{3,2,1,0:T(8,128)(2,1)S(1)}, u32[]{:S(2)}, u32[]{:S(2)}) async-start(bf16[8,2,8,256]{3,2,1,0:T(8,128)(2,1)} %broadcast_in_dim.195), calls=%async_computation | async-start | bytes 131072 | tf_op jit(solution)/shard_map/all_to_all | solution.py:136
  8.5 0.8 iota_compare_fusion.1
  9.3 1.0 %and_reduce_fusion = pred[2,8]{1,0:T(4,128)(4,1)S(1)} fusion(s32[2,8]{1,0:T(2,128)} %param.16, pred[8,8]{1,0:T(8,128)(4,1)S(1)} %iota_compare_fusion.2), kind=kLoop, calls=%fused_computation.46 | loop fusion | flops 368 | bytes 144 | tf_op jit(solution)/shard_map/reduce_or | solution.py:129
  10.3 0.8 %select_reduce_fusion.3 = s32[2,8,2]{1,2,0:T(2,128)S(1)} fusion(s32[2,32,2]{1,2,0:T(2,128)} %param.14, pred[2,8,32]{2,1,0:T(8,128)(4,1)S(1)} %iota_compare_fusion.1), kind=kLoop, calls=%fused_computation.40 | loop fusion | flops 2016 | bytes 1152 | tf_op jit(solution)/shard_map/reduce_sum | solution.py:125
  11.1 0.9 %select_reduce_fusion = s32[2,8,32]{2,1,0:T(8,128)S(1)} fusion(s32[2,32,32]{2,1,0:T(8,128)} %param.15, pred[2,8,32]{2,1,0:T(8,128)(4,1)S(1)} %iota_compare_fusion.1), kind=kLoop, calls=%fused_computation.16 | loop fusion | flops 32256 | bytes 10752 | tf_op jit(solution)/shard_map/reduce_sum | solution.py:126
  12.0 0.8 reshape.164
  13.7 0.7 fusion.32
  18.2 0.3 select_reduce_fusion.2
  18.6 0.4 fusion.1
  19.1 0.3 fusion.19
  19.4 0.9 %copy.66 = bf16[64,16,128]{2,1,0:T(8,128)(2,1)} copy(bf16[64,16,128]{2,0,1:T(8,128)(2,1)S(1)} %fusion.19) | data formatting | bytes 524288 | tf_op jit(solution)/shard_map/dr,rxw->dxw/dot_general | solution.py:178
  20.2 16.2 %all-to-all-start.1 = ((bf16[64,16,128]{2,1,0:T(8,128)(2,1)}), bf16[64,16,128]{2,1,0:T(8,128)(2,1)S(1)}, u32[]{:S(2)}, u32[]{:S(2)}) async-start(bf16[64,16,128]{2,1,0:T(8,128)(2,1)} %copy.66), calls=%async_computation.1 | async-start | bytes 524288 | tf_op jit(solution)/shard_map/all_to_all | solution.py:181
  38.5 11.7 %all-to-all-done.1.incoming_ref = bf16[64,16,128]{2,1,0:T(8,128)(2,1)S(1)} async-done(((bf16[64,16,128]{2,1,0:T(8,128)(2,1)}), bf16[64,16,128]{2,1,0:T(8,128)(2,1)S(1)}, u32[]{:S(2)}, u32[]{:S(2)}) %all-to-all-start.1) | async-done | bytes 262176 | tf_op jit(solution)/shard_map/all_to_all | solution.py:181
  50.3 1.4 %copy-done.1 = bf16[3,2,1024,128]{3,2,1,0:T(8,128)(2,1)S(1)} copy-done((bf16[3,2,1024,128]{3,2,1,0:T(8,128)(2,1)S(1)}, bf16[3,2,1024,128]{3,2,1,0:T(8,128)(2,1)}, u32[]{:S(2)}) %copy-start.1) | copy-done | bytes 1572888
  51.7 2.8 %shard_map.100 = bf16[64,32,128]{2,1,0:T(8,128)(2,1)} custom-call(s32[3]{0:T(128)S(1)} %and_select_fusion.home_ref, s32[3]{0:T(128)S(1)} %copy-done.2, bf16[64,16,128]{2,1,0:T(8,128)(2,1)S(1)} %all-to-all-done.1.incoming_ref, bf16[3,2,1024,128]{3,2,1,0:T(8,128)(2,1)S(1)} %copy-done.1), custom_call_target="tpu_custom_call" | custom-call | flops 25165824 | bytes 2359296 | tf_op jit(solution)/shard_map/pallas_call | solution.py:72
  54.5 6.6 %all-to-all-start.2 = ((bf16[64,32,128]{2,1,0:T(8,128)(2,1)}), bf16[64,32,128]{2,1,0:T(8,128)(2,1)}, u32[]{:S(2)}, u32[]{:S(2)}) async-start(bf16[64,32,128]{2,1,0:T(8,128)(2,1)} %shard_map.100), calls=%async_computation.2 | async-start | bytes 1048576 | tf_op jit(solution)/shard_map/all_to_all | solution.py:186
  61.1 0.5 fusion.14
  61.7 0.2 convolution_convert_fusion
  62.2 17.5 %all-to-all-done.2 = bf16[64,32,128]{2,1,0:T(8,128)(2,1)} async-done(((bf16[64,32,128]{2,1,0:T(8,128)(2,1)}), bf16[64,32,128]{2,1,0:T(8,128)(2,1)}, u32[]{:S(2)}, u32[]{:S(2)}) %all-to-all-start.2) | async-done | bytes 524320 | tf_op jit(solution)/shard_map/all_to_all | solution.py:186
  79.6 0.7 constant_dynamic-slice_fusion
  81.2 0.2 fusion.7
  81.4 0.6 copy.58
  (47 shorter events, 2.2 us)
Async XLA Ops:
  0.0 18.5 %copy-start = (bf16[4,2048,128]{2,1,0:T(8,128)(2,1)S(1)}, bf16[4,2048,128]{2,1,0:T(8,128)(2,1)}, u32[]{:S(2)}) copy-start(bf16[4,2048,128]{2,1,0:T(8,128)(2,1)} %param.11) | copy-start | bytes 6291460
  1.7 36.7 %copy-start.5 = (s32[192]{0:T(256)S(1)}, s32[192]{0:T(256)}, u32[]{:S(2)}) copy-start(s32[192]{0:T(256)} %param.19) | copy-start | bytes 2308
  1.7 48.5 %copy-start.2 = (s32[3]{0:T(128)S(1)}, s32[3]{0:T(128)}, u32[]{:S(2)}) copy-start(s32[3]{0:T(128)} %len_ref.1) | copy-start | bytes 40
  1.7 16.8 %all-to-all-start = ((bf16[8,2,8,256]{3,2,1,0:T(8,128)(2,1)}), bf16[8,2,8,256]{3,2,1,0:T(8,128)(2,1)S(1)}, u32[]{:S(2)}, u32[]{:S(2)}) async-start(bf16[8,2,8,256]{3,2,1,0:T(8,128)(2,1)} %broadcast_in_dim.195), calls=%async_computation | async-start | bytes 131072 | tf_op jit(solution)/shard_map/all_to_all | solution.py:136
  19.1 42.0 %copy-start.4 = (f32[2048,4]{0,1:T(4,128)S(1)}, f32[2048,4]{0,1:T(4,128)}, u32[]{:S(2)}) copy-start(f32[2048,4]{0,1:T(4,128)} %param.13) | copy-start | bytes 98308
  19.4 42.3 %copy-start.3 = (bf16[2,2048,128]{2,1,0:T(8,128)(2,1)S(1)}, bf16[2,2048,128]{2,1,0:T(8,128)(2,1)}, u32[]{:S(2)}) copy-start(bf16[2,2048,128]{2,1,0:T(8,128)(2,1)} %param.12) | copy-start | bytes 3145732
  20.2 30.0 %all-to-all-start.1 = ((bf16[64,16,128]{2,1,0:T(8,128)(2,1)}), bf16[64,16,128]{2,1,0:T(8,128)(2,1)S(1)}, u32[]{:S(2)}, u32[]{:S(2)}) async-start(bf16[64,16,128]{2,1,0:T(8,128)(2,1)} %copy.66), calls=%async_computation.1 | async-start | bytes 524288 | tf_op jit(solution)/shard_map/all_to_all | solution.py:181
  50.3 1.4 %copy-start.1 = (bf16[3,2,1024,128]{3,2,1,0:T(8,128)(2,1)S(1)}, bf16[3,2,1024,128]{3,2,1,0:T(8,128)(2,1)}, u32[]{:S(2)}) copy-start(bf16[3,2,1024,128]{3,2,1,0:T(8,128)(2,1)} %cache_hbm.1) | copy-start | bytes 4718596
  54.5 25.2 %all-to-all-start.2 = ((bf16[64,32,128]{2,1,0:T(8,128)(2,1)}), bf16[64,32,128]{2,1,0:T(8,128)(2,1)}, u32[]{:S(2)}, u32[]{:S(2)}) async-start(bf16[64,32,128]{2,1,0:T(8,128)(2,1)} %shard_map.100), calls=%async_computation.2 | async-start | bytes 1048576 | tf_op jit(solution)/shard_map/all_to_all | solution.py:186

commit v11 on v9

--- a/solution.py
+++ b/solution.py
@@ -19,25 +19,16 @@
     return (peak_score, denominator, numerator)
 
 
-def slot_attention_kernel(
-    home_ref, len_ref, incoming_ref, cache_hbm, out_ref, cache_buf, sems, *, scale
-):
-    slot_count = cache_buf.shape[0]
+def slot_attention_kernel(home_ref, len_ref, incoming_ref, cache_ref, out_ref, *, scale):
+    slot_count = cache_ref.shape[0]
     rows = incoming_ref.shape[1]
-    copies = [
-        pltpu.make_async_copy(cache_hbm.at[i], cache_buf.at[i], sems.at[i])
-        for i in range(slot_count)
-    ]
-    for copy in copies:
-        copy.start()
     out_ref[...] = jnp.zeros(out_ref.shape, out_ref.dtype)
     for i in range(slot_count):
         home = home_ref[i]
-        copies[i].wait()
         scores = (
             lax.dot_general(
                 incoming_ref[home],
-                cache_buf[i, 0],
+                cache_ref[i, 0],
                 (((1,), (1,)), ((), ())),
                 preferred_element_type=jnp.float32,
             )
@@ -48,7 +39,7 @@
         peak = jnp.max(masked, axis=1, keepdims=True)
         weights = jnp.exp(masked - peak).astype(jnp.bfloat16)
         den = jnp.sum(weights.astype(jnp.float32), axis=1, keepdims=True)
-        num = jnp.dot(weights, cache_buf[i, 1], preferred_element_type=jnp.float32)
+        num = jnp.dot(weights, cache_ref[i, 1], preferred_element_type=jnp.float32)
         peak_low = peak.astype(jnp.bfloat16).astype(jnp.float32)
         shift = jnp.exp(peak - peak_low)
         shifted_den = den * shift
@@ -76,14 +67,9 @@
             pl.BlockSpec(memory_space=pltpu.SMEM),
             pl.BlockSpec(memory_space=pltpu.SMEM),
             pl.BlockSpec(memory_space=pltpu.VMEM),
-            pl.BlockSpec(memory_space=pl.ANY),
+            pl.BlockSpec(memory_space=pltpu.VMEM),
         ],
         out_specs=pl.BlockSpec(memory_space=pltpu.VMEM),
-        scratch_shapes=[
-            pltpu.VMEM(cache_kv.shape, cache_kv.dtype),
-            pltpu.SemaphoreType.DMA((slot_count,)),
-        ],
-        compiler_params=pltpu.CompilerParams(vmem_limit_bytes=16 * 1024 * 1024),
         cost_estimate=pl.CostEstimate(
             flops=flops, transcendentals=slot_count * rows * cache_size, bytes_accessed=moved
         ),
@@ -172,12 +158,11 @@
     picked = jnp.sum(jnp.where(mine, local_of, 0), axis=1)
     any_mine = jnp.any(mine, axis=1)
     query_rows = queries.reshape(requests, kept_rows * topk_count, head_width)
-    send_pick = (
-        any_mine[:, None] & (picked[:, None] == jnp.arange(requests, dtype=jnp.int32)[None, :])
-    ).astype(query_rows.dtype)
-    outgoing = jnp.einsum(
-        "dr,rxw->dxw", send_pick, query_rows, preferred_element_type=jnp.float32
-    ).astype(query_rows.dtype)
+    outgoing = jnp.where(
+        any_mine[:, None, None],
+        jnp.where((picked == 1)[:, None, None], query_rows[1][None], query_rows[0][None]),
+        jnp.zeros((), query_rows.dtype),
+    )
     incoming = lax.all_to_all(outgoing, "grp", 0, 0, tiled=True)
 
     my_slots = lax.dynamic_slice_in_dim(slot_request, group_idx * slot_count, slot_count)

time: 79.2 us -> 78.5 us (level)
  local copies, waits for them, and re-layouts: 4.76 us -> 3.19 us
  other arithmetic: 5.27 us -> 6.68 us
    select_n x0 -> x1, other arithmetic: none -> 0.9 us  [on_device(): jnp.where(any_mine[:, None, None], jnp.where((picked == 1)[:, None, None]...]
    dot_general x1 -> x0, local copies, waits for them, and re-layouts: 0.87 us -> none  [on_device(): jnp.einsum('dr,rxw->dxw', send_pick, query_rows, preferred_element_type=j...]
  transfers between devices with their start and end apart: 3 -> 3, of which waited for: 2 -> 2; matrix products, arithmetic and copies ran while one was open for 8% -> 9% of each run, Pallas kernels for 0% -> 0%
where the time goes in v11:
time: 78.5 us; the launch traced here: 78 us
  waiting for transfers between devices  30.4 us (39%)
  starting transfers between devices  30.2 us (38%)
  other arithmetic  6.68 us (9%)
  matrix products  3.92 us (5%)
  Pallas kernels  3.3 us (4%)
  local copies, waits for them, and re-layouts  3.19 us (4%)
    all_to_all x1, waiting for transfers between devices, on_device(): back = lax.all_to_all(returning, 'grp', 0, 0, tiled=True)  17.4 us
    all_to_all x1, starting transfers between devices, on_device(): incoming = lax.all_to_all(outgoing, 'grp', 0, 0, tiled=True)  17.2 us
    all_to_all x1, waiting for transfers between devices, on_device(): incoming = lax.all_to_all(outgoing, 'grp', 0, 0, tiled=True)  13 us
    all_to_all x1, starting transfers between devices, on_device(): lax.all_to_all(jnp.broadcast_to(acc_part[None], (model_count,) + acc_part...  6.66 us
    all_to_all x1, starting transfers between devices, on_device(): back = lax.all_to_all(returning, 'grp', 0, 0, tiled=True)  6.4 us
    pallas_call x1, Pallas kernels, slot_attention(): pl.pallas_call(functools.partial(slot_attention_kernel, scale=scale), out...  3.3 us
  transfers between devices with their start and end apart: 3, of which 2 were waited for; matrix products, arithmetic and copies ran while one was open for 9% of the time, Pallas kernels for 0%

profile of v11, /device:TPU:1, one launch (start us, length us, event | category | flops | bytes accessed | tf_op | source)
XLA Modules:
  0.0 78.0 jit_solution(16059818296782785830)
XLA Ops:
  0.0 1.1 %convolution_convert_fusion.1 = bf16[2,8,256]{2,1,0:T(8,128)(2,1)S(1)} fusion(bf16[2,32,256]{2,1,0:T(8,128)(2,1)} %param.10, s32[2,8]{1,0:T(2,128)} %param.16), kind=kOutput, calls=%fused_computation.11 | convolution fusion | flops 266752 | bytes 41024 | tf_op jit(solution)/shard_map/rat,rtd->rad/dot_general | solution.py:105
  1.1 0.6 broadcast_in_dim.227
  1.7 6.7 %all-to-all-start = ((bf16[8,2,8,256]{3,2,1,0:T(8,128)(2,1)}), bf16[8,2,8,256]{3,2,1,0:T(8,128)(2,1)S(1)}, u32[]{:S(2)}, u32[]{:S(2)}) async-start(bf16[8,2,8,256]{3,2,1,0:T(8,128)(2,1)} %broadcast_in_dim.227), calls=%async_computation | async-start | bytes 131072 | tf_op jit(solution)/shard_map/all_to_all | solution.py:122
  8.4 0.8 iota_compare_fusion.1
  9.2 1.0 %and_reduce_fusion = pred[2,8]{1,0:T(4,128)(4,1)S(1)} fusion(s32[2,8]{1,0:T(2,128)} %param.16, pred[8,8]{1,0:T(8,128)(4,1)S(1)} %iota_compare_fusion.2), kind=kLoop, calls=%fused_computation.47 | loop fusion | flops 368 | bytes 144 | tf_op jit(solution)/shard_map/reduce_or | solution.py:115
  10.1 0.8 %select_reduce_fusion.3 = s32[2,8,2]{1,2,0:T(2,128)S(1)} fusion(s32[2,32,2]{1,2,0:T(2,128)} %param.14, pred[2,8,32]{2,1,0:T(8,128)(4,1)S(1)} %iota_compare_fusion.1), kind=kLoop, calls=%fused_computation.43 | loop fusion | flops 2016 | bytes 1152 | tf_op jit(solution)/shard_map/reduce_sum | solution.py:111
  11.0 0.9 %select_reduce_fusion = s32[2,8,32]{2,1,0:T(8,128)S(1)} fusion(s32[2,32,32]{2,1,0:T(8,128)} %param.15, pred[2,8,32]{2,1,0:T(8,128)(4,1)S(1)} %iota_compare_fusion.1), kind=kLoop, calls=%fused_computation.20 | loop fusion | flops 32256 | bytes 10752 | tf_op jit(solution)/shard_map/reduce_sum | solution.py:112
  11.9 0.3 select_reduce_fusion.2
  12.2 0.8 %reshape.173 = s32[64,3]{1,0:T(8,128)S(1)} reshape(s32[192]{0:T(256)} %param.19) | data formatting | bytes 1536 | tf_op jit(solution)/shard_map/reshape | solution.py:154
  13.8 0.4 fusion.1
  14.3 0.9 %select_select_fusion = bf16[64,16,128]{2,1,0:T(8,128)(2,1)} fusion(pred[64]{0:T(512)(128)(4,1)S(1)} %broadcast_compare_fusion, pred[64]{0:T(512)(128)(4,1)S(1)} %get-tuple-element.9, bf16[16,128]{1,0:T(8,128)(2,1)S(1)} %bitcast.66, bf16[16,128]{1,0:T(8,128)(2,1)S(1)} %bitcast.65), kind=kLoop, calls=%fused_computation.19 | loop fusion | flops 262144 | bytes 270464 | tf_op jit(solution)/shard_map/jit(_where)/select_n | solution.py:161
  15.2 17.2 %all-to-all-start.1 = ((bf16[64,16,128]{2,1,0:T(8,128)(2,1)}), bf16[64,16,128]{2,1,0:T(8,128)(2,1)S(1)}, u32[]{:S(2)}, u32[]{:S(2)}) async-start(bf16[64,16,128]{2,1,0:T(8,128)(2,1)} %select_select_fusion), calls=%async_computation.1 | async-start | bytes 524288 | tf_op jit(solution)/shard_map/all_to_all | solution.py:166
  32.4 0.6 and_select_fusion.home_ref
  33.2 13.0 %all-to-all-done.1.incoming_ref = bf16[64,16,128]{2,1,0:T(8,128)(2,1)S(1)} async-done(((bf16[64,16,128]{2,1,0:T(8,128)(2,1)}), bf16[64,16,128]{2,1,0:T(8,128)(2,1)S(1)}, u32[]{:S(2)}, u32[]{:S(2)}) %all-to-all-start.1) | async-done | bytes 262176 | tf_op jit(solution)/shard_map/all_to_all | solution.py:166
  46.2 0.7 copy-done.1
  46.9 3.3 %shard_map.100 = bf16[64,32,128]{2,1,0:T(8,128)(2,1)} custom-call(s32[3]{0:T(128)} %and_select_fusion.home_ref, s32[3]{0:T(128)} %len_ref.1, bf16[64,16,128]{2,1,0:T(8,128)(2,1)} %copy-done.1, bf16[3,2,1024,128]{3,2,1,0:T(8,128)(2,1)} %cache_ref.1), custom_call_target="tpu_custom_call" | custom-call | flops 25165824 | bytes 2359296 | tf_op jit(solution)/shard_map/pallas_call | solution.py:63
  50.2 6.4 %all-to-all-start.2 = ((bf16[64,32,128]{2,1,0:T(8,128)(2,1)}), bf16[64,32,128]{2,1,0:T(8,128)(2,1)}, u32[]{:S(2)}, u32[]{:S(2)}) async-start(bf16[64,32,128]{2,1,0:T(8,128)(2,1)} %shard_map.100), calls=%async_computation.2 | async-start | bytes 1048576 | tf_op jit(solution)/shard_map/all_to_all | solution.py:171
  56.7 0.5 fusion.18
  57.2 0.2 convolution_convert_fusion
  57.7 17.4 %all-to-all-done.2 = bf16[64,32,128]{2,1,0:T(8,128)(2,1)} async-done(((bf16[64,32,128]{2,1,0:T(8,128)(2,1)}), bf16[64,32,128]{2,1,0:T(8,128)(2,1)}, u32[]{:S(2)}, u32[]{:S(2)}) %all-to-all-start.2) | async-done | bytes 524320 | tf_op jit(solution)/shard_map/all_to_all | solution.py:171
  75.2 1.3 %fusion.11 = f32[3,32,128]{2,0,1:T(4,128)S(1)} fusion(s32[64]{0:T(128)S(1)} %add_reduce_fusion, pred[64]{0:T(512)(128)(4,1)S(1)} %get-tuple-element.9, bf16[8,8,32,128]{3,2,1,0:T(8,128)(2,1)} %bitcast.27), kind=kOutput, calls=%fused_computation.16 | convolution fusion | flops 1573248 | bytes 573760 | tf_op jit(solution)/shard_map/kd,dx->kx/dot_general | solution.py:182
  76.5 0.2 fusion.17
  77.2 0.2 fusion.7
  77.4 0.6 copy.58
  (43 shorter events, 1.8 us)
Async XLA Ops:
  0.0 13.8 %copy-start = (bf16[4,2048,128]{2,1,0:T(8,128)(2,1)S(1)}, bf16[4,2048,128]{2,1,0:T(8,128)(2,1)}, u32[]{:S(2)}) copy-start(bf16[4,2048,128]{2,1,0:T(8,128)(2,1)} %param.11) | copy-start | bytes 6291460
  0.0 32.4 %copy-start.4 = (s32[192]{0:T(256)S(1)}, s32[192]{0:T(256)}, u32[]{:S(2)}) copy-start(s32[192]{0:T(256)} %param.19) | copy-start | bytes 2308
  1.7 12.0 %all-to-all-start = ((bf16[8,2,8,256]{3,2,1,0:T(8,128)(2,1)}), bf16[8,2,8,256]{3,2,1,0:T(8,128)(2,1)S(1)}, u32[]{:S(2)}, u32[]{:S(2)}) async-start(bf16[8,2,8,256]{3,2,1,0:T(8,128)(2,1)} %broadcast_in_dim.227), calls=%async_computation | async-start | bytes 131072 | tf_op jit(solution)/shard_map/all_to_all | solution.py:122
  14.3 42.4 %copy-start.3 = (f32[2048,4]{0,1:T(4,128)S(1)}, f32[2048,4]{0,1:T(4,128)}, u32[]{:S(2)}) copy-start(f32[2048,4]{0,1:T(4,128)} %param.13) | copy-start | bytes 98308
  14.3 42.9 %copy-start.2 = (bf16[2,2048,128]{2,1,0:T(8,128)(2,1)S(1)}, bf16[2,2048,128]{2,1,0:T(8,128)(2,1)}, u32[]{:S(2)}) copy-start(bf16[2,2048,128]{2,1,0:T(8,128)(2,1)} %param.12) | copy-start | bytes 3145732
  15.2 31.0 %all-to-all-start.1 = ((bf16[64,16,128]{2,1,0:T(8,128)(2,1)}), bf16[64,16,128]{2,1,0:T(8,128)(2,1)S(1)}, u32[]{:S(2)}, u32[]{:S(2)}) async-start(bf16[64,16,128]{2,1,0:T(8,128)(2,1)} %select_select_fusion), calls=%async_computation.1 | async-start | bytes 524288 | tf_op jit(solution)/shard_map/all_to_all | solution.py:166
  46.2 0.7 copy-start.1
  50.2 24.9 %all-to-all-start.2 = ((bf16[64,32,128]{2,1,0:T(8,128)(2,1)}), bf16[64,32,128]{2,1,0:T(8,128)(2,1)}, u32[]{:S(2)}, u32[]{:S(2)}) async-start(bf16[64,32,128]{2,1,0:T(8,128)(2,1)} %shard_map.100), calls=%async_computation.2 | async-start | bytes 1048576 | tf_op jit(solution)/shard_map/all_to_all | solution.py:171

commit v12 on v11

--- a/solution.py
+++ b/solution.py
@@ -76,6 +76,43 @@
     )(home, cache_len, incoming, cache_kv)
 
 
+def blend_kernel(
+    index_ref, request_ref, back_ref, peak_ref, den_ref, num_ref, gate_ref, out_ref
+):
+    rows = num_ref.shape[1]
+    for j in range(out_ref.shape[0]):
+        blocks = []
+        for k in range(index_ref.shape[0]):
+            block = index_ref[k]
+            serves = request_ref[k] == j
+            blocks.append((block, serves, back_ref[block, rows:, 0:1].astype(jnp.float32)))
+        running_max = peak_ref[j]
+        for block, serves, peak in blocks:
+            running_max = jnp.where(serves, jnp.maximum(running_max, peak), running_max)
+        rescale = jnp.exp(peak_ref[j] - running_max)
+        denominator = den_ref[j] * rescale
+        numerator = num_ref[j] * rescale
+        for block, serves, peak in blocks:
+            weight = jnp.where(serves, jnp.exp(peak - running_max), 0.0)
+            total = back_ref[block, rows:, 1:2].astype(jnp.float32) + back_ref[
+                block, rows:, 2:3
+            ].astype(jnp.float32)
+            denominator = denominator + weight * total
+            numerator = numerator + weight * back_ref[block, :rows, :].astype(jnp.float32)
+        out_ref[j] = (gate_ref[j] * numerator / denominator).astype(out_ref.dtype)
+
+
+def blend(index, request, back, peak, den, num, gate):
+    smem = pl.BlockSpec(memory_space=pltpu.SMEM)
+    vmem = pl.BlockSpec(memory_space=pltpu.VMEM)
+    return pl.pallas_call(
+        blend_kernel,
+        out_shape=jax.ShapeDtypeStruct(num.shape, jnp.bfloat16),
+        in_specs=[smem, smem, vmem, vmem, vmem, vmem, vmem],
+        out_specs=vmem,
+    )(index, request, back, peak, den, num, gate)
+
+
 def on_device(
     draft_hidden,
     q_weight,
@@ -178,33 +215,19 @@
     source_request = jnp.sum(
         jnp.where(source_pick, jnp.sum(jnp.where(mine, local_of, 0), axis=1)[None, :], 0), axis=1
     )
-    chosen_blocks = (
-        jnp.einsum(
-            "kd,dx->kx",
-            source_pick.astype(back.dtype),
-            back.reshape(group_count, -1),
-            preferred_element_type=jnp.float32,
-        )
-        .reshape(slot_count, 2 * row_count, head_width)
-    )
-    back_num = chosen_blocks[:, :row_count].reshape(slot_count, kept_rows, topk_count, head_width)
-    back_facts = chosen_blocks[:, row_count:, :3]
-    back_peak = back_facts[..., 0].reshape(slot_count, kept_rows, topk_count)
-    back_den = (back_facts[..., 1] + back_facts[..., 2]).reshape(slot_count, kept_rows, topk_count)
-
-    matched = (
-        source_valid[None, :]
-        & (source_request[None, :] == jnp.arange(requests, dtype=jnp.int32)[:, None])
-    )
-    candidate = jnp.where(matched[:, :, None, None], back_peak[None], -jnp.inf)
-    running_max = jnp.maximum(tree_peak, jnp.max(candidate, axis=1))
-    rescale = jnp.exp(tree_peak - running_max)
-    weight = jnp.exp(candidate - running_max[:, None])
-    denominator = tree_den * rescale + jnp.sum(weight * back_den[None], axis=1)
-    numerator = tree_num * rescale[..., None] + jnp.sum(
-        weight[..., None] * back_num[None], axis=1
-    )
-    mixed = gate_probs[..., None] * numerator / denominator[..., None]
+    source_index = jnp.sum(
+        jnp.where(source_pick, jnp.arange(group_count, dtype=jnp.int32)[None, :], 0), axis=1
+    )
+    source_request = jnp.where(source_valid, source_request, -1)
+    mixed = blend(
+        source_index,
+        source_request,
+        back,
+        tree_peak.reshape(requests, row_count, 1),
+        tree_den.reshape(requests, row_count, 1),
+        tree_num.reshape(requests, row_count, head_width),
+        gate_probs.reshape(requests, row_count, 1),
+    )
     return mixed.reshape(requests, kept_rows, topk_count, head_width).astype(jnp.bfloat16)
 
 

time: 78.5 us -> 80.2 us (1.022)
  waiting for transfers between devices: 30.4 us -> 27.1 us
  local copies, waits for them, and re-layouts: 3.19 us -> 6.05 us
  Pallas kernels: 3.3 us -> 5.22 us
  other arithmetic: 6.68 us -> 7.95 us
  starting transfers between devices: 30.2 us -> 29.2 us
    all_to_all x1, waiting for transfers between devices: 17.4 us -> 13.9 us  [on_device(): back = lax.all_to_all(returning, 'grp', 0, 0, tiled=True)]
    pallas_call x0 -> x1, Pallas kernels: none -> 1.92 us  [blend(): pl.pallas_call(blend_kernel, out_shape=jax.ShapeDtypeStruct(num.shape, jn...]
    reshape x0 -> x2, local copies, waits for them, and re-layouts: none -> 1.35 us  [the longest x1 0.68 us: on_device(): tree_den.reshape(requests, row_count, 1)]
    dot_general x1 -> x0, matrix products: 1.3 us -> none  [on_device(): jnp.einsum('kd,dx->kx', source_pick.astype(back.dtype), back.reshape(grou...]
    dot_general x1, matrix products: 0.25 us -> 1.47 us  [on_device(): jnp.einsum('rtd,cdw->rtcw', acc_hidden, kv_weight, preferred_element_type...]
    all_to_all x1, starting transfers between devices: 17.2 us -> 16.2 us  [on_device(): incoming = lax.all_to_all(outgoing, 'grp', 0, 0, tiled=True)]
  transfers between devices with their start and end apart: 3 -> 3, of which waited for: 2 -> 2; matrix products, arithmetic and copies ran while one was open for 9% -> 17% of each run, Pallas kernels for 0% -> 0%
where the time goes in v12:
time: 80.2 us; the launch traced here: 79.6 us
  starting transfers between devices  29.2 us (36%)
  waiting for transfers between devices  27.1 us (34%)
  other arithmetic  7.95 us (10%)
  local copies, waits for them, and re-layouts  6.05 us (8%)
  Pallas kernels  5.22 us (7%)
  matrix products  3.85 us (5%)
    all_to_all x1, starting transfers between devices, on_device(): incoming = lax.all_to_all(outgoing, 'grp', 0, 0, tiled=True)  16.2 us
    all_to_all x1, waiting for transfers between devices, on_device(): back = lax.all_to_all(returning, 'grp', 0, 0, tiled=True)  13.9 us
    all_to_all x1, waiting for transfers between devices, on_device(): incoming = lax.all_to_all(outgoing, 'grp', 0, 0, tiled=True)  13.2 us
    all_to_all x1, starting transfers between devices, on_device(): lax.all_to_all(jnp.broadcast_to(acc_part[None], (model_count,) + acc_part...  6.66 us
    all_to_all x1, starting transfers between devices, on_device(): back = lax.all_to_all(returning, 'grp', 0, 0, tiled=True)  6.37 us
    pallas_call x1, Pallas kernels, slot_attention(): pl.pallas_call(functools.partial(slot_attention_kernel, scale=scale), out...  3.3 us
    pallas_call x1, Pallas kernels, blend(): pl.pallas_call(blend_kernel, out_shape=jax.ShapeDtypeStruct(num.shape, jn...  1.92 us
  transfers between devices with their start and end apart: 3, of which 2 were waited for; matrix products, arithmetic and copies ran while one was open for 17% of the time, Pallas kernels for 0%

profile of v12, /device:TPU:1, one launch (start us, length us, event | category | flops | bytes accessed | tf_op | source)
XLA Modules:
  0.0 79.6 jit_solution(3191297874284092029)
XLA Ops:
  0.0 1.1 %convolution_convert_fusion.1 = bf16[2,8,256]{2,1,0:T(8,128)(2,1)S(1)} fusion(bf16[2,32,256]{2,1,0:T(8,128)(2,1)} %param.10, s32[2,8]{1,0:T(2,128)} %param.16), kind=kOutput, calls=%fused_computation.6 | convolution fusion | flops 266752 | bytes 41024 | tf_op jit(solution)/shard_map/rat,rtd->rad/dot_general | solution.py:142
  1.1 0.6 broadcast_in_dim.214
  1.7 6.7 %all-to-all-start = ((bf16[8,2,8,256]{3,2,1,0:T(8,128)(2,1)}), bf16[8,2,8,256]{3,2,1,0:T(8,128)(2,1)S(1)}, u32[]{:S(2)}, u32[]{:S(2)}) async-start(bf16[8,2,8,256]{3,2,1,0:T(8,128)(2,1)} %broadcast_in_dim.214), calls=%async_computation | async-start | bytes 131072 | tf_op jit(solution)/shard_map/all_to_all | solution.py:159
  8.4 0.8 iota_compare_fusion.1
  9.2 1.0 %and_reduce_fusion = pred[2,8]{1,0:T(4,128)(4,1)S(1)} fusion(s32[2,8]{1,0:T(2,128)} %param.16, pred[8,8]{1,0:T(8,128)(4,1)S(1)} %iota_compare_fusion.2), kind=kLoop, calls=%fused_computation.34 | loop fusion | flops 368 | bytes 144 | tf_op jit(solution)/shard_map/reduce_or | solution.py:152
  10.1 0.8 %select_reduce_fusion.3 = s32[2,8,2]{1,2,0:T(2,128)S(1)} fusion(s32[2,32,2]{1,2,0:T(2,128)} %param.14, pred[2,8,32]{2,1,0:T(8,128)(4,1)S(1)} %iota_compare_fusion.1), kind=kLoop, calls=%fused_computation.30 | loop fusion | flops 2016 | bytes 1152 | tf_op jit(solution)/shard_map/reduce_sum | solution.py:148
  11.0 0.9 %select_reduce_fusion = s32[2,8,32]{2,1,0:T(8,128)S(1)} fusion(s32[2,32,32]{2,1,0:T(8,128)} %param.15, pred[2,8,32]{2,1,0:T(8,128)(4,1)S(1)} %iota_compare_fusion.1), kind=kLoop, calls=%fused_computation.10 | loop fusion | flops 32256 | bytes 10752 | tf_op jit(solution)/shard_map/reduce_sum | solution.py:149
  12.2 0.8 %reshape.145 = s32[64,3]{1,0:T(8,128)S(1)} reshape(s32[192]{0:T(256)} %param.19) | data formatting | bytes 1536 | tf_op jit(solution)/shard_map/reshape | solution.py:191
  13.8 0.7 select_reduce_fusion.5
  15.0 1.3 %and_select_fusion.home_ref = s32[3]{0:T(128)} fusion(s32[192]{0:T(256)} %param.19, s32[]{:T(128)S(6)} %select_n.74), kind=kLoop, calls=%fused_computation.44 | loop fusion | flops 45 | bytes 28 | tf_op jit(solution)/shard_map/jit(floor_divide)/jit(_where)/select_n | solution.py:207
  16.9 0.9 %select_select_fusion = bf16[64,16,128]{2,1,0:T(8,128)(2,1)} fusion(pred[64]{0:T(512)(128)(4,1)S(1)} %broadcast_compare_fusion, pred[64]{0:T(512)(128)(4,1)S(1)} %reduce_or.27, bf16[16,128]{1,0:T(8,128)(2,1)S(1)} %bitcast.47, bf16[16,128]{1,0:T(8,128)(2,1)S(1)} %bitcast.46), kind=kLoop, calls=%fused_computation.11 | loop fusion | flops 262144 | bytes 270464 | tf_op jit(solution)/shard_map/jit(_where)/select_n | solution.py:198
  17.8 16.2 %all-to-all-start.1 = ((bf16[64,16,128]{2,1,0:T(8,128)(2,1)}), bf16[64,16,128]{2,1,0:T(8,128)(2,1)S(1)}, u32[]{:S(2)}, u32[]{:S(2)}) async-start(bf16[64,16,128]{2,1,0:T(8,128)(2,1)} %select_select_fusion), calls=%async_computation.1 | async-start | bytes 524288 | tf_op jit(solution)/shard_map/all_to_all | solution.py:203
  34.6 13.2 %all-to-all-done.1.incoming_ref = bf16[64,16,128]{2,1,0:T(8,128)(2,1)S(1)} async-done(((bf16[64,16,128]{2,1,0:T(8,128)(2,1)}), bf16[64,16,128]{2,1,0:T(8,128)(2,1)S(1)}, u32[]{:S(2)}, u32[]{:S(2)}) %all-to-all-start.1) | async-done | bytes 262176 | tf_op jit(solution)/shard_map/all_to_all | solution.py:203
  47.8 0.7 copy-done.2
  48.5 3.3 %shard_map.100 = bf16[64,32,128]{2,1,0:T(8,128)(2,1)} custom-call(s32[3]{0:T(128)} %and_select_fusion.home_ref, s32[3]{0:T(128)} %len_ref.1, bf16[64,16,128]{2,1,0:T(8,128)(2,1)} %copy-done.2, bf16[3,2,1024,128]{3,2,1,0:T(8,128)(2,1)} %cache_ref.1), custom_call_target="tpu_custom_call" | custom-call | flops 25165824 | bytes 2359296 | tf_op jit(solution)/shard_map/pallas_call | solution.py:63
  51.8 6.4 %all-to-all-start.2 = ((bf16[64,32,128]{2,1,0:T(8,128)(2,1)}), bf16[64,32,128]{2,1,0:T(8,128)(2,1)S(1)}, u32[]{:S(2)}, u32[]{:S(2)}) async-start(bf16[64,32,128]{2,1,0:T(8,128)(2,1)} %shard_map.100), calls=%async_computation.2 | async-start | bytes 1048576 | tf_op jit(solution)/shard_map/all_to_all | solution.py:208
  58.3 0.7 div.47.gate_ref
  59.0 1.5 %convolution_convert_fusion = bf16[2,8,2,128]{3,1,2,0:T(8,128)(2,1)S(1)} fusion(bf16[2,8,2048,1]{2,1,3,0:T(8,128)(2,1)S(1)} %bitcast.43, bf16[2,2048,128]{2,1,0:T(8,128)(2,1)} %param.12), kind=kOutput, calls=%fused_computation.5 | convolution fusion | flops 16781312 | bytes 1122304 | tf_op jit(solution)/shard_map/rtd,cdw->rtcw/dot_general | solution.py:171
  60.9 0.6 copy.53
  61.6 0.7 reshape.159.den_ref
  62.3 0.7 reshape.158.peak_ref
  63.0 13.9 %all-to-all-done.2.back_ref = bf16[64,32,128]{2,1,0:T(8,128)(2,1)S(1)} async-done(((bf16[64,32,128]{2,1,0:T(8,128)(2,1)}), bf16[64,32,128]{2,1,0:T(8,128)(2,1)S(1)}, u32[]{:S(2)}, u32[]{:S(2)}) %all-to-all-start.2) | async-done | bytes 524320 | tf_op jit(solution)/shard_map/all_to_all | solution.py:208
  76.9 0.8 copy-done.1
  77.7 1.9 %shard_map.101 = bf16[2,16,128]{2,1,0:T(8,128)(2,1)} custom-call(s32[3]{0:T(128)} %get-tuple-element.6.index_ref, s32[3]{0:T(128)} %broadcast_select_fusion.request_ref, bf16[64,32,128]{2,1,0:T(8,128)(2,1)} %copy-done.1, f32[2,16,1]{2,1,0:T(8,128)} %reshape.158.peak_ref, f32[2,16,1]{2,1,0:T(8,128)} %reshape.159.den_ref, f32[2,16,128]{2,1,0:T(8,128)} %bitcast.45, ...), custom_call_target="tpu_custom_call" | custom-call | tf_op jit(solution)/shard_map/pallas_call | solution.py:108
  (38 shorter events, 3.4 us)
Async XLA Ops:
  0.0 16.3 %copy-start = (bf16[4,2048,128]{2,1,0:T(8,128)(2,1)S(1)}, bf16[4,2048,128]{2,1,0:T(8,128)(2,1)}, u32[]{:S(2)}) copy-start(bf16[4,2048,128]{2,1,0:T(8,128)(2,1)} %param.11) | copy-start | bytes 6291460
  0.0 33.9 %copy-start.3 = (f32[2048,4]{0,1:T(4,128)S(1)}, f32[2048,4]{0,1:T(4,128)}, u32[]{:S(2)}) copy-start(f32[2048,4]{0,1:T(4,128)} %param.13) | copy-start | bytes 98308
  1.7 14.6 %all-to-all-start = ((bf16[8,2,8,256]{3,2,1,0:T(8,128)(2,1)}), bf16[8,2,8,256]{3,2,1,0:T(8,128)(2,1)S(1)}, u32[]{:S(2)}, u32[]{:S(2)}) async-start(bf16[8,2,8,256]{3,2,1,0:T(8,128)(2,1)} %broadcast_in_dim.214), calls=%async_computation | async-start | bytes 131072 | tf_op jit(solution)/shard_map/all_to_all | solution.py:159
  17.8 30.0 %all-to-all-start.1 = ((bf16[64,16,128]{2,1,0:T(8,128)(2,1)}), bf16[64,16,128]{2,1,0:T(8,128)(2,1)S(1)}, u32[]{:S(2)}, u32[]{:S(2)}) async-start(bf16[64,16,128]{2,1,0:T(8,128)(2,1)} %select_select_fusion), calls=%async_computation.1 | async-start | bytes 524288 | tf_op jit(solution)/shard_map/all_to_all | solution.py:203
  47.8 0.7 copy-start.2
  51.8 25.1 %all-to-all-start.2 = ((bf16[64,32,128]{2,1,0:T(8,128)(2,1)}), bf16[64,32,128]{2,1,0:T(8,128)(2,1)S(1)}, u32[]{:S(2)}, u32[]{:S(2)}) async-start(bf16[64,32,128]{2,1,0:T(8,128)(2,1)} %shard_map.100), calls=%async_computation.2 | async-start | bytes 1048576 | tf_op jit(solution)/shard_map/all_to_all | solution.py:208
  76.9 0.8 copy-start.1

commit v13 on v11

--- a/solution.py
+++ b/solution.py
@@ -19,15 +19,24 @@
     return (peak_score, denominator, numerator)
 
 
-def slot_attention_kernel(home_ref, len_ref, incoming_ref, cache_ref, out_ref, *, scale):
+def slot_attention_kernel(
+    home_ref, len_ref, incoming_hbm, cache_ref, out_ref, query_buf, sems, *, scale
+):
     slot_count = cache_ref.shape[0]
-    rows = incoming_ref.shape[1]
+    rows = incoming_hbm.shape[1]
+    copies = [
+        pltpu.make_async_copy(incoming_hbm.at[home_ref[i]], query_buf.at[i], sems.at[i])
+        for i in range(slot_count)
+    ]
+    for copy in copies:
+        copy.start()
     out_ref[...] = jnp.zeros(out_ref.shape, out_ref.dtype)
     for i in range(slot_count):
         home = home_ref[i]
+        copies[i].wait()
         scores = (
             lax.dot_general(
-                incoming_ref[home],
+                query_buf[i],
                 cache_ref[i, 0],
                 (((1,), (1,)), ((), ())),
                 preferred_element_type=jnp.float32,
@@ -66,10 +75,14 @@
         in_specs=[
             pl.BlockSpec(memory_space=pltpu.SMEM),
             pl.BlockSpec(memory_space=pltpu.SMEM),
-            pl.BlockSpec(memory_space=pltpu.VMEM),
+            pl.BlockSpec(memory_space=pl.ANY),
             pl.BlockSpec(memory_space=pltpu.VMEM),
         ],
         out_specs=pl.BlockSpec(memory_space=pltpu.VMEM),
+        scratch_shapes=[
+            pltpu.VMEM((slot_count, rows, width), incoming.dtype),
+            pltpu.SemaphoreType.DMA((slot_count,)),
+        ],
         cost_estimate=pl.CostEstimate(
             flops=flops, transcendentals=slot_count * rows * cache_size, bytes_accessed=moved
         ),

time: 78.5 us -> 79.4 us (1.011)
  Pallas kernels: 3.3 us -> 4.14 us
    pallas_call x1, Pallas kernels: 3.3 us -> 4.14 us  [slot_attention(): pl.pallas_call(functools.partial(slot_attention_kernel, scale=scale), out...]
where the time goes in v13:
time: 79.4 us; the launch traced here: 78.9 us
  waiting for transfers between devices  30.4 us (38%)
  starting transfers between devices  30.2 us (38%)
  other arithmetic  6.68 us (8%)
  Pallas kernels  4.14 us (5%)
  matrix products  3.92 us (5%)
  local copies, waits for them, and re-layouts  3.19 us (4%)
    all_to_all x1, waiting for transfers between devices, on_device(): back = lax.all_to_all(returning, 'grp', 0, 0, tiled=True)  17.4 us
    all_to_all x1, starting transfers between devices, on_device(): incoming = lax.all_to_all(outgoing, 'grp', 0, 0, tiled=True)  17.2 us
    all_to_all x1, waiting for transfers between devices, on_device(): incoming = lax.all_to_all(outgoing, 'grp', 0, 0, tiled=True)  13 us
    all_to_all x1, starting transfers between devices, on_device(): lax.all_to_all(jnp.broadcast_to(acc_part[None], (model_count,) + acc_part...  6.66 us
    all_to_all x1, starting transfers between devices, on_device(): back = lax.all_to_all(returning, 'grp', 0, 0, tiled=True)  6.41 us
    pallas_call x1, Pallas kernels, slot_attention(): pl.pallas_call(functools.partial(slot_attention_kernel, scale=scale), out...  4.14 us
  transfers between devices with their start and end apart: 3, of which 2 were waited for; matrix products, arithmetic and copies ran while one was open for 9% of the time, Pallas kernels for 0%

profile of v13, /device:TPU:1, one launch (start us, length us, event | category | flops | bytes accessed | tf_op | source)
XLA Modules:
  0.0 78.9 jit_solution(8903841597456332234)
XLA Ops:
  0.0 1.1 %convolution_convert_fusion.1 = bf16[2,8,256]{2,1,0:T(8,128)(2,1)S(1)} fusion(bf16[2,32,256]{2,1,0:T(8,128)(2,1)} %param.10, s32[2,8]{1,0:T(2,128)} %param.16), kind=kOutput, calls=%fused_computation.11 | convolution fusion | flops 266752 | bytes 41024 | tf_op jit(solution)/shard_map/rat,rtd->rad/dot_general | solution.py:118
  1.1 0.6 broadcast_in_dim.227
  1.7 6.7 %all-to-all-start = ((bf16[8,2,8,256]{3,2,1,0:T(8,128)(2,1)}), bf16[8,2,8,256]{3,2,1,0:T(8,128)(2,1)S(1)}, u32[]{:S(2)}, u32[]{:S(2)}) async-start(bf16[8,2,8,256]{3,2,1,0:T(8,128)(2,1)} %broadcast_in_dim.227), calls=%async_computation | async-start | bytes 131072 | tf_op jit(solution)/shard_map/all_to_all | solution.py:135
  8.4 0.8 iota_compare_fusion.1
  9.2 1.0 %and_reduce_fusion = pred[2,8]{1,0:T(4,128)(4,1)S(1)} fusion(s32[2,8]{1,0:T(2,128)} %param.16, pred[8,8]{1,0:T(8,128)(4,1)S(1)} %iota_compare_fusion.2), kind=kLoop, calls=%fused_computation.47 | loop fusion | flops 368 | bytes 144 | tf_op jit(solution)/shard_map/reduce_or | solution.py:128
  10.1 0.8 %select_reduce_fusion.3 = s32[2,8,2]{1,2,0:T(2,128)S(1)} fusion(s32[2,32,2]{1,2,0:T(2,128)} %param.14, pred[2,8,32]{2,1,0:T(8,128)(4,1)S(1)} %iota_compare_fusion.1), kind=kLoop, calls=%fused_computation.43 | loop fusion | flops 2016 | bytes 1152 | tf_op jit(solution)/shard_map/reduce_sum | solution.py:124
  11.0 0.9 %select_reduce_fusion = s32[2,8,32]{2,1,0:T(8,128)S(1)} fusion(s32[2,32,32]{2,1,0:T(8,128)} %param.15, pred[2,8,32]{2,1,0:T(8,128)(4,1)S(1)} %iota_compare_fusion.1), kind=kLoop, calls=%fused_computation.20 | loop fusion | flops 32256 | bytes 10752 | tf_op jit(solution)/shard_map/reduce_sum | solution.py:125
  11.9 0.3 select_reduce_fusion.2
  12.2 0.8 %reshape.173 = s32[64,3]{1,0:T(8,128)S(1)} reshape(s32[192]{0:T(256)} %param.19) | data formatting | bytes 1536 | tf_op jit(solution)/shard_map/reshape | solution.py:167
  13.8 0.4 fusion.1
  14.3 0.9 %select_select_fusion = bf16[64,16,128]{2,1,0:T(8,128)(2,1)} fusion(pred[64]{0:T(512)(128)(4,1)S(1)} %broadcast_compare_fusion, pred[64]{0:T(512)(128)(4,1)S(1)} %get-tuple-element.9, bf16[16,128]{1,0:T(8,128)(2,1)S(1)} %bitcast.66, bf16[16,128]{1,0:T(8,128)(2,1)S(1)} %bitcast.65), kind=kLoop, calls=%fused_computation.19 | loop fusion | flops 262144 | bytes 270464 | tf_op jit(solution)/shard_map/jit(_where)/select_n | solution.py:174
  15.2 17.2 %all-to-all-start.1 = ((bf16[64,16,128]{2,1,0:T(8,128)(2,1)}), bf16[64,16,128]{2,1,0:T(8,128)(2,1)S(1)}, u32[]{:S(2)}, u32[]{:S(2)}) async-start(bf16[64,16,128]{2,1,0:T(8,128)(2,1)} %select_select_fusion), calls=%async_computation.1 | async-start | bytes 524288 | tf_op jit(solution)/shard_map/all_to_all | solution.py:179
  32.4 0.6 and_select_fusion.home_ref
  33.2 13.0 %all-to-all-done.1.incoming_hbm = bf16[64,16,128]{2,1,0:T(8,128)(2,1)S(1)} async-done(((bf16[64,16,128]{2,1,0:T(8,128)(2,1)}), bf16[64,16,128]{2,1,0:T(8,128)(2,1)S(1)}, u32[]{:S(2)}, u32[]{:S(2)}) %all-to-all-start.1) | async-done | bytes 262176 | tf_op jit(solution)/shard_map/all_to_all | solution.py:179
  46.2 0.7 copy-done.1
  46.9 4.1 %shard_map.100 = bf16[64,32,128]{2,1,0:T(8,128)(2,1)} custom-call(s32[3]{0:T(128)} %and_select_fusion.home_ref, s32[3]{0:T(128)} %len_ref.1, bf16[64,16,128]{2,1,0:T(8,128)(2,1)} %copy-done.1, bf16[3,2,1024,128]{3,2,1,0:T(8,128)(2,1)} %cache_ref.1), custom_call_target="tpu_custom_call" | custom-call | flops 25165824 | bytes 2359296 | tf_op jit(solution)/shard_map/pallas_call | solution.py:72
  51.1 6.4 %all-to-all-start.2 = ((bf16[64,32,128]{2,1,0:T(8,128)(2,1)}), bf16[64,32,128]{2,1,0:T(8,128)(2,1)}, u32[]{:S(2)}, u32[]{:S(2)}) async-start(bf16[64,32,128]{2,1,0:T(8,128)(2,1)} %shard_map.100), calls=%async_computation.2 | async-start | bytes 1048576 | tf_op jit(solution)/shard_map/all_to_all | solution.py:184
  57.5 0.5 fusion.18
  58.1 0.2 convolution_convert_fusion
  58.6 17.4 %all-to-all-done.2 = bf16[64,32,128]{2,1,0:T(8,128)(2,1)} async-done(((bf16[64,32,128]{2,1,0:T(8,128)(2,1)}), bf16[64,32,128]{2,1,0:T(8,128)(2,1)}, u32[]{:S(2)}, u32[]{:S(2)}) %all-to-all-start.2) | async-done | bytes 524320 | tf_op jit(solution)/shard_map/all_to_all | solution.py:184
  76.1 1.3 %fusion.11 = f32[3,32,128]{2,0,1:T(4,128)S(1)} fusion(s32[64]{0:T(128)S(1)} %add_reduce_fusion, pred[64]{0:T(512)(128)(4,1)S(1)} %get-tuple-element.9, bf16[8,8,32,128]{3,2,1,0:T(8,128)(2,1)} %bitcast.27), kind=kOutput, calls=%fused_computation.16 | convolution fusion | flops 1573248 | bytes 573760 | tf_op jit(solution)/shard_map/kd,dx->kx/dot_general | solution.py:195
  77.3 0.2 fusion.17
  78.0 0.2 fusion.7
  78.2 0.6 copy.58
  (43 shorter events, 1.8 us)
Async XLA Ops:
  0.0 13.8 %copy-start = (bf16[4,2048,128]{2,1,0:T(8,128)(2,1)S(1)}, bf16[4,2048,128]{2,1,0:T(8,128)(2,1)}, u32[]{:S(2)}) copy-start(bf16[4,2048,128]{2,1,0:T(8,128)(2,1)} %param.11) | copy-start | bytes 6291460
  0.0 32.4 %copy-start.4 = (s32[192]{0:T(256)S(1)}, s32[192]{0:T(256)}, u32[]{:S(2)}) copy-start(s32[192]{0:T(256)} %param.19) | copy-start | bytes 2308
  1.7 12.0 %all-to-all-start = ((bf16[8,2,8,256]{3,2,1,0:T(8,128)(2,1)}), bf16[8,2,8,256]{3,2,1,0:T(8,128)(2,1)S(1)}, u32[]{:S(2)}, u32[]{:S(2)}) async-start(bf16[8,2,8,256]{3,2,1,0:T(8,128)(2,1)} %broadcast_in_dim.227), calls=%async_computation | async-start | bytes 131072 | tf_op jit(solution)/shard_map/all_to_all | solution.py:135
  14.3 43.2 %copy-start.3 = (f32[2048,4]{0,1:T(4,128)S(1)}, f32[2048,4]{0,1:T(4,128)}, u32[]{:S(2)}) copy-start(f32[2048,4]{0,1:T(4,128)} %param.13) | copy-start | bytes 98308
  14.3 43.8 %copy-start.2 = (bf16[2,2048,128]{2,1,0:T(8,128)(2,1)S(1)}, bf16[2,2048,128]{2,1,0:T(8,128)(2,1)}, u32[]{:S(2)}) copy-start(bf16[2,2048,128]{2,1,0:T(8,128)(2,1)} %param.12) | copy-start | bytes 3145732
  15.2 31.0 %all-to-all-start.1 = ((bf16[64,16,128]{2,1,0:T(8,128)(2,1)}), bf16[64,16,128]{2,1,0:T(8,128)(2,1)S(1)}, u32[]{:S(2)}, u32[]{:S(2)}) async-start(bf16[64,16,128]{2,1,0:T(8,128)(2,1)} %select_select_fusion), calls=%async_computation.1 | async-start | bytes 524288 | tf_op jit(solution)/shard_map/all_to_all | solution.py:179
  46.2 0.7 copy-start.1
  51.1 25.0 %all-to-all-start.2 = ((bf16[64,32,128]{2,1,0:T(8,128)(2,1)}), bf16[64,32,128]{2,1,0:T(8,128)(2,1)}, u32[]{:S(2)}, u32[]{:S(2)}) async-start(bf16[64,32,128]{2,1,0:T(8,128)(2,1)} %shard_map.100), calls=%async_computation.2 | async-start | bytes 1048576 | tf_op jit(solution)/shard_map/all_to_all | solution.py:184

commit v14 on v11

--- a/solution.py
+++ b/solution.py
@@ -19,12 +19,25 @@
     return (peak_score, denominator, numerator)
 
 
-def slot_attention_kernel(home_ref, len_ref, incoming_ref, cache_ref, out_ref, *, scale):
+def slot_attention_kernel(
+    home_ref, len_ref, incoming_ref, cache_hbm, out_ref, cache_ref, sems, *, scale
+):
     slot_count = cache_ref.shape[0]
     rows = incoming_ref.shape[1]
+    copies = [
+        [
+            pltpu.make_async_copy(cache_hbm.at[i, c], cache_ref.at[i, c], sems.at[i, c])
+            for c in range(2)
+        ]
+        for i in range(slot_count)
+    ]
+    for pair in copies:
+        for copy in pair:
+            copy.start()
     out_ref[...] = jnp.zeros(out_ref.shape, out_ref.dtype)
     for i in range(slot_count):
         home = home_ref[i]
+        copies[i][0].wait()
         scores = (
             lax.dot_general(
                 incoming_ref[home],
@@ -39,6 +52,7 @@
         peak = jnp.max(masked, axis=1, keepdims=True)
         weights = jnp.exp(masked - peak).astype(jnp.bfloat16)
         den = jnp.sum(weights.astype(jnp.float32), axis=1, keepdims=True)
+        copies[i][1].wait()
         num = jnp.dot(weights, cache_ref[i, 1], preferred_element_type=jnp.float32)
         peak_low = peak.astype(jnp.bfloat16).astype(jnp.float32)
         shift = jnp.exp(peak - peak_low)
@@ -67,9 +81,13 @@
             pl.BlockSpec(memory_space=pltpu.SMEM),
             pl.BlockSpec(memory_space=pltpu.SMEM),
             pl.BlockSpec(memory_space=pltpu.VMEM),
-            pl.BlockSpec(memory_space=pltpu.VMEM),
+            pl.BlockSpec(memory_space=pl.ANY),
         ],
         out_specs=pl.BlockSpec(memory_space=pltpu.VMEM),
+        scratch_shapes=[
+            pltpu.VMEM(cache_kv.shape, cache_kv.dtype),
+            pltpu.SemaphoreType.DMA((slot_count, 2)),
+        ],
         cost_estimate=pl.CostEstimate(
             flops=flops, transcendentals=slot_count * rows * cache_size, bytes_accessed=moved
         ),

time: 78.5 us -> 79.6 us (1.014)
  Pallas kernels: 3.3 us -> 4.3 us
    pallas_call x1, Pallas kernels: 3.3 us -> 4.3 us  [slot_attention(): pl.pallas_call(functools.partial(slot_attention_kernel, scale=scale), out...]
where the time goes in v14:
time: 79.6 us; the launch traced here: 79 us
  waiting for transfers between devices  30.4 us (38%)
  starting transfers between devices  30.2 us (38%)
  other arithmetic  6.68 us (8%)
  Pallas kernels  4.3 us (5%)
  matrix products  3.92 us (5%)
  local copies, waits for them, and re-layouts  3.19 us (4%)
    all_to_all x1, waiting for transfers between devices, on_device(): back = lax.all_to_all(returning, 'grp', 0, 0, tiled=True)  17.4 us
    all_to_all x1, starting transfers between devices, on_device(): incoming = lax.all_to_all(outgoing, 'grp', 0, 0, tiled=True)  17.2 us
    all_to_all x1, waiting for transfers between devices, on_device(): incoming = lax.all_to_all(outgoing, 'grp', 0, 0, tiled=True)  13 us
    all_to_all x1, starting transfers between devices, on_device(): lax.all_to_all(jnp.broadcast_to(acc_part[None], (model_count,) + acc_part...  6.66 us
    all_to_all x1, starting transfers between devices, on_device(): back = lax.all_to_all(returning, 'grp', 0, 0, tiled=True)  6.41 us
    pallas_call x1, Pallas kernels, slot_attention(): pl.pallas_call(functools.partial(slot_attention_kernel, scale=scale), out...  4.3 us
  transfers between devices with their start and end apart: 3, of which 2 were waited for; matrix products, arithmetic and copies ran while one was open for 9% of the time, Pallas kernels for 0%

profile of v14, /device:TPU:1, one launch (start us, length us, event | category | flops | bytes accessed | tf_op | source)
XLA Modules:
  0.0 79.0 jit_solution(3591157888181060351)
XLA Ops:
  0.0 1.1 %convolution_convert_fusion.1 = bf16[2,8,256]{2,1,0:T(8,128)(2,1)S(1)} fusion(bf16[2,32,256]{2,1,0:T(8,128)(2,1)} %param.10, s32[2,8]{1,0:T(2,128)} %param.16), kind=kOutput, calls=%fused_computation.11 | convolution fusion | flops 266752 | bytes 41024 | tf_op jit(solution)/shard_map/rat,rtd->rad/dot_general | solution.py:123
  1.1 0.6 broadcast_in_dim.227
  1.7 6.7 %all-to-all-start = ((bf16[8,2,8,256]{3,2,1,0:T(8,128)(2,1)}), bf16[8,2,8,256]{3,2,1,0:T(8,128)(2,1)S(1)}, u32[]{:S(2)}, u32[]{:S(2)}) async-start(bf16[8,2,8,256]{3,2,1,0:T(8,128)(2,1)} %broadcast_in_dim.227), calls=%async_computation | async-start | bytes 131072 | tf_op jit(solution)/shard_map/all_to_all | solution.py:140
  8.4 0.8 iota_compare_fusion.1
  9.2 1.0 %and_reduce_fusion = pred[2,8]{1,0:T(4,128)(4,1)S(1)} fusion(s32[2,8]{1,0:T(2,128)} %param.16, pred[8,8]{1,0:T(8,128)(4,1)S(1)} %iota_compare_fusion.2), kind=kLoop, calls=%fused_computation.47 | loop fusion | flops 368 | bytes 144 | tf_op jit(solution)/shard_map/reduce_or | solution.py:133
  10.1 0.8 %select_reduce_fusion.3 = s32[2,8,2]{1,2,0:T(2,128)S(1)} fusion(s32[2,32,2]{1,2,0:T(2,128)} %param.14, pred[2,8,32]{2,1,0:T(8,128)(4,1)S(1)} %iota_compare_fusion.1), kind=kLoop, calls=%fused_computation.43 | loop fusion | flops 2016 | bytes 1152 | tf_op jit(solution)/shard_map/reduce_sum | solution.py:129
  11.0 0.9 %select_reduce_fusion = s32[2,8,32]{2,1,0:T(8,128)S(1)} fusion(s32[2,32,32]{2,1,0:T(8,128)} %param.15, pred[2,8,32]{2,1,0:T(8,128)(4,1)S(1)} %iota_compare_fusion.1), kind=kLoop, calls=%fused_computation.20 | loop fusion | flops 32256 | bytes 10752 | tf_op jit(solution)/shard_map/reduce_sum | solution.py:130
  11.9 0.3 select_reduce_fusion.2
  12.2 0.8 %reshape.173 = s32[64,3]{1,0:T(8,128)S(1)} reshape(s32[192]{0:T(256)} %param.19) | data formatting | bytes 1536 | tf_op jit(solution)/shard_map/reshape | solution.py:172
  13.8 0.4 fusion.1
  14.3 0.9 %select_select_fusion = bf16[64,16,128]{2,1,0:T(8,128)(2,1)} fusion(pred[64]{0:T(512)(128)(4,1)S(1)} %broadcast_compare_fusion, pred[64]{0:T(512)(128)(4,1)S(1)} %get-tuple-element.9, bf16[16,128]{1,0:T(8,128)(2,1)S(1)} %bitcast.66, bf16[16,128]{1,0:T(8,128)(2,1)S(1)} %bitcast.65), kind=kLoop, calls=%fused_computation.19 | loop fusion | flops 262144 | bytes 270464 | tf_op jit(solution)/shard_map/jit(_where)/select_n | solution.py:179
  15.2 17.2 %all-to-all-start.1 = ((bf16[64,16,128]{2,1,0:T(8,128)(2,1)}), bf16[64,16,128]{2,1,0:T(8,128)(2,1)S(1)}, u32[]{:S(2)}, u32[]{:S(2)}) async-start(bf16[64,16,128]{2,1,0:T(8,128)(2,1)} %select_select_fusion), calls=%async_computation.1 | async-start | bytes 524288 | tf_op jit(solution)/shard_map/all_to_all | solution.py:184
  32.4 0.6 and_select_fusion.home_ref
  33.2 13.0 %all-to-all-done.1.incoming_ref = bf16[64,16,128]{2,1,0:T(8,128)(2,1)S(1)} async-done(((bf16[64,16,128]{2,1,0:T(8,128)(2,1)}), bf16[64,16,128]{2,1,0:T(8,128)(2,1)S(1)}, u32[]{:S(2)}, u32[]{:S(2)}) %all-to-all-start.1) | async-done | bytes 262176 | tf_op jit(solution)/shard_map/all_to_all | solution.py:184
  46.2 0.7 copy-done.1
  46.9 4.3 %shard_map.100 = bf16[64,32,128]{2,1,0:T(8,128)(2,1)} custom-call(s32[3]{0:T(128)} %and_select_fusion.home_ref, s32[3]{0:T(128)} %len_ref.1, bf16[64,16,128]{2,1,0:T(8,128)(2,1)} %copy-done.1, bf16[3,2,1024,128]{3,2,1,0:T(8,128)(2,1)} %cache_hbm.1), custom_call_target="tpu_custom_call" | custom-call | flops 25165824 | bytes 2359296 | tf_op jit(solution)/shard_map/pallas_call | solution.py:77
  51.3 6.4 %all-to-all-start.2 = ((bf16[64,32,128]{2,1,0:T(8,128)(2,1)}), bf16[64,32,128]{2,1,0:T(8,128)(2,1)}, u32[]{:S(2)}, u32[]{:S(2)}) async-start(bf16[64,32,128]{2,1,0:T(8,128)(2,1)} %shard_map.100), calls=%async_computation.2 | async-start | bytes 1048576 | tf_op jit(solution)/shard_map/all_to_all | solution.py:189
  57.7 0.5 fusion.18
  58.3 0.2 convolution_convert_fusion
  58.8 17.4 %all-to-all-done.2 = bf16[64,32,128]{2,1,0:T(8,128)(2,1)} async-done(((bf16[64,32,128]{2,1,0:T(8,128)(2,1)}), bf16[64,32,128]{2,1,0:T(8,128)(2,1)}, u32[]{:S(2)}, u32[]{:S(2)}) %all-to-all-start.2) | async-done | bytes 524320 | tf_op jit(solution)/shard_map/all_to_all | solution.py:189
  76.2 1.3 %fusion.11 = f32[3,32,128]{2,0,1:T(4,128)S(1)} fusion(s32[64]{0:T(128)S(1)} %add_reduce_fusion, pred[64]{0:T(512)(128)(4,1)S(1)} %get-tuple-element.9, bf16[8,8,32,128]{3,2,1,0:T(8,128)(2,1)} %bitcast.27), kind=kOutput, calls=%fused_computation.16 | convolution fusion | flops 1573248 | bytes 573760 | tf_op jit(solution)/shard_map/kd,dx->kx/dot_general | solution.py:200
  77.5 0.2 fusion.17
  78.2 0.2 fusion.7
  78.4 0.6 copy.58
  (43 shorter events, 1.8 us)
Async XLA Ops:
  0.0 13.8 %copy-start = (bf16[4,2048,128]{2,1,0:T(8,128)(2,1)S(1)}, bf16[4,2048,128]{2,1,0:T(8,128)(2,1)}, u32[]{:S(2)}) copy-start(bf16[4,2048,128]{2,1,0:T(8,128)(2,1)} %param.11) | copy-start | bytes 6291460
  0.0 32.4 %copy-start.4 = (s32[192]{0:T(256)S(1)}, s32[192]{0:T(256)}, u32[]{:S(2)}) copy-start(s32[192]{0:T(256)} %param.19) | copy-start | bytes 2308
  1.7 12.0 %all-to-all-start = ((bf16[8,2,8,256]{3,2,1,0:T(8,128)(2,1)}), bf16[8,2,8,256]{3,2,1,0:T(8,128)(2,1)S(1)}, u32[]{:S(2)}, u32[]{:S(2)}) async-start(bf16[8,2,8,256]{3,2,1,0:T(8,128)(2,1)} %broadcast_in_dim.227), calls=%async_computation | async-start | bytes 131072 | tf_op jit(solution)/shard_map/all_to_all | solution.py:140
  14.3 43.4 %copy-start.3 = (f32[2048,4]{0,1:T(4,128)S(1)}, f32[2048,4]{0,1:T(4,128)}, u32[]{:S(2)}) copy-start(f32[2048,4]{0,1:T(4,128)} %param.13) | copy-start | bytes 98308
  14.3 44.0 %copy-start.2 = (bf16[2,2048,128]{2,1,0:T(8,128)(2,1)S(1)}, bf16[2,2048,128]{2,1,0:T(8,128)(2,1)}, u32[]{:S(2)}) copy-start(bf16[2,2048,128]{2,1,0:T(8,128)(2,1)} %param.12) | copy-start | bytes 3145732
  15.2 31.0 %all-to-all-start.1 = ((bf16[64,16,128]{2,1,0:T(8,128)(2,1)}), bf16[64,16,128]{2,1,0:T(8,128)(2,1)S(1)}, u32[]{:S(2)}, u32[]{:S(2)}) async-start(bf16[64,16,128]{2,1,0:T(8,128)(2,1)} %select_select_fusion), calls=%async_computation.1 | async-start | bytes 524288 | tf_op jit(solution)/shard_map/all_to_all | solution.py:184
  46.2 0.7 copy-start.1
  51.3 25.0 %all-to-all-start.2 = ((bf16[64,32,128]{2,1,0:T(8,128)(2,1)}), bf16[64,32,128]{2,1,0:T(8,128)(2,1)}, u32[]{:S(2)}, u32[]{:S(2)}) async-start(bf16[64,32,128]{2,1,0:T(8,128)(2,1)} %shard_map.100), calls=%async_computation.2 | async-start | bytes 1048576 | tf_op jit(solution)/shard_map/all_to_all | solution.py:189

commit v15 on v11

--- a/solution.py
+++ b/solution.py
@@ -169,7 +169,10 @@
     row_count = kept_rows * topk_count
     returning = slot_attention(my_slots // requests, cache_len, incoming, cache_kv, score_scale)
     back = lax.all_to_all(returning, "grp", 0, 0, tiled=True)
-    serving = jnp.any(home_of == group_idx, axis=1)
+    late_home, late_local, _ = lax.optimization_barrier((home_of, local_of, returning))
+    mine = late_home == group_idx
+    local_of = late_local
+    serving = jnp.any(mine, axis=1)
     place = jnp.cumsum(serving.astype(jnp.int32)) - 1
     source_pick = serving[None, :] & (
         place[None, :] == jnp.arange(slot_count, dtype=jnp.int32)[:, None]
@@ -178,15 +181,12 @@
     source_request = jnp.sum(
         jnp.where(source_pick, jnp.sum(jnp.where(mine, local_of, 0), axis=1)[None, :], 0), axis=1
     )
-    chosen_blocks = (
-        jnp.einsum(
-            "kd,dx->kx",
-            source_pick.astype(back.dtype),
-            back.reshape(group_count, -1),
-            preferred_element_type=jnp.float32,
-        )
-        .reshape(slot_count, 2 * row_count, head_width)
-    )
+    source_index = jnp.sum(
+        jnp.where(source_pick, jnp.arange(group_count, dtype=jnp.int32)[None, :], 0), axis=1
+    )
+    chosen_blocks = jnp.stack(
+        [lax.dynamic_index_in_dim(back, source_index[k], 0, keepdims=False) for k in range(slot_count)]
+    ).astype(jnp.float32)
     back_num = chosen_blocks[:, :row_count].reshape(slot_count, kept_rows, topk_count, head_width)
     back_facts = chosen_blocks[:, row_count:, :3]
     back_peak = back_facts[..., 0].reshape(slot_count, kept_rows, topk_count)

time: 78.5 us -> 80.5 us (1.025)
  between operations: 0.23 us -> 5.92 us
  waiting for transfers between devices: 30.4 us -> 25.1 us
  other arithmetic: 6.68 us -> 7.6 us
  starting transfers between devices: 30.2 us -> 29.3 us
  local copies, waits for them, and re-layouts: 3.19 us -> 4.01 us
    all_to_all x1, waiting for transfers between devices: 17.4 us -> 11.5 us  [on_device(): back = lax.all_to_all(returning, 'grp', 0, 0, tiled=True)]
    dot_general x1 -> x0, matrix products: 1.3 us -> none  [on_device(): jnp.einsum('kd,dx->kx', source_pick.astype(back.dtype), back.reshape(grou...]
    dot_general x1, matrix products: 0.25 us -> 1.47 us  [on_device(): jnp.einsum('rtd,cdw->rtcw', acc_hidden, kv_weight, preferred_element_type...]
    all_to_all x1, starting transfers between devices: 17.2 us -> 16.2 us  [on_device(): incoming = lax.all_to_all(outgoing, 'grp', 0, 0, tiled=True)]
  transfers between devices with their start and end apart: 3 -> 3, of which waited for: 2 -> 2; matrix products, arithmetic and copies ran while one was open for 9% -> 10% of each run, Pallas kernels for 0% -> 0%
where the time goes in v15:
time: 80.5 us; the launch traced here: 79.8 us
  starting transfers between devices  29.3 us (36%)
  waiting for transfers between devices  25.1 us (31%)
  other arithmetic  7.6 us (9%)
  between operations  5.92 us (7%)
  matrix products  4.6 us (6%)
  local copies, waits for them, and re-layouts  4.01 us (5%)
  Pallas kernels  3.3 us (4%)
    all_to_all x1, starting transfers between devices, on_device(): incoming = lax.all_to_all(outgoing, 'grp', 0, 0, tiled=True)  16.2 us
    all_to_all x1, waiting for transfers between devices, on_device(): incoming = lax.all_to_all(outgoing, 'grp', 0, 0, tiled=True)  13.6 us
    all_to_all x1, waiting for transfers between devices, on_device(): back = lax.all_to_all(returning, 'grp', 0, 0, tiled=True)  11.5 us
    all_to_all x1, starting transfers between devices, on_device(): lax.all_to_all(jnp.broadcast_to(acc_part[None], (model_count,) + acc_part...  6.66 us
    all_to_all x1, starting transfers between devices, on_device(): back = lax.all_to_all(returning, 'grp', 0, 0, tiled=True)  6.39 us
    pallas_call x1, Pallas kernels, slot_attention(): pl.pallas_call(functools.partial(slot_attention_kernel, scale=scale), out...  3.3 us
  transfers between devices with their start and end apart: 3, of which 2 were waited for; matrix products, arithmetic and copies ran while one was open for 10% of the time, Pallas kernels for 0%

profile of v15, /device:TPU:1, one launch (start us, length us, event | category | flops | bytes accessed | tf_op | source)
XLA Modules:
  0.0 79.8 jit_solution(6192803499114386321)
XLA Ops:
  0.0 1.1 %convolution_convert_fusion.1 = bf16[2,8,256]{2,1,0:T(8,128)(2,1)S(1)} fusion(bf16[2,32,256]{2,1,0:T(8,128)(2,1)} %param.10, s32[2,8]{1,0:T(2,128)} %param.16), kind=kOutput, calls=%fused_computation.11 | convolution fusion | flops 266752 | bytes 41024 | tf_op jit(solution)/shard_map/rat,rtd->rad/dot_general | solution.py:105
  1.1 0.6 broadcast_in_dim.234
  1.7 6.7 %all-to-all-start = ((bf16[8,2,8,256]{3,2,1,0:T(8,128)(2,1)}), bf16[8,2,8,256]{3,2,1,0:T(8,128)(2,1)S(1)}, u32[]{:S(2)}, u32[]{:S(2)}) async-start(bf16[8,2,8,256]{3,2,1,0:T(8,128)(2,1)} %broadcast_in_dim.234), calls=%async_computation | async-start | bytes 131072 | tf_op jit(solution)/shard_map/all_to_all | solution.py:122
  8.4 0.8 iota_compare_fusion.1
  9.2 1.0 %and_reduce_fusion = pred[2,8]{1,0:T(4,128)(4,1)S(1)} fusion(s32[2,8]{1,0:T(2,128)} %param.16, pred[8,8]{1,0:T(8,128)(4,1)S(1)} %iota_compare_fusion.2), kind=kLoop, calls=%fused_computation.45 | loop fusion | flops 368 | bytes 144 | tf_op jit(solution)/shard_map/reduce_or | solution.py:115
  10.1 0.8 %select_reduce_fusion.5 = s32[2,8,2]{1,2,0:T(2,128)S(1)} fusion(s32[2,32,2]{1,2,0:T(2,128)} %param.14, pred[2,8,32]{2,1,0:T(8,128)(4,1)S(1)} %iota_compare_fusion.1), kind=kLoop, calls=%fused_computation.41 | loop fusion | flops 2016 | bytes 1152 | tf_op jit(solution)/shard_map/reduce_sum | solution.py:111
  11.0 0.9 %select_reduce_fusion = s32[2,8,32]{2,1,0:T(8,128)S(1)} fusion(s32[2,32,32]{2,1,0:T(8,128)} %param.15, pred[2,8,32]{2,1,0:T(8,128)(4,1)S(1)} %iota_compare_fusion.1), kind=kLoop, calls=%fused_computation.16 | loop fusion | flops 32256 | bytes 10752 | tf_op jit(solution)/shard_map/reduce_sum | solution.py:112
  11.9 0.3 select_reduce_fusion.2
  12.2 0.8 %reshape.168 = s32[64,3]{1,0:T(8,128)S(1)} reshape(s32[192]{0:T(256)} %param.19) | data formatting | bytes 1536 | tf_op jit(solution)/shard_map/reshape | solution.py:154
  13.4 1.3 %and_select_fusion.home_ref = s32[3]{0:T(128)} fusion(s32[192]{0:T(256)} %param.19, s32[]{:T(128)S(6)} %select_n.92), kind=kLoop, calls=%fused_computation.61 | loop fusion | flops 45 | bytes 28 | tf_op jit(solution)/shard_map/jit(floor_divide)/jit(_where)/select_n | solution.py:170
  14.7 1.3 %fusion.11 = f32[2,8,4]{1,2,0:T(4,128)S(1)} fusion(bf16[2,8,2048]{2,1,0:T(8,128)(2,1)S(1)} %bitcast.43, f32[2048,4]{0,1:T(4,128)} %param.13), kind=kOutput, calls=%fused_computation.25 | convolution fusion | flops 1572864 | bytes 98560 | tf_op jit(solution)/shard_map/rad,de->rae/dot_general | solution.py:135
  16.0 1.5 %convolution_convert_fusion = bf16[2,8,2,128]{3,1,2,0:T(8,128)(2,1)S(1)} fusion(bf16[2,8,2048,1]{2,1,3,0:T(8,128)(2,1)S(1)} %bitcast.44, bf16[2,2048,128]{2,1,0:T(8,128)(2,1)} %param.12), kind=kOutput, calls=%fused_computation.10 | convolution fusion | flops 16781312 | bytes 1122304 | tf_op jit(solution)/shard_map/rtd,cdw->rtcw/dot_general | solution.py:134
  17.5 0.4 fusion.1
  18.0 0.9 %select_select_fusion = bf16[64,16,128]{2,1,0:T(8,128)(2,1)} fusion(pred[64]{0:T(512)(128)(4,1)S(1)} %broadcast_compare_fusion.2, pred[64]{0:T(512)(128)(4,1)S(1)} %get-tuple-element.19, bf16[16,128]{1,0:T(8,128)(2,1)S(1)} %bitcast.49, bf16[16,128]{1,0:T(8,128)(2,1)S(1)} %bitcast.48), kind=kLoop, calls=%fused_computation.15 | loop fusion | flops 262144 | bytes 270464 | tf_op jit(solution)/shard_map/jit(_where)/select_n | solution.py:161
  18.9 16.2 %all-to-all-start.1 = ((bf16[64,16,128]{2,1,0:T(8,128)(2,1)}), bf16[64,16,128]{2,1,0:T(8,128)(2,1)S(1)}, u32[]{:S(2)}, u32[]{:S(2)}) async-start(bf16[64,16,128]{2,1,0:T(8,128)(2,1)} %select_select_fusion), calls=%async_computation.1 | async-start | bytes 524288 | tf_op jit(solution)/shard_map/all_to_all | solution.py:166
  35.2 0.2 fusion.23
  35.4 13.6 %all-to-all-done.1.incoming_ref = bf16[64,16,128]{2,1,0:T(8,128)(2,1)S(1)} async-done(((bf16[64,16,128]{2,1,0:T(8,128)(2,1)}), bf16[64,16,128]{2,1,0:T(8,128)(2,1)S(1)}, u32[]{:S(2)}, u32[]{:S(2)}) %all-to-all-start.1) | async-done | bytes 262176 | tf_op jit(solution)/shard_map/all_to_all | solution.py:166
  49.0 0.7 copy-done.1
  49.7 3.3 %shard_map.100 = bf16[64,32,128]{2,1,0:T(8,128)(2,1)} custom-call(s32[3]{0:T(128)} %and_select_fusion.home_ref, s32[3]{0:T(128)} %len_ref.1, bf16[64,16,128]{2,1,0:T(8,128)(2,1)} %copy-done.1, bf16[3,2,1024,128]{3,2,1,0:T(8,128)(2,1)} %cache_ref.1), custom_call_target="tpu_custom_call" | custom-call | flops 25165824 | bytes 2359296 | tf_op jit(solution)/shard_map/pallas_call | solution.py:63
  53.0 6.4 %all-to-all-start.2 = ((bf16[64,32,128]{2,1,0:T(8,128)(2,1)}), bf16[64,32,128]{2,1,0:T(8,128)(2,1)S(1)}, u32[]{:S(2)}, u32[]{:S(2)}) async-start(bf16[64,32,128]{2,1,0:T(8,128)(2,1)} %shard_map.100), calls=%async_computation.2 | async-start | bytes 1048576 | tf_op jit(solution)/shard_map/all_to_all | solution.py:171
  60.3 0.7 fusion.22
  66.7 11.5 %all-to-all-done.2 = bf16[64,32,128]{2,1,0:T(8,128)(2,1)S(1)} async-done(((bf16[64,32,128]{2,1,0:T(8,128)(2,1)}), bf16[64,32,128]{2,1,0:T(8,128)(2,1)S(1)}, u32[]{:S(2)}, u32[]{:S(2)}) %all-to-all-start.2) | async-done | bytes 524320 | tf_op jit(solution)/shard_map/all_to_all | solution.py:171
  79.0 0.2 fusion.7
  79.2 0.6 copy.44
  (43 shorter events, 2.2 us)
Async XLA Ops:
  0.0 17.5 %copy-start = (bf16[4,2048,128]{2,1,0:T(8,128)(2,1)S(1)}, bf16[4,2048,128]{2,1,0:T(8,128)(2,1)}, u32[]{:S(2)}) copy-start(bf16[4,2048,128]{2,1,0:T(8,128)(2,1)} %param.11) | copy-start | bytes 6291460
  1.7 13.0 %all-to-all-start = ((bf16[8,2,8,256]{3,2,1,0:T(8,128)(2,1)}), bf16[8,2,8,256]{3,2,1,0:T(8,128)(2,1)S(1)}, u32[]{:S(2)}, u32[]{:S(2)}) async-start(bf16[8,2,8,256]{3,2,1,0:T(8,128)(2,1)} %broadcast_in_dim.234), calls=%async_computation | async-start | bytes 131072 | tf_op jit(solution)/shard_map/all_to_all | solution.py:122
  18.9 30.1 %all-to-all-start.1 = ((bf16[64,16,128]{2,1,0:T(8,128)(2,1)}), bf16[64,16,128]{2,1,0:T(8,128)(2,1)S(1)}, u32[]{:S(2)}, u32[]{:S(2)}) async-start(bf16[64,16,128]{2,1,0:T(8,128)(2,1)} %select_select_fusion), calls=%async_computation.1 | async-start | bytes 524288 | tf_op jit(solution)/shard_map/all_to_all | solution.py:166
  49.0 0.7 copy-start.1
  53.0 25.1 %all-to-all-start.2 = ((bf16[64,32,128]{2,1,0:T(8,128)(2,1)}), bf16[64,32,128]{2,1,0:T(8,128)(2,1)S(1)}, u32[]{:S(2)}, u32[]{:S(2)}) async-start(bf16[64,32,128]{2,1,0:T(8,128)(2,1)} %shard_map.100), calls=%async_computation.2 | async-start | bytes 1048576 | tf_op jit(solution)/shard_map/all_to_all | solution.py:171

commit v16 on v11

--- a/solution.py
+++ b/solution.py
@@ -70,6 +70,7 @@
             pl.BlockSpec(memory_space=pltpu.VMEM),
         ],
         out_specs=pl.BlockSpec(memory_space=pltpu.VMEM),
+        compiler_params=pltpu.CompilerParams(vmem_limit_bytes=16 * 1024 * 1024),
         cost_estimate=pl.CostEstimate(
             flops=flops, transcendentals=slot_count * rows * cache_size, bytes_accessed=moved
         ),

time: 78.5 us -> 78.3 us (level)
  Pallas kernels: 3.3 us -> 2.35 us
    pallas_call x1, Pallas kernels: 3.3 us -> 2.35 us  [slot_attention(): pl.pallas_call(functools.partial(slot_attention_kernel, scale=scale), out...]
where the time goes in v16:
time: 78.3 us; the launch traced here: 77.8 us
  waiting for transfers between devices  31 us (40%)
  starting transfers between devices  30.2 us (39%)
  other arithmetic  6.17 us (8%)
  matrix products  3.92 us (5%)
  local copies, waits for them, and re-layouts  3.9 us (5%)
  Pallas kernels  2.35 us (3%)
    all_to_all x1, waiting for transfers between devices, on_device(): back = lax.all_to_all(returning, 'grp', 0, 0, tiled=True)  17.4 us
    all_to_all x1, starting transfers between devices, on_device(): incoming = lax.all_to_all(outgoing, 'grp', 0, 0, tiled=True)  17.2 us
    all_to_all x1, waiting for transfers between devices, on_device(): incoming = lax.all_to_all(outgoing, 'grp', 0, 0, tiled=True)  13.5 us
    all_to_all x1, starting transfers between devices, on_device(): lax.all_to_all(jnp.broadcast_to(acc_part[None], (model_count,) + acc_part...  6.66 us
    all_to_all x1, starting transfers between devices, on_device(): back = lax.all_to_all(returning, 'grp', 0, 0, tiled=True)  6.4 us
    pallas_call x1, Pallas kernels, slot_attention(): pl.pallas_call(functools.partial(slot_attention_kernel, scale=scale), out...  2.35 us
  transfers between devices with their start and end apart: 3, of which 2 were waited for; matrix products, arithmetic and copies ran while one was open for 9% of the time, Pallas kernels for 0%

profile of v16, /device:TPU:1, one launch (start us, length us, event | category | flops | bytes accessed | tf_op | source)
XLA Modules:
  0.0 77.8 jit_solution(2822247601771028583)
XLA Ops:
  0.0 1.1 %convolution_convert_fusion.1 = bf16[2,8,256]{2,1,0:T(8,128)(2,1)S(1)} fusion(bf16[2,32,256]{2,1,0:T(8,128)(2,1)} %param.10, s32[2,8]{1,0:T(2,128)} %param.16), kind=kOutput, calls=%fused_computation.11 | convolution fusion | flops 266752 | bytes 41024 | tf_op jit(solution)/shard_map/rat,rtd->rad/dot_general | solution.py:106
  1.1 0.6 broadcast_in_dim.227
  1.7 6.7 %all-to-all-start = ((bf16[8,2,8,256]{3,2,1,0:T(8,128)(2,1)}), bf16[8,2,8,256]{3,2,1,0:T(8,128)(2,1)S(1)}, u32[]{:S(2)}, u32[]{:S(2)}) async-start(bf16[8,2,8,256]{3,2,1,0:T(8,128)(2,1)} %broadcast_in_dim.227), calls=%async_computation | async-start | bytes 131072 | tf_op jit(solution)/shard_map/all_to_all | solution.py:123
  8.4 0.8 iota_compare_fusion.1
  9.2 1.0 %and_reduce_fusion = pred[2,8]{1,0:T(4,128)(4,1)S(1)} fusion(s32[2,8]{1,0:T(2,128)} %param.16, pred[8,8]{1,0:T(8,128)(4,1)S(1)} %iota_compare_fusion.2), kind=kLoop, calls=%fused_computation.47 | loop fusion | flops 368 | bytes 144 | tf_op jit(solution)/shard_map/reduce_or | solution.py:116
  10.1 0.8 %select_reduce_fusion.3 = s32[2,8,2]{1,2,0:T(2,128)S(1)} fusion(s32[2,32,2]{1,2,0:T(2,128)} %param.14, pred[2,8,32]{2,1,0:T(8,128)(4,1)S(1)} %iota_compare_fusion.1), kind=kLoop, calls=%fused_computation.43 | loop fusion | flops 2016 | bytes 1152 | tf_op jit(solution)/shard_map/reduce_sum | solution.py:112
  11.0 0.9 %select_reduce_fusion = s32[2,8,32]{2,1,0:T(8,128)S(1)} fusion(s32[2,32,32]{2,1,0:T(8,128)} %param.15, pred[2,8,32]{2,1,0:T(8,128)(4,1)S(1)} %iota_compare_fusion.1), kind=kLoop, calls=%fused_computation.20 | loop fusion | flops 32256 | bytes 10752 | tf_op jit(solution)/shard_map/reduce_sum | solution.py:113
  11.9 0.3 select_reduce_fusion.2
  12.3 0.8 %reshape.173 = s32[64,3]{1,0:T(8,128)S(1)} reshape(s32[192]{0:T(256)} %param.19) | data formatting | bytes 1536 | tf_op jit(solution)/shard_map/reshape | solution.py:155
  13.8 0.4 fusion.1
  14.3 0.9 %select_select_fusion = bf16[64,16,128]{2,1,0:T(8,128)(2,1)} fusion(pred[64]{0:T(512)(128)(4,1)S(1)} %broadcast_compare_fusion, pred[64]{0:T(512)(128)(4,1)S(1)} %get-tuple-element.9, bf16[16,128]{1,0:T(8,128)(2,1)S(1)} %bitcast.66, bf16[16,128]{1,0:T(8,128)(2,1)S(1)} %bitcast.65), kind=kLoop, calls=%fused_computation.19 | loop fusion | flops 262144 | bytes 270464 | tf_op jit(solution)/shard_map/jit(_where)/select_n | solution.py:162
  15.2 17.2 %all-to-all-start.1 = ((bf16[64,16,128]{2,1,0:T(8,128)(2,1)}), bf16[64,16,128]{2,1,0:T(8,128)(2,1)S(1)}, u32[]{:S(2)}, u32[]{:S(2)}) async-start(bf16[64,16,128]{2,1,0:T(8,128)(2,1)} %select_select_fusion), calls=%async_computation.1 | async-start | bytes 524288 | tf_op jit(solution)/shard_map/all_to_all | solution.py:167
  32.7 13.5 %all-to-all-done.1.incoming_ref = bf16[64,16,128]{2,1,0:T(8,128)(2,1)S(1)} async-done(((bf16[64,16,128]{2,1,0:T(8,128)(2,1)}), bf16[64,16,128]{2,1,0:T(8,128)(2,1)S(1)}, u32[]{:S(2)}, u32[]{:S(2)}) %all-to-all-start.1) | async-done | bytes 262176 | tf_op jit(solution)/shard_map/all_to_all | solution.py:167
  46.2 1.4 %copy-done.1 = bf16[3,2,1024,128]{3,2,1,0:T(8,128)(2,1)S(1)} copy-done((bf16[3,2,1024,128]{3,2,1,0:T(8,128)(2,1)S(1)}, bf16[3,2,1024,128]{3,2,1,0:T(8,128)(2,1)}, u32[]{:S(2)}) %copy-start.1) | copy-done | bytes 1572888
  47.7 2.4 %shard_map.100 = bf16[64,32,128]{2,1,0:T(8,128)(2,1)} custom-call(s32[3]{0:T(128)S(1)} %and_select_fusion.home_ref, s32[3]{0:T(128)S(1)} %copy-done.2, bf16[64,16,128]{2,1,0:T(8,128)(2,1)S(1)} %all-to-all-done.1.incoming_ref, bf16[3,2,1024,128]{3,2,1,0:T(8,128)(2,1)S(1)} %copy-done.1), custom_call_target="tpu_custom_call" | custom-call | flops 25165824 | bytes 2359296 | tf_op jit(solution)/shard_map/pallas_call | solution.py:63
  50.0 6.4 %all-to-all-start.2 = ((bf16[64,32,128]{2,1,0:T(8,128)(2,1)}), bf16[64,32,128]{2,1,0:T(8,128)(2,1)}, u32[]{:S(2)}, u32[]{:S(2)}) async-start(bf16[64,32,128]{2,1,0:T(8,128)(2,1)} %shard_map.100), calls=%async_computation.2 | async-start | bytes 1048576 | tf_op jit(solution)/shard_map/all_to_all | solution.py:172
  56.4 0.5 fusion.18
  57.0 0.2 convolution_convert_fusion
  57.3 0.2 fusion.30
  57.5 17.4 %all-to-all-done.2 = bf16[64,32,128]{2,1,0:T(8,128)(2,1)} async-done(((bf16[64,32,128]{2,1,0:T(8,128)(2,1)}), bf16[64,32,128]{2,1,0:T(8,128)(2,1)}, u32[]{:S(2)}, u32[]{:S(2)}) %all-to-all-start.2) | async-done | bytes 524320 | tf_op jit(solution)/shard_map/all_to_all | solution.py:172
  74.9 1.3 %fusion.11 = f32[3,32,128]{2,0,1:T(4,128)S(1)} fusion(s32[64]{0:T(128)S(1)} %add_reduce_fusion, pred[64]{0:T(512)(128)(4,1)S(1)} %get-tuple-element.9, bf16[8,8,32,128]{3,2,1,0:T(8,128)(2,1)} %bitcast.27), kind=kOutput, calls=%fused_computation.16 | convolution fusion | flops 1573248 | bytes 573760 | tf_op jit(solution)/shard_map/kd,dx->kx/dot_general | solution.py:183
  76.2 0.2 fusion.17
  76.9 0.2 fusion.7
  77.1 0.6 copy.58
  (45 shorter events, 1.7 us)
Async XLA Ops:
  0.0 13.8 %copy-start = (bf16[4,2048,128]{2,1,0:T(8,128)(2,1)S(1)}, bf16[4,2048,128]{2,1,0:T(8,128)(2,1)}, u32[]{:S(2)}) copy-start(bf16[4,2048,128]{2,1,0:T(8,128)(2,1)} %param.11) | copy-start | bytes 6291460
  0.0 32.4 %copy-start.5 = (s32[192]{0:T(256)S(1)}, s32[192]{0:T(256)}, u32[]{:S(2)}) copy-start(s32[192]{0:T(256)} %param.19) | copy-start | bytes 2308
  0.0 46.2 %copy-start.2 = (s32[3]{0:T(128)S(1)}, s32[3]{0:T(128)}, u32[]{:S(2)}) copy-start(s32[3]{0:T(128)} %len_ref.1) | copy-start | bytes 40
  1.7 12.0 %all-to-all-start = ((bf16[8,2,8,256]{3,2,1,0:T(8,128)(2,1)}), bf16[8,2,8,256]{3,2,1,0:T(8,128)(2,1)S(1)}, u32[]{:S(2)}, u32[]{:S(2)}) async-start(bf16[8,2,8,256]{3,2,1,0:T(8,128)(2,1)} %broadcast_in_dim.227), calls=%async_computation | async-start | bytes 131072 | tf_op jit(solution)/shard_map/all_to_all | solution.py:123
  14.3 42.1 %copy-start.4 = (f32[2048,4]{0,1:T(4,128)S(1)}, f32[2048,4]{0,1:T(4,128)}, u32[]{:S(2)}) copy-start(f32[2048,4]{0,1:T(4,128)} %param.13) | copy-start | bytes 98308
  15.2 31.0 %all-to-all-start.1 = ((bf16[64,16,128]{2,1,0:T(8,128)(2,1)}), bf16[64,16,128]{2,1,0:T(8,128)(2,1)S(1)}, u32[]{:S(2)}, u32[]{:S(2)}) async-start(bf16[64,16,128]{2,1,0:T(8,128)(2,1)} %select_select_fusion), calls=%async_computation.1 | async-start | bytes 524288 | tf_op jit(solution)/shard_map/all_to_all | solution.py:167
  46.2 1.4 %copy-start.1 = (bf16[3,2,1024,128]{3,2,1,0:T(8,128)(2,1)S(1)}, bf16[3,2,1024,128]{3,2,1,0:T(8,128)(2,1)}, u32[]{:S(2)}) copy-start(bf16[3,2,1024,128]{3,2,1,0:T(8,128)(2,1)} %cache_ref.1) | copy-start | bytes 4718596
  47.7 9.3 %copy-start.3 = (bf16[2,2048,128]{2,1,0:T(8,128)(2,1)S(1)}, bf16[2,2048,128]{2,1,0:T(8,128)(2,1)}, u32[]{:S(2)}) copy-start(bf16[2,2048,128]{2,1,0:T(8,128)(2,1)} %param.12) | copy-start | bytes 3145732
  50.0 24.9 %all-to-all-start.2 = ((bf16[64,32,128]{2,1,0:T(8,128)(2,1)}), bf16[64,32,128]{2,1,0:T(8,128)(2,1)}, u32[]{:S(2)}, u32[]{:S(2)}) async-start(bf16[64,32,128]{2,1,0:T(8,128)(2,1)} %shard_map.100), calls=%async_computation.2 | async-start | bytes 1048576 | tf_op jit(solution)/shard_map/all_to_all | solution.py:172
